TPU v7x, 512 devices: a whole 4x4x16 slice. The times are simulated.
512 devices in a mesh: blk: 32 (over z, core), col: 16 (over y, x).
Axes of the slice: x: 4, y: 4, z: 16, core: 2. Of those that a mesh axis runs over, the one named last changes fastest.
Arguments:
- density: float32 [96, 7, 256, 256], P('blk', None, 'col'), as said below
- band_widths: int32 [96], P('blk'), may hold values from 1 to 3, as said below
Outputs:
- purified: float32 [96, 7, 256, 256], P('blk', None, 'col')
Inputs may be any that keep to these rules, and one draw needn't show every extreme that they name: `band_widths`: each block row keeps between 1 and 3 blocks on each side; 3 is reached in every draw. `density`: diagonal entries of the diagonal blocks lie between 0.05 and 0.95, all other entries are small.
All inputs are finite; a program needn't handle non-finite values.
Results may differ from a plain program's by a relative error of at most 0.00013.
Values sent between devices are 32-bit elements; how exact they have to be, the bound alone decides.
No kernel may reach another device: no remote copies, remote signals or barrier semaphores. Data moves between devices by JAX's collectives and lax.ppermute only.
A program may use at most 64 MiB of HBM per device.

v0:
```python
import jax
import jax.numpy as jnp
from jax import lax
from jax.sharding import PartitionSpec as P

W = 3


def padded(cells, sides, width):
    for axis, dim in sides:
        count = lax.axis_size(axis)
        head = lax.slice_in_dim(cells, 0, width, axis=dim)
        tail = lax.slice_in_dim(cells, cells.shape[dim] - width, cells.shape[dim], axis=dim)
        cells = jnp.concatenate(
            [
                lax.ppermute(tail, axis, [(i, (i + 1) % count) for i in range(count)]),
                cells,
                lax.ppermute(head, axis, [((i + 1) % count, i) for i in range(count)]),
            ],
            axis=dim,
        )
    return cells


def extend(right):
    return padded(right, (("blk", 0),), W)


def contract(extended, shard_rows):
    local_rows = shard_rows.shape[0]
    summed_bands = [None] * (2 * W + 1)
    for inner_band in range(2 * W + 1):
        lowest = max(0, inner_band - W)
        highest = min(2 * W, inner_band + W)
        source_low = lowest - inner_band + W
        source_high = highest - inner_band + W
        block_terms = jnp.einsum(
            "ibcs,isr->ibcr",
            extended[inner_band : inner_band + local_rows, source_low : source_high + 1],
            shard_rows[:, inner_band],
            precision=lax.Precision.HIGHEST,
        )
        for right_band in range(lowest, highest + 1):
            term = block_terms[:, right_band - lowest]
            summed_bands[right_band] = (
                term if summed_bands[right_band] is None else summed_bands[right_band] + term
            )
    return jnp.stack(summed_bands, axis=1)


def on_device(density, band_widths):
    offsets = jnp.abs(jnp.arange(2 * W + 1, dtype=jnp.int32) - W)
    pattern = (offsets[None, :] <= band_widths[:, None]).astype(jnp.float32)[:, :, None, None]
    current = density * pattern
    for purify_step in range(2):
        gathered = lax.all_gather(current, "col", axis=2, tiled=True)
        square = contract(extend(current), gathered) * pattern
        third_power = contract(extend(square), gathered) * pattern
        current = 3.0 * square - 2.0 * third_power
    return current


def solution(mesh):
    in_specs = (P("blk", None, "col", None), P("blk"))
    out_specs = P("blk", None, "col", None)
    return jax.shard_map(
        on_device, mesh=mesh, in_specs=in_specs, out_specs=out_specs, check_vma=False
    )
```

profile of v0, /device:TPU:6, one launch (start us, length us, event | category | flops | bytes accessed | tf_op | source)
XLA Modules:
  0.0 212.1 jit_solution(5076322240943868647)
XLA Ops:
  6.5 0.7 compare_convert_fusion
  7.3 1.8 copy_multiply_fusion
  9.1 0.0 all-gather.5.cloned.1.call-start
  9.1 0.0 collective-permute-start
  9.2 8.9 %collective-permute-start.1 = (f32[3,7,16,256]{3,2,0,1:T(8,128)}, f32[3,7,16,256]{3,2,0,1:T(8,128)S(1)}, u32[]{:S(2)}, u32[]{:S(2)}) collective-permute-start(f32[3,7,16,256]{3,2,0,1:T(8,128)} %copy_multiply_fusion), channel_id=1, source_target_pairs={{16,0},{32,16},{48,32},{64,48},{80,64},{96,80},{112,96},{128,112},... | collective-permute-start | bytes 1032200 | tf_op jit(solution)/shard_map/ppermute | solution.py:18
  18.1 69.7 %all-gather.3.cloned.1.call-done = f32[3,7,256,256]{3,2,0,1:T(8,128)} async-done(((f32[3,7,16,256]{3,2,0,1:T(8,128)}), f32[3,7,256,256]{3,2,0,1:T(8,128)}) %all-gather.3.cloned.1.call-update) | async-done | bytes 5505040 | tf_op jit(solution)/shard_map/all_gather | solution.py:56
  87.8 2.0 fusion.7
  89.8 1.7 fusion.1
  91.5 1.8 fusion.5
  93.3 1.8 fusion.3
  95.2 0.6 fusion.9
  95.8 0.6 fusion.11
  96.4 0.6 fusion.13
  97.1 0.1 broadcast_multiply_fusion.1
  97.2 0.0 collective-permute-start.2
  97.3 3.5 %collective-permute-start.3 = (f32[3,7,16,256]{3,2,0,1:T(8,128)S(1)}, f32[3,7,16,256]{3,2,0,1:T(8,128)S(1)}, u32[]{:S(2)}, u32[]{:S(2)}) collective-permute-start(f32[3,7,16,256]{3,2,0,1:T(8,128)S(1)} %broadcast_multiply_fusion.1), channel_id=1, source_target_pairs={{16,0},{32,16},{48,32},{64,48},{80,64},{96,80},{112,96},{128,112},... | collective-permute-start | bytes 1032200 | tf_op jit(solution)/shard_map/ppermute | solution.py:18
  100.8 0.6 fusion.6
  101.3 4.3 %collective-permute-done.2 = f32[3,7,16,256]{3,2,0,1:T(8,128)S(1)} collective-permute-done((f32[3,7,16,256]{3,2,0,1:T(8,128)S(1)}, f32[3,7,16,256]{3,2,0,1:T(8,128)S(1)}, u32[]{:S(2)}, u32[]{:S(2)}) %collective-permute-start.2) | collective-permute-done | bytes 344096 | tf_op jit(solution)/shard_map/ppermute | solution.py:16
  105.7 0.6 fusion
  106.3 0.6 fusion.4
  106.9 0.6 fusion.2
  107.5 0.6 fusion.8
  108.1 0.6 fusion.10
  108.7 0.6 fusion.12
  109.5 0.9 multiply_subtract_fusion.1
  110.3 0.0 collective-permute-start.4
  110.4 2.9 %collective-permute-start.5 = (f32[3,7,16,256]{3,2,0,1:T(8,128)}, f32[3,7,16,256]{3,2,0,1:T(8,128)S(1)}, u32[]{:S(2)}, u32[]{:S(2)}) collective-permute-start(f32[3,7,16,256]{3,2,0,1:T(8,128)} %multiply_subtract_fusion.1), channel_id=1, source_target_pairs={{16,0},{32,16},{48,32},{64,48},{80,64},{96,80},{112,96},{128,112},... | collective-permute-start | bytes 1032200 | tf_op jit(solution)/shard_map/ppermute | solution.py:18
  113.3 69.4 %all-gather.5.cloned.1.call-done = f32[3,7,256,256]{3,2,0,1:T(8,128)} async-done(((f32[3,7,16,256]{3,2,0,1:T(8,128)}), f32[3,7,256,256]{3,2,0,1:T(8,128)}) %all-gather.5.cloned.1.call-update) | async-done | bytes 5505040 | tf_op jit(solution)/shard_map/all_gather | solution.py:56
  182.7 2.0 fusion.21
  184.7 1.7 fusion.15
  186.4 1.8 fusion.19
  188.3 1.8 fusion.17
  190.1 0.6 fusion.23
  190.7 0.6 fusion.25
  191.3 0.6 fusion.27
  192.1 0.1 broadcast_multiply_fusion
  192.1 0.0 collective-permute-start.6
  192.2 3.5 %collective-permute-start.7 = (f32[3,7,16,256]{3,2,0,1:T(8,128)S(1)}, f32[3,7,16,256]{3,2,0,1:T(8,128)S(1)}, u32[]{:S(2)}, u32[]{:S(2)}) collective-permute-start(f32[3,7,16,256]{3,2,0,1:T(8,128)S(1)} %broadcast_multiply_fusion), channel_id=1, source_target_pairs={{16,0},{32,16},{48,32},{64,48},{80,64},{96,80},{112,96},{128,112},... | collective-permute-start | bytes 1032200 | tf_op jit(solution)/shard_map/ppermute | solution.py:18
  195.7 0.8 fusion.20
  196.5 4.1 %collective-permute-done.6 = f32[3,7,16,256]{3,2,0,1:T(8,128)S(1)} collective-permute-done((f32[3,7,16,256]{3,2,0,1:T(8,128)S(1)}, f32[3,7,16,256]{3,2,0,1:T(8,128)S(1)}, u32[]{:S(2)}, u32[]{:S(2)}) %collective-permute-start.6) | collective-permute-done | bytes 344096 | tf_op jit(solution)/shard_map/ppermute | solution.py:16
  200.6 0.6 fusion.14
  201.2 0.6 fusion.18
  201.8 0.6 fusion.16
  202.4 0.6 fusion.22
  203.0 0.6 fusion.24
  203.6 0.6 fusion.26
  204.4 0.1 multiply_subtract_fusion
  204.5 0.8 copy.180
  (46 shorter events, 0.6 us)
Async XLA Ops:
  6.5 81.3 %all-gather.3.cloned.1.call-start = ((), (), s32[]{:S(2)}) async-start(), calls=%async_computation | async-start | bytes 5849088 | tf_op jit(solution)/shard_map/all_gather | solution.py:56
  9.1 86.1 %copy-start.2 = (f32[3,7,16,256]{3,2,0,1:T(8,128)S(1)}, f32[3,7,16,256]{3,2,0,1:T(8,128)}, u32[]{:S(2)}) copy-start(f32[3,7,16,256]{3,2,0,1:T(8,128)} %copy_multiply_fusion) | copy-start | bytes 1032196
  9.1 173.6 %all-gather.5.cloned.1.call-start = ((), (), s32[]{:S(2)}) async-start(), calls=%async_computation.1 | async-start | bytes 5849088 | tf_op jit(solution)/shard_map/all_gather | solution.py:56
  9.1 80.6 %collective-permute-start = (f32[3,7,16,256]{3,2,0,1:T(8,128)}, f32[3,7,16,256]{3,2,0,1:T(8,128)S(1)}, u32[]{:S(2)}, u32[]{:S(2)}) collective-permute-start(f32[3,7,16,256]{3,2,0,1:T(8,128)} %copy_multiply_fusion), channel_id=1, source_target_pairs={{0,16},{16,32},{32,48},{48,64},{64,80},{80,96},{96,112},{112,128},... | collective-permute-start | bytes 1032200 | tf_op jit(solution)/shard_map/ppermute | solution.py:16
  9.2 86.0 %collective-permute-start.1 = (f32[3,7,16,256]{3,2,0,1:T(8,128)}, f32[3,7,16,256]{3,2,0,1:T(8,128)S(1)}, u32[]{:S(2)}, u32[]{:S(2)}) collective-permute-start(f32[3,7,16,256]{3,2,0,1:T(8,128)} %copy_multiply_fusion), channel_id=1, source_target_pairs={{16,0},{32,16},{48,32},{64,48},{80,64},{96,80},{112,96},{128,112},... | collective-permute-start | bytes 1032200 | tf_op jit(solution)/shard_map/ppermute | solution.py:18
  87.8 7.4 %copy-start = (f32[3,7,256,256]{3,2,0,1:T(8,128)S(1)}, f32[3,7,256,256]{3,2,0,1:T(8,128)}, u32[]{:S(2)}) copy-start(f32[3,7,256,256]{3,2,0,1:T(8,128)} %all-gather.3.cloned.1.call-done) | copy-start | bytes 16515076
  97.2 8.4 %collective-permute-start.2 = (f32[3,7,16,256]{3,2,0,1:T(8,128)S(1)}, f32[3,7,16,256]{3,2,0,1:T(8,128)S(1)}, u32[]{:S(2)}, u32[]{:S(2)}) collective-permute-start(f32[3,7,16,256]{3,2,0,1:T(8,128)S(1)} %broadcast_multiply_fusion.1), channel_id=1, source_target_pairs={{0,16},{16,32},{32,48},{48,64},{64,80},{80,96},{96,112},{112,128},... | collective-permute-start | bytes 1032200 | tf_op jit(solution)/shard_map/ppermute | solution.py:16
  97.3 10.2 %collective-permute-start.3 = (f32[3,7,16,256]{3,2,0,1:T(8,128)S(1)}, f32[3,7,16,256]{3,2,0,1:T(8,128)S(1)}, u32[]{:S(2)}, u32[]{:S(2)}) collective-permute-start(f32[3,7,16,256]{3,2,0,1:T(8,128)S(1)} %broadcast_multiply_fusion.1), channel_id=1, source_target_pairs={{16,0},{32,16},{48,32},{64,48},{80,64},{96,80},{112,96},{128,112},... | collective-permute-start | bytes 1032200 | tf_op jit(solution)/shard_map/ppermute | solution.py:18
  110.3 79.8 %copy-start.3 = (f32[3,7,16,256]{3,2,0,1:T(8,128)S(1)}, f32[3,7,16,256]{3,2,0,1:T(8,128)}, u32[]{:S(2)}) copy-start(f32[3,7,16,256]{3,2,0,1:T(8,128)} %multiply_subtract_fusion.1) | copy-start | bytes 1032196
  110.3 74.4 %collective-permute-start.4 = (f32[3,7,16,256]{3,2,0,1:T(8,128)}, f32[3,7,16,256]{3,2,0,1:T(8,128)S(1)}, u32[]{:S(2)}, u32[]{:S(2)}) collective-permute-start(f32[3,7,16,256]{3,2,0,1:T(8,128)} %multiply_subtract_fusion.1), channel_id=1, source_target_pairs={{0,16},{16,32},{32,48},{48,64},{64,80},{80,96},{96,112},{112,128},... | collective-permute-start | bytes 1032200 | tf_op jit(solution)/shard_map/ppermute | solution.py:16
  110.4 79.7 %collective-permute-start.5 = (f32[3,7,16,256]{3,2,0,1:T(8,128)}, f32[3,7,16,256]{3,2,0,1:T(8,128)S(1)}, u32[]{:S(2)}, u32[]{:S(2)}) collective-permute-start(f32[3,7,16,256]{3,2,0,1:T(8,128)} %multiply_subtract_fusion.1), channel_id=1, source_target_pairs={{16,0},{32,16},{48,32},{64,48},{80,64},{96,80},{112,96},{128,112},... | collective-permute-start | bytes 1032200 | tf_op jit(solution)/shard_map/ppermute | solution.py:18
  182.7 7.4 %copy-start.1 = (f32[3,7,256,256]{3,2,0,1:T(8,128)S(1)}, f32[3,7,256,256]{3,2,0,1:T(8,128)}, u32[]{:S(2)}) copy-start(f32[3,7,256,256]{3,2,0,1:T(8,128)} %all-gather.5.cloned.1.call-done) | copy-start | bytes 16515076
  192.1 8.4 %collective-permute-start.6 = (f32[3,7,16,256]{3,2,0,1:T(8,128)S(1)}, f32[3,7,16,256]{3,2,0,1:T(8,128)S(1)}, u32[]{:S(2)}, u32[]{:S(2)}) collective-permute-start(f32[3,7,16,256]{3,2,0,1:T(8,128)S(1)} %broadcast_multiply_fusion), channel_id=1, source_target_pairs={{0,16},{16,32},{32,48},{48,64},{64,80},{80,96},{96,112},{112,128},... | collective-permute-start | bytes 1032200 | tf_op jit(solution)/shard_map/ppermute | solution.py:16
  192.2 10.2 %collective-permute-start.7 = (f32[3,7,16,256]{3,2,0,1:T(8,128)S(1)}, f32[3,7,16,256]{3,2,0,1:T(8,128)S(1)}, u32[]{:S(2)}, u32[]{:S(2)}) collective-permute-start(f32[3,7,16,256]{3,2,0,1:T(8,128)S(1)} %broadcast_multiply_fusion), channel_id=1, source_target_pairs={{16,0},{32,16},{48,32},{64,48},{80,64},{96,80},{112,96},{128,112},... | collective-permute-start | bytes 1032200 | tf_op jit(solution)/shard_map/ppermute | solution.py:18
Sparse Core Ops, SparseCore 0:
  10.4 77.3 all-gather.2
  110.5 72.2 all-gather.4
where the time goes:
time: 212 us
  waiting for transfers between devices  148 us (70%)
  matrix products  26.7 us (13%)
  starting transfers between devices  19 us (9%)
  between operations  13.8 us (7%)
  other arithmetic  4.26 us (2%)
    all_gather x2, waiting for transfers between devices, on_device(): gathered = lax.all_gather(current, 'col', axis=2, tiled=True)  139 us
    dot_general x28, matrix products, contract(): jnp.einsum('ibcs,isr->ibcr', extended[inner_band:inner_band + local_rows,...  26.7 us
    ppermute x4, starting transfers between devices, padded(): lax.ppermute(head, axis, [((i + 1) % count, i) for i in range(count)])  18.9 us
    ppermute x4, waiting for transfers between devices, padded(): lax.ppermute(tail, axis, [(i, (i + 1) % count) for i in range(count)])  8.44 us
  transfers between devices with their start and end apart: 10, of which 4 were waited for; matrix products, arithmetic and copies ran while one was open for 9% of the time, Pallas kernels for 0%

commit v1 on v0

--- a/solution.py
+++ b/solution.py
@@ -48,12 +48,18 @@
     return jnp.stack(summed_bands, axis=1)
 
 
+def gather_columns(cells):
+    count = lax.axis_size("col")
+    copies = jnp.tile(cells, (1, 1, count, 1))
+    return lax.all_to_all(copies, "col", 2, 2, tiled=True)
+
+
 def on_device(density, band_widths):
     offsets = jnp.abs(jnp.arange(2 * W + 1, dtype=jnp.int32) - W)
     pattern = (offsets[None, :] <= band_widths[:, None]).astype(jnp.float32)[:, :, None, None]
     current = density * pattern
     for purify_step in range(2):
-        gathered = lax.all_gather(current, "col", axis=2, tiled=True)
+        gathered = gather_columns(current)
         square = contract(extend(current), gathered) * pattern
         third_power = contract(extend(square), gathered) * pattern
         current = 3.0 * square - 2.0 * third_power

time: 212 us -> 298 us (1.41); the launches traced: 212 us -> 294 us
  local copies, waits for them, and re-layouts: 0.77 us -> 48.1 us
  starting transfers between devices: 19 us -> 52.9 us
  between operations: 13.8 us -> 0.48 us
  waiting for transfers between devices: 148 us -> 158 us
  matrix products: 26.7 us -> 30.8 us
    all_to_all x0 -> x2, waiting for transfers between devices: none -> 150 us  [gather_columns(): return lax.all_to_all(copies, 'col', 2, 2, tiled=True)]
    all_gather x2 -> x0, waiting for transfers between devices: 139 us -> none  [on_device(): gathered = lax.all_gather(current, 'col', axis=2, tiled=True)]
    slice x0 -> x2, local copies, waits for them, and re-layouts: none -> 41.2 us  [contract(): shard_rows[:, inner_band]]
    all_to_all x0 -> x2, starting transfers between devices: none -> 17.2 us  [gather_columns(): return lax.all_to_all(copies, 'col', 2, 2, tiled=True)]
    ppermute x4, starting transfers between devices: 18.9 us -> 35.7 us  [padded(): lax.ppermute(head, axis, [((i + 1) % count, i) for i in range(count)])]
    another operation x0 -> x2, local copies, waits for them, and re-layouts: none -> 6.47 us  [gather_columns(): copies = jnp.tile(cells, (1, 1, count, 1))]
    dot_general x28, matrix products: 26.7 us -> 30.8 us  [contract(): jnp.einsum('ibcs,isr->ibcr', extended[inner_band:inner_band + local_rows,...]
  transfers between devices with their start and end apart: 10 -> 10, of which waited for: 4 -> 4; matrix products, arithmetic and copies ran while one was open for 9% -> 20% of each run, Pallas kernels for 0% -> 0%
where the time goes in v1:
time: 298 us; the launch traced here: 294 us
  waiting for transfers between devices  158 us (53%)
  starting transfers between devices  52.9 us (18%)
  local copies, waits for them, and re-layouts  48.1 us (16%)
  matrix products  30.8 us (10%)
  other arithmetic  3.53 us (1%)
    all_to_all x2, waiting for transfers between devices, gather_columns(): return lax.all_to_all(copies, 'col', 2, 2, tiled=True)  150 us
    slice x2, local copies, waits for them, and re-layouts, contract(): shard_rows[:, inner_band]  41.2 us
    ppermute x4, starting transfers between devices, padded(): lax.ppermute(head, axis, [((i + 1) % count, i) for i in range(count)])  35.7 us
    dot_general x28, matrix products, contract(): jnp.einsum('ibcs,isr->ibcr', extended[inner_band:inner_band + local_rows,...  30.8 us
    all_to_all x2, starting transfers between devices, gather_columns(): return lax.all_to_all(copies, 'col', 2, 2, tiled=True)  17.2 us
    ppermute x4, waiting for transfers between devices, padded(): lax.ppermute(tail, axis, [(i, (i + 1) % count) for i in range(count)])  8.63 us
    another operation x2, local copies, waits for them, and re-layouts, gather_columns(): copies = jnp.tile(cells, (1, 1, count, 1))  6.47 us
  transfers between devices with their start and end apart: 10, of which 4 were waited for; matrix products, arithmetic and copies ran while one was open for 20% of the time, Pallas kernels for 0%

profile of v1, /device:TPU:6, one launch (start us, length us, event | category | flops | bytes accessed | tf_op | source)
XLA Modules:
  0.0 294.1 jit_solution(9465738125793480264)
XLA Ops:
  0.0 0.7 compare_convert_fusion
  0.7 1.1 broadcast_multiply_fusion.2
  1.8 0.2 copy.21
  2.0 3.2 %tile.8 = f32[3,7,16,16,256]{4,1,0,3,2:T(8,128)} broadcast(f32[3,7,16,256]{3,1,0,2:T(8,128)S(1)} %copy.21), dimensions={0,1,3,4} | broadcast | bytes 5849088 | tf_op jit(solution)/shard_map/tile | solution.py:53
  5.3 10.2 %all-to-all-start = ((f32[3,7,256,256]{3,1,0,2:T(8,128)}), f32[3,7,256,256]{3,1,0,2:T(8,128)}, u32[]{:S(2)}, u32[]{:S(2)}) async-start(f32[3,7,256,256]{3,1,0,2:T(8,128)} %bitcast.112), calls=%async_computation | async-start | bytes 12582912 | tf_op jit(solution)/shard_map/all_to_all | solution.py:54
  15.5 5.6 %collective-permute-start.1 = (f32[3,7,16,256]{3,2,1,0:T(8,128)S(1)}, f32[3,7,16,256]{3,2,1,0:T(8,128)}, u32[]{:S(2)}, u32[]{:S(2)}) collective-permute-start(f32[3,7,16,256]{3,2,1,0:T(8,128)S(1)} %broadcast_multiply_fusion.2), channel_id=1, source_target_pairs={{16,0},{32,16},{48,32},{64,48},{80,64},{96,80},{112,96},{128,112},... | collective-permute-start | bytes 1032200 | tf_op jit(solution)/shard_map/ppermute | solution.py:18
  21.1 78.1 %all-to-all-done = f32[3,7,256,256]{3,1,0,2:T(8,128)} async-done(((f32[3,7,256,256]{3,1,0,2:T(8,128)}), f32[3,7,256,256]{3,1,0,2:T(8,128)}, u32[]{:S(2)}, u32[]{:S(2)}) %all-to-all-start) | async-done | bytes 5505056 | tf_op jit(solution)/shard_map/all_to_all | solution.py:54
  99.2 20.6 %fusion.45 = (f32[3,1,256,256]{3,1,0,2:T(1,128)S(1)}, f32[3,1,256,256]{3,1,0,2:T(1,128)}, f32[3,1,256,256]{3,1,0,2:T(1,128)S(1)}, f32[3,1,256,256]{3,1,0,2:T(1,1...) fusion(f32[3,7,256,256]{3,1,0,2:T(8,128)} %all-to-all-done), kind=kLoop, calls=%fused_computation.222 | loop fusion | bytes 11010048 | tf_op jit(solution)/shard_map/slice | solution.py:40
  119.8 1.8 fusion.7
  121.6 1.5 fusion.5
  123.1 1.5 fusion.1
  124.7 1.8 fusion.3
  126.5 1.5 fusion.9
  128.1 1.5 fusion.11
  129.7 1.5 fusion.13
  131.4 13.2 %collective-permute-start.3 = (f32[3,7,16,256]{3,2,1,0:T(8,128)S(1)}, f32[3,7,16,256]{3,2,1,0:T(8,128)S(1)}, u32[]{:S(2)}, u32[]{:S(2)}) collective-permute-start(f32[3,7,16,256]{3,2,1,0:T(8,128)S(1)} %broadcast_multiply_fusion.1), channel_id=1, source_target_pairs={{16,0},{32,16},{48,32},{64,48},{80,64},{96,80},{112,96},{128,112},... | collective-permute-start | bytes 1032200 | tf_op jit(solution)/shard_map/ppermute | solution.py:18
  144.7 0.6 fusion.6
  145.2 4.3 %collective-permute-done.2 = f32[3,7,16,256]{3,2,1,0:T(8,128)S(1)} collective-permute-done((f32[3,7,16,256]{3,2,1,0:T(8,128)S(1)}, f32[3,7,16,256]{3,2,1,0:T(8,128)S(1)}, u32[]{:S(2)}, u32[]{:S(2)}) %collective-permute-start.2) | collective-permute-done | bytes 344096 | tf_op jit(solution)/shard_map/ppermute | solution.py:16
  149.6 0.6 fusion
  150.2 0.6 fusion.4
  150.8 0.6 fusion.2
  151.4 0.6 fusion.8
  152.0 0.6 fusion.10
  152.6 0.6 fusion.12
  153.3 0.1 multiply_subtract_fusion.1
  153.5 0.2 copy.29
  153.7 3.2 %tile.20 = f32[3,7,16,16,256]{4,1,0,3,2:T(8,128)} broadcast(f32[3,7,16,256]{3,1,0,2:T(8,128)S(1)} %copy.29), dimensions={0,1,3,4} | broadcast | bytes 5849088 | tf_op jit(solution)/shard_map/tile | solution.py:53
  156.9 7.0 %all-to-all-start.1 = ((f32[3,7,256,256]{3,1,0,2:T(8,128)}), f32[3,7,256,256]{3,1,0,2:T(8,128)}, u32[]{:S(2)}, u32[]{:S(2)}) async-start(f32[3,7,256,256]{3,1,0,2:T(8,128)} %bitcast.113), calls=%async_computation.1 | async-start | bytes 12582912 | tf_op jit(solution)/shard_map/all_to_all | solution.py:54
  163.9 0.6 collective-permute-start.5
  164.5 71.4 %all-to-all-done.1 = f32[3,7,256,256]{3,1,0,2:T(8,128)} async-done(((f32[3,7,256,256]{3,1,0,2:T(8,128)}), f32[3,7,256,256]{3,1,0,2:T(8,128)}, u32[]{:S(2)}, u32[]{:S(2)}) %all-to-all-start.1) | async-done | bytes 5505056 | tf_op jit(solution)/shard_map/all_to_all | solution.py:54
  235.9 20.6 %fusion.44 = (f32[3,1,256,256]{3,1,0,2:T(1,128)S(1)}, f32[3,1,256,256]{3,1,0,2:T(1,128)}, f32[3,1,256,256]{3,1,0,2:T(1,128)S(1)}, f32[3,1,256,256]{3,1,0,2:T(1,1...) fusion(f32[3,7,256,256]{3,1,0,2:T(8,128)} %all-to-all-done.1), kind=kLoop, calls=%fused_computation.221 | loop fusion | bytes 11010048 | tf_op jit(solution)/shard_map/slice | solution.py:40
  256.6 1.8 fusion.21
  258.4 1.6 fusion.15
  260.0 1.5 fusion.19
  261.4 1.8 fusion.17
  263.3 1.5 fusion.23
  264.9 1.5 fusion.25
  266.4 1.5 fusion.27
  268.2 16.3 %collective-permute-start.7 = (f32[3,7,16,256]{3,2,1,0:T(8,128)S(1)}, f32[3,7,16,256]{3,2,1,0:T(8,128)S(1)}, u32[]{:S(2)}, u32[]{:S(2)}) collective-permute-start(f32[3,7,16,256]{3,2,1,0:T(8,128)S(1)} %broadcast_multiply_fusion), channel_id=1, source_target_pairs={{16,0},{32,16},{48,32},{64,48},{80,64},{96,80},{112,96},{128,112},... | collective-permute-start | bytes 1032200 | tf_op jit(solution)/shard_map/ppermute | solution.py:18
  284.5 0.6 fusion.20
  285.1 4.3 %collective-permute-done.6 = f32[3,7,16,256]{3,2,1,0:T(8,128)S(1)} collective-permute-done((f32[3,7,16,256]{3,2,1,0:T(8,128)S(1)}, f32[3,7,16,256]{3,2,1,0:T(8,128)S(1)}, u32[]{:S(2)}, u32[]{:S(2)}) %collective-permute-start.6) | collective-permute-done | bytes 344096 | tf_op jit(solution)/shard_map/ppermute | solution.py:16
  289.4 0.6 fusion.14
  290.0 0.6 fusion.18
  290.6 0.6 fusion.16
  291.2 0.6 fusion.22
  291.8 0.6 fusion.24
  292.5 0.6 fusion.26
  293.2 0.9 multiply_subtract_fusion
  (53 shorter events, 0.8 us)
Async XLA Ops:
  5.3 93.9 %all-to-all-start = ((f32[3,7,256,256]{3,1,0,2:T(8,128)}), f32[3,7,256,256]{3,1,0,2:T(8,128)}, u32[]{:S(2)}, u32[]{:S(2)}) async-start(f32[3,7,256,256]{3,1,0,2:T(8,128)} %bitcast.112), calls=%async_computation | async-start | bytes 12582912 | tf_op jit(solution)/shard_map/all_to_all | solution.py:54
  15.5 106.1 %collective-permute-start = (f32[3,7,16,256]{3,2,1,0:T(8,128)S(1)}, f32[3,7,16,256]{3,2,1,0:T(8,128)}, u32[]{:S(2)}, u32[]{:S(2)}) collective-permute-start(f32[3,7,16,256]{3,2,1,0:T(8,128)S(1)} %broadcast_multiply_fusion.2), channel_id=1, source_target_pairs={{0,16},{16,32},{32,48},{48,64},{64,80},{80,96},{96,112},{112,128},... | collective-permute-start | bytes 1032200 | tf_op jit(solution)/shard_map/ppermute | solution.py:16
  15.5 111.0 %collective-permute-start.1 = (f32[3,7,16,256]{3,2,1,0:T(8,128)S(1)}, f32[3,7,16,256]{3,2,1,0:T(8,128)}, u32[]{:S(2)}, u32[]{:S(2)}) collective-permute-start(f32[3,7,16,256]{3,2,1,0:T(8,128)S(1)} %broadcast_multiply_fusion.2), channel_id=1, source_target_pairs={{16,0},{32,16},{48,32},{64,48},{80,64},{96,80},{112,96},{128,112},... | collective-permute-start | bytes 1032200 | tf_op jit(solution)/shard_map/ppermute | solution.py:18
  119.8 8.3 %copy-start.2 = (f32[3,1,256,256]{3,1,0,2:T(1,128)S(1)}, f32[3,1,256,256]{3,1,0,2:T(1,128)}, u32[]{:S(2)}) copy-start(f32[3,1,256,256]{3,1,0,2:T(1,128)} %get-tuple-element.13) | copy-start | bytes 2359300
  121.6 23.1 %copy-start = (f32[3,1,256,256]{3,1,0,2:T(1,128)S(1)}, f32[3,1,256,256]{3,1,0,2:T(1,128)}, u32[]{:S(2)}) copy-start(f32[3,1,256,256]{3,1,0,2:T(1,128)} %get-tuple-element.15) | copy-start | bytes 2359300
  126.5 24.3 %copy-start.4 = (f32[3,1,256,256]{3,1,0,2:T(1,128)S(1)}, f32[3,1,256,256]{3,1,0,2:T(1,128)}, u32[]{:S(2)}) copy-start(f32[3,1,256,256]{3,1,0,2:T(1,128)} %get-tuple-element.17) | copy-start | bytes 2359300
  131.4 18.2 %collective-permute-start.2 = (f32[3,7,16,256]{3,2,1,0:T(8,128)S(1)}, f32[3,7,16,256]{3,2,1,0:T(8,128)S(1)}, u32[]{:S(2)}, u32[]{:S(2)}) collective-permute-start(f32[3,7,16,256]{3,2,1,0:T(8,128)S(1)} %broadcast_multiply_fusion.1), channel_id=1, source_target_pairs={{0,16},{16,32},{32,48},{48,64},{64,80},{80,96},{96,112},{112,128},... | collective-permute-start | bytes 1032200 | tf_op jit(solution)/shard_map/ppermute | solution.py:16
  131.4 19.9 %collective-permute-start.3 = (f32[3,7,16,256]{3,2,1,0:T(8,128)S(1)}, f32[3,7,16,256]{3,2,1,0:T(8,128)S(1)}, u32[]{:S(2)}, u32[]{:S(2)}) collective-permute-start(f32[3,7,16,256]{3,2,1,0:T(8,128)S(1)} %broadcast_multiply_fusion.1), channel_id=1, source_target_pairs={{16,0},{32,16},{48,32},{64,48},{80,64},{96,80},{112,96},{128,112},... | collective-permute-start | bytes 1032200 | tf_op jit(solution)/shard_map/ppermute | solution.py:18
  156.9 79.0 %all-to-all-start.1 = ((f32[3,7,256,256]{3,1,0,2:T(8,128)}), f32[3,7,256,256]{3,1,0,2:T(8,128)}, u32[]{:S(2)}, u32[]{:S(2)}) async-start(f32[3,7,256,256]{3,1,0,2:T(8,128)} %bitcast.113), calls=%async_computation.1 | async-start | bytes 12582912 | tf_op jit(solution)/shard_map/all_to_all | solution.py:54
  163.9 99.4 %collective-permute-start.5 = (f32[3,7,16,256]{3,2,1,0:T(8,128)S(1)}, f32[3,7,16,256]{3,2,1,0:T(8,128)}, u32[]{:S(2)}, u32[]{:S(2)}) collective-permute-start(f32[3,7,16,256]{3,2,1,0:T(8,128)S(1)} %multiply_subtract_fusion.1), channel_id=1, source_target_pairs={{16,0},{32,16},{48,32},{64,48},{80,64},{96,80},{112,96},{128,112},... | collective-permute-start | bytes 1032200 | tf_op jit(solution)/shard_map/ppermute | solution.py:18
  164.5 93.9 %collective-permute-start.4 = (f32[3,7,16,256]{3,2,1,0:T(8,128)S(1)}, f32[3,7,16,256]{3,2,1,0:T(8,128)}, u32[]{:S(2)}, u32[]{:S(2)}) collective-permute-start(f32[3,7,16,256]{3,2,1,0:T(8,128)S(1)} %multiply_subtract_fusion.1), channel_id=1, source_target_pairs={{0,16},{16,32},{32,48},{48,64},{64,80},{80,96},{96,112},{112,128},... | collective-permute-start | bytes 1032200 | tf_op jit(solution)/shard_map/ppermute | solution.py:16
  256.6 8.3 %copy-start.3 = (f32[3,1,256,256]{3,1,0,2:T(1,128)S(1)}, f32[3,1,256,256]{3,1,0,2:T(1,128)}, u32[]{:S(2)}) copy-start(f32[3,1,256,256]{3,1,0,2:T(1,128)} %get-tuple-element.6) | copy-start | bytes 2359300
  258.3 26.2 %copy-start.1 = (f32[3,1,256,256]{3,1,0,2:T(1,128)S(1)}, f32[3,1,256,256]{3,1,0,2:T(1,128)}, u32[]{:S(2)}) copy-start(f32[3,1,256,256]{3,1,0,2:T(1,128)} %get-tuple-element.8) | copy-start | bytes 2359300
  263.3 27.3 %copy-start.5 = (f32[3,1,256,256]{3,1,0,2:T(1,128)S(1)}, f32[3,1,256,256]{3,1,0,2:T(1,128)}, u32[]{:S(2)}) copy-start(f32[3,1,256,256]{3,1,0,2:T(1,128)} %get-tuple-element.10) | copy-start | bytes 2359300
  268.2 21.2 %collective-permute-start.6 = (f32[3,7,16,256]{3,2,1,0:T(8,128)S(1)}, f32[3,7,16,256]{3,2,1,0:T(8,128)S(1)}, u32[]{:S(2)}, u32[]{:S(2)}) collective-permute-start(f32[3,7,16,256]{3,2,1,0:T(8,128)S(1)} %broadcast_multiply_fusion), channel_id=1, source_target_pairs={{0,16},{16,32},{32,48},{48,64},{64,80},{80,96},{96,112},{112,128},... | collective-permute-start | bytes 1032200 | tf_op jit(solution)/shard_map/ppermute | solution.py:16
  268.2 23.0 %collective-permute-start.7 = (f32[3,7,16,256]{3,2,1,0:T(8,128)S(1)}, f32[3,7,16,256]{3,2,1,0:T(8,128)S(1)}, u32[]{:S(2)}, u32[]{:S(2)}) collective-permute-start(f32[3,7,16,256]{3,2,1,0:T(8,128)S(1)} %broadcast_multiply_fusion), channel_id=1, source_target_pairs={{16,0},{32,16},{48,32},{64,48},{80,64},{96,80},{112,96},{128,112},... | collective-permute-start | bytes 1032200 | tf_op jit(solution)/shard_map/ppermute | solution.py:18

commit v2 on v0

v2 whole, which is shorter than its diff:
```python
import jax
import jax.numpy as jnp
from jax import lax
from jax.sharding import PartitionSpec as P

W = 3


def send(cells, shift):
    count = lax.axis_size("blk")
    return lax.ppermute(cells, "blk", [(i, (i + shift) % count) for i in range(count)])


def halo_pieces(cells):
    rows = cells.shape[0]
    tail = [cells[rows - W + k, W - k :] for k in range(W)]
    head = [cells[k, : 2 * W - k] for k in range(W)]
    return tail, head


def extend(right):
    tail, head = halo_pieces(right)
    from_left = send(jnp.concatenate(tail, axis=0), 1)
    from_right = send(jnp.concatenate(head, axis=0), -1)
    zero = jnp.zeros((1,) + right.shape[2:], right.dtype)
    rows = []
    start = 0
    for k in range(W):
        width = 2 * W + 1 - (W - k)
        piece = from_left[start : start + width]
        start += width
        rows.append(jnp.concatenate([jnp.broadcast_to(zero, (W - k,) + right.shape[2:]), piece], axis=0))
    left = jnp.stack(rows)
    rows = []
    start = 0
    for k in range(W):
        width = 2 * W - k
        piece = from_right[start : start + width]
        start += width
        rows.append(jnp.concatenate([piece, jnp.broadcast_to(zero, (k + 1,) + right.shape[2:])], axis=0))
    right_rows = jnp.stack(rows)
    return jnp.concatenate([left, right, right_rows], axis=0)


def contract(extended, shard_rows, pattern):
    local_rows = shard_rows.shape[0]
    summed_bands = [None] * (2 * W + 1)
    for inner_band in range(2 * W + 1):
        lowest = max(0, inner_band - W)
        highest = min(2 * W, inner_band + W)
        source_low = lowest - inner_band + W
        source_high = highest - inner_band + W
        block_terms = jnp.einsum(
            "ibcs,isr->ibcr",
            extended[inner_band : inner_band + local_rows, source_low : source_high + 1],
            shard_rows[:, inner_band] * pattern[:, inner_band],
            precision=lax.Precision.HIGHEST,
        )
        for right_band in range(lowest, highest + 1):
            term = block_terms[:, right_band - lowest]
            summed_bands[right_band] = (
                term if summed_bands[right_band] is None else summed_bands[right_band] + term
            )
    return jnp.stack(summed_bands, axis=1)


def on_device(density, band_widths):
    offsets = jnp.abs(jnp.arange(2 * W + 1, dtype=jnp.int32) - W)
    pattern = (offsets[None, :] <= band_widths[:, None]).astype(jnp.float32)[:, :, None, None]
    current = density * pattern
    for purify_step in range(2):
        source = density if purify_step == 0 else current
        gathered = lax.all_gather(source, "col", axis=2, tiled=True)
        square = contract(extend(current), gathered, pattern) * pattern
        third_power = contract(extend(square), gathered, pattern) * pattern
        current = 3.0 * square - 2.0 * third_power
    return current


def solution(mesh):
    in_specs = (P("blk", None, "col", None), P("blk"))
    out_specs = P("blk", None, "col", None)
    return jax.shard_map(
        on_device, mesh=mesh, in_specs=in_specs, out_specs=out_specs, check_vma=False
    )
```

time: 212 us -> 215 us (1.014); the launches traced: 212 us -> 213 us
  waiting for transfers between devices: 148 us -> 140 us
  local copies, waits for them, and re-layouts: 0.77 us -> 5.04 us
    all_gather x2, waiting for transfers between devices: 139 us -> 127 us  [on_device(): gathered = lax.all_gather(source, 'col', axis=2, tiled=True)]
    ppermute x8, waiting for transfers between devices: 8.45 us -> 13.3 us  [send(): lax.ppermute(cells, 'blk', [(i, (i + shift) % count) for i in range(count)])]
    squeeze x0 -> x12, local copies, waits for them, and re-layouts: none -> 2.98 us  [halo_pieces(): head = [cells[k, :2 * W - k] for k in range(W)]]
  transfers between devices with their start and end apart: 10 -> 10, of which waited for: 4 -> 6; matrix products, arithmetic and copies ran while one was open for 9% -> 4% of each run, Pallas kernels for 0% -> 0%
where the time goes in v2:
time: 215 us; the launch traced here: 213 us
  waiting for transfers between devices  140 us (65%)
  matrix products  28.8 us (13%)
  starting transfers between devices  19 us (9%)
  between operations  14.2 us (7%)
  other arithmetic  6.1 us (3%)
  local copies, waits for them, and re-layouts  5.04 us (2%)
    all_gather x2, waiting for transfers between devices, on_device(): gathered = lax.all_gather(source, 'col', axis=2, tiled=True)  127 us
    dot_general x28, matrix products, contract(): jnp.einsum('ibcs,isr->ibcr', extended[inner_band:inner_band + local_rows,...  28.8 us
    ppermute x8, starting transfers between devices, send(): lax.ppermute(cells, 'blk', [(i, (i + shift) % count) for i in range(count)])  19 us
    ppermute x8, waiting for transfers between devices, send(): lax.ppermute(cells, 'blk', [(i, (i + shift) % count) for i in range(count)])  13.3 us
  transfers between devices with their start and end apart: 10, of which 6 were waited for; matrix products, arithmetic and copies ran while one was open for 4% of the time, Pallas kernels for 0%

profile of v2, /device:TPU:6, one launch (start us, length us, event | category | flops | bytes accessed | tf_op | source)
XLA Modules:
  0.0 212.9 jit_solution(9925120033447639439)
XLA Ops:
  6.5 1.7 copy.3
  8.4 0.7 compare_convert_fusion.1
  9.1 1.1 broadcast_multiply_fusion.2
  10.3 8.9 %collective-permute-start.1 = (f32[15,16,256]{2,1,0:T(8,128)S(1)}, f32[15,16,256]{2,1,0:T(8,128)S(1)}, u32[]{:S(2)}, u32[]{:S(2)}) collective-permute-start(f32[15,16,256]{2,1,0:T(8,128)S(1)} %pad_maximum_fusion.1), channel_id=1, source_target_pairs={{0,496},{16,0},{32,16},{48,32},{64,48},{80,64},{96,80},{112,96},{1... | collective-permute-start | bytes 737288 | tf_op jit(solution)/shard_map/ppermute | solution.py:11
  19.2 0.7 compare_convert_fusion
  20.0 3.1 %collective-permute-done = f32[15,16,256]{2,1,0:T(8,128)S(1)} collective-permute-done((f32[15,16,256]{2,1,0:T(8,128)S(1)}, f32[15,16,256]{2,1,0:T(8,128)S(1)}, u32[]{:S(2)}, u32[]{:S(2)}) %collective-permute-start) | collective-permute-done | bytes 245792 | tf_op jit(solution)/shard_map/ppermute | solution.py:11
  23.2 0.7 fusion.219
  23.9 63.9 %all-gather.3.cloned.1.call-done = f32[3,7,256,256]{3,2,0,1:T(8,128)} async-done(((f32[3,7,16,256]{3,2,0,1:T(8,128)}), f32[3,7,256,256]{3,2,0,1:T(8,128)}) %all-gather.3.cloned.1.call-update) | async-done | bytes 5505040 | tf_op jit(solution)/shard_map/all_gather | solution.py:73
  87.8 1.9 fusion.42
  89.8 1.8 fusion.38
  91.6 1.8 fusion.34
  93.4 1.8 fusion.30
  95.2 0.7 fusion.46
  96.0 0.7 fusion.50
  96.7 0.7 fusion.54
  97.7 3.5 %collective-permute-start.3 = (f32[15,16,256]{2,1,0:T(8,128)S(1)}, f32[15,16,256]{2,1,0:T(8,128)S(1)}, u32[]{:S(2)}, u32[]{:S(2)}) collective-permute-start(f32[15,16,256]{2,1,0:T(8,128)S(1)} %pad_maximum_fusion.3), channel_id=1, source_target_pairs={{0,496},{16,0},{32,16},{48,32},{64,48},{80,64},{96,80},{112,96},{1... | collective-permute-start | bytes 737288 | tf_op jit(solution)/shard_map/ppermute | solution.py:11
  101.2 0.7 fusion.40
  101.9 3.2 %collective-permute-done.2 = f32[15,16,256]{2,1,0:T(8,128)S(1)} collective-permute-done((f32[15,16,256]{2,1,0:T(8,128)S(1)}, f32[15,16,256]{2,1,0:T(8,128)S(1)}, u32[]{:S(2)}, u32[]{:S(2)}) %collective-permute-start.2) | collective-permute-done | bytes 245792 | tf_op jit(solution)/shard_map/ppermute | solution.py:11
  105.2 0.7 fusion.36
  105.9 0.7 fusion.32
  106.6 0.7 fusion.28
  107.4 0.7 fusion.44
  108.1 0.7 fusion.48
  108.8 0.7 fusion.52
  109.6 0.9 multiply_subtract_fusion.1
  110.5 0.9 slice_bitcast_fusion.32
  111.4 1.0 slice_bitcast_fusion.24
  112.4 1.0 slice_bitcast_fusion.16
  113.4 2.9 %collective-permute-start.5 = (f32[15,16,256]{2,1,0:T(8,128)S(1)}, f32[15,16,256]{2,1,0:T(8,128)S(1)}, u32[]{:S(2)}, u32[]{:S(2)}) collective-permute-start(f32[15,16,256]{2,1,0:T(8,128)S(1)} %pad_maximum_fusion.5), channel_id=1, source_target_pairs={{0,496},{16,0},{32,16},{48,32},{64,48},{80,64},{96,80},{112,96},{1... | collective-permute-start | bytes 737288 | tf_op jit(solution)/shard_map/ppermute | solution.py:11
  116.4 3.8 %collective-permute-done.4 = f32[15,16,256]{2,1,0:T(8,128)S(1)} collective-permute-done((f32[15,16,256]{2,1,0:T(8,128)S(1)}, f32[15,16,256]{2,1,0:T(8,128)S(1)}, u32[]{:S(2)}, u32[]{:S(2)}) %collective-permute-start.4) | collective-permute-done | bytes 245792 | tf_op jit(solution)/shard_map/ppermute | solution.py:11
  120.5 62.7 %all-gather.5.cloned.1.call-done = f32[3,7,256,256]{3,2,1,0:T(8,128)} async-done(((f32[3,7,16,256]{3,2,1,0:T(8,128)}), f32[3,7,256,256]{3,2,1,0:T(8,128)}) %all-gather.5.cloned.1.call-update) | async-done | bytes 5505040 | tf_op jit(solution)/shard_map/all_gather | solution.py:73
  183.1 2.1 fusion.70
  185.2 1.8 fusion.66
  187.0 1.8 fusion.62
  188.8 1.8 fusion.58
  190.7 0.9 fusion.74
  191.6 0.7 fusion.78
  192.3 0.7 fusion.82
  193.4 3.5 %collective-permute-start.7 = (f32[15,16,256]{2,1,0:T(8,128)S(1)}, f32[15,16,256]{2,1,0:T(8,128)S(1)}, u32[]{:S(2)}, u32[]{:S(2)}) collective-permute-start(f32[15,16,256]{2,1,0:T(8,128)S(1)} %pad_maximum_fusion.7), channel_id=1, source_target_pairs={{0,496},{16,0},{32,16},{48,32},{64,48},{80,64},{96,80},{112,96},{1... | collective-permute-start | bytes 737288 | tf_op jit(solution)/shard_map/ppermute | solution.py:11
  196.8 0.7 fusion.68
  197.5 3.2 %collective-permute-done.6 = f32[15,16,256]{2,1,0:T(8,128)S(1)} collective-permute-done((f32[15,16,256]{2,1,0:T(8,128)S(1)}, f32[15,16,256]{2,1,0:T(8,128)S(1)}, u32[]{:S(2)}, u32[]{:S(2)}) %collective-permute-start.6) | collective-permute-done | bytes 245792 | tf_op jit(solution)/shard_map/ppermute | solution.py:11
  200.8 0.7 fusion.64
  201.5 0.7 fusion.60
  202.2 0.7 fusion.56
  203.0 0.7 fusion.72
  203.7 0.7 fusion.76
  204.4 0.7 fusion.80
  205.2 0.9 multiply_subtract_fusion
  (110 shorter events, 1.7 us)
Async XLA Ops:
  6.5 81.3 %all-gather.3.cloned.1.call-start = ((), (), s32[]{:S(2)}) async-start(), calls=%async_computation | async-start | bytes 5849088 | tf_op jit(solution)/shard_map/all_gather | solution.py:73
  8.3 174.8 %all-gather.5.cloned.1.call-start = ((), (), s32[]{:S(2)}) async-start(), calls=%async_computation.1 | async-start | bytes 5849088 | tf_op jit(solution)/shard_map/all_gather | solution.py:73
  10.2 12.8 %collective-permute-start = (f32[15,16,256]{2,1,0:T(8,128)S(1)}, f32[15,16,256]{2,1,0:T(8,128)S(1)}, u32[]{:S(2)}, u32[]{:S(2)}) collective-permute-start(f32[15,16,256]{2,1,0:T(8,128)S(1)} %pad_maximum_fusion), channel_id=1, source_target_pairs={{0,16},{16,32},{32,48},{48,64},{64,80},{80,96},{96,112},{112,128},... | collective-permute-start | bytes 737288 | tf_op jit(solution)/shard_map/ppermute | solution.py:11
  10.3 12.8 %collective-permute-start.1 = (f32[15,16,256]{2,1,0:T(8,128)S(1)}, f32[15,16,256]{2,1,0:T(8,128)S(1)}, u32[]{:S(2)}, u32[]{:S(2)}) collective-permute-start(f32[15,16,256]{2,1,0:T(8,128)S(1)} %pad_maximum_fusion.1), channel_id=1, source_target_pairs={{0,496},{16,0},{32,16},{48,32},{64,48},{80,64},{96,80},{112,96},{1... | collective-permute-start | bytes 737288 | tf_op jit(solution)/shard_map/ppermute | solution.py:11
  87.8 7.4 %copy-start.1 = (f32[3,7,256,256]{3,2,0,1:T(8,128)S(1)}, f32[3,7,256,256]{3,2,0,1:T(8,128)}, u32[]{:S(2)}) copy-start(f32[3,7,256,256]{3,2,0,1:T(8,128)} %all-gather.3.cloned.1.call-done) | copy-start | bytes 16515076
  97.4 9.9 %copy-start.3 = (pred[7]{0:T(512)(128)(4,1)S(1)}, pred[7]{0:T(512)(128)(4,1)}, u32[]{:S(2)}) copy-start(pred[7]{0:T(512)(128)(4,1)} %constant.13.clone.1) | copy-start | bytes 25
  97.7 7.4 %collective-permute-start.2 = (f32[15,16,256]{2,1,0:T(8,128)S(1)}, f32[15,16,256]{2,1,0:T(8,128)S(1)}, u32[]{:S(2)}, u32[]{:S(2)}) collective-permute-start(f32[15,16,256]{2,1,0:T(8,128)S(1)} %pad_maximum_fusion.2), channel_id=1, source_target_pairs={{0,16},{16,32},{32,48},{48,64},{64,80},{80,96},{96,112},{112,128},... | collective-permute-start | bytes 737288 | tf_op jit(solution)/shard_map/ppermute | solution.py:11
  97.7 7.4 %collective-permute-start.3 = (f32[15,16,256]{2,1,0:T(8,128)S(1)}, f32[15,16,256]{2,1,0:T(8,128)S(1)}, u32[]{:S(2)}, u32[]{:S(2)}) collective-permute-start(f32[15,16,256]{2,1,0:T(8,128)S(1)} %pad_maximum_fusion.3), channel_id=1, source_target_pairs={{0,496},{16,0},{32,16},{48,32},{64,48},{80,64},{96,80},{112,96},{1... | collective-permute-start | bytes 737288 | tf_op jit(solution)/shard_map/ppermute | solution.py:11
  110.5 74.7 %copy-start = (f32[3,7,16,256]{3,2,1,0:T(8,128)S(1)}, f32[3,7,16,256]{3,2,1,0:T(8,128)}, u32[]{:S(2)}) copy-start(f32[3,7,16,256]{3,2,1,0:T(8,128)} %multiply_subtract_fusion.1) | copy-start | bytes 1032196
  113.4 6.8 %collective-permute-start.4 = (f32[15,16,256]{2,1,0:T(8,128)S(1)}, f32[15,16,256]{2,1,0:T(8,128)S(1)}, u32[]{:S(2)}, u32[]{:S(2)}) collective-permute-start(f32[15,16,256]{2,1,0:T(8,128)S(1)} %pad_maximum_fusion.4), channel_id=1, source_target_pairs={{0,16},{16,32},{32,48},{48,64},{64,80},{80,96},{96,112},{112,128},... | collective-permute-start | bytes 737288 | tf_op jit(solution)/shard_map/ppermute | solution.py:11
  113.4 6.8 %collective-permute-start.5 = (f32[15,16,256]{2,1,0:T(8,128)S(1)}, f32[15,16,256]{2,1,0:T(8,128)S(1)}, u32[]{:S(2)}, u32[]{:S(2)}) collective-permute-start(f32[15,16,256]{2,1,0:T(8,128)S(1)} %pad_maximum_fusion.5), channel_id=1, source_target_pairs={{0,496},{16,0},{32,16},{48,32},{64,48},{80,64},{96,80},{112,96},{1... | collective-permute-start | bytes 737288 | tf_op jit(solution)/shard_map/ppermute | solution.py:11
  183.1 7.6 %copy-start.2 = (f32[3,7,256,256]{3,2,1,0:T(8,128)S(1)}, f32[3,7,256,256]{3,2,1,0:T(8,128)}, u32[]{:S(2)}) copy-start(f32[3,7,256,256]{3,2,1,0:T(8,128)} %all-gather.5.cloned.1.call-done) | copy-start | bytes 16515076
  193.3 7.4 %collective-permute-start.6 = (f32[15,16,256]{2,1,0:T(8,128)S(1)}, f32[15,16,256]{2,1,0:T(8,128)S(1)}, u32[]{:S(2)}, u32[]{:S(2)}) collective-permute-start(f32[15,16,256]{2,1,0:T(8,128)S(1)} %pad_maximum_fusion.6), channel_id=1, source_target_pairs={{0,16},{16,32},{32,48},{48,64},{64,80},{80,96},{96,112},{112,128},... | collective-permute-start | bytes 737288 | tf_op jit(solution)/shard_map/ppermute | solution.py:11
  193.4 7.4 %collective-permute-start.7 = (f32[15,16,256]{2,1,0:T(8,128)S(1)}, f32[15,16,256]{2,1,0:T(8,128)S(1)}, u32[]{:S(2)}, u32[]{:S(2)}) collective-permute-start(f32[15,16,256]{2,1,0:T(8,128)S(1)} %pad_maximum_fusion.7), channel_id=1, source_target_pairs={{0,496},{16,0},{32,16},{48,32},{64,48},{80,64},{96,80},{112,96},{1... | collective-permute-start | bytes 737288 | tf_op jit(solution)/shard_map/ppermute | solution.py:11
Sparse Core Ops, SparseCore 0:
  10.4 77.3 all-gather.2
  110.6 72.4 all-gather.4

commit v3 on v2

--- a/solution.py
+++ b/solution.py
@@ -42,7 +42,7 @@
     return jnp.concatenate([left, right, right_rows], axis=0)
 
 
-def contract(extended, shard_rows, pattern):
+def contract(extended, shard_rows):
     local_rows = shard_rows.shape[0]
     summed_bands = [None] * (2 * W + 1)
     for inner_band in range(2 * W + 1):
@@ -53,7 +53,7 @@
         block_terms = jnp.einsum(
             "ibcs,isr->ibcr",
             extended[inner_band : inner_band + local_rows, source_low : source_high + 1],
-            shard_rows[:, inner_band] * pattern[:, inner_band],
+            shard_rows[:, inner_band],
             precision=lax.Precision.HIGHEST,
         )
         for right_band in range(lowest, highest + 1):
@@ -64,15 +64,22 @@
     return jnp.stack(summed_bands, axis=1)
 
 
+def gather_columns(cells):
+    count = lax.axis_size("col")
+    copies = jnp.broadcast_to(cells[None], (count,) + cells.shape)
+    pieces = lax.all_to_all(copies, "col", 0, 0, tiled=False)
+    rows, bands, width, depth = cells.shape
+    return jnp.moveaxis(pieces, 0, 2).reshape(rows, bands, count * width, depth)
+
+
 def on_device(density, band_widths):
     offsets = jnp.abs(jnp.arange(2 * W + 1, dtype=jnp.int32) - W)
     pattern = (offsets[None, :] <= band_widths[:, None]).astype(jnp.float32)[:, :, None, None]
     current = density * pattern
     for purify_step in range(2):
-        source = density if purify_step == 0 else current
-        gathered = lax.all_gather(source, "col", axis=2, tiled=True)
-        square = contract(extend(current), gathered, pattern) * pattern
-        third_power = contract(extend(square), gathered, pattern) * pattern
+        gathered = gather_columns(current)
+        square = contract(extend(current), gathered) * pattern
+        third_power = contract(extend(square), gathered) * pattern
         current = 3.0 * square - 2.0 * third_power
     return current
 

time: 215 us -> 223 us (1.037)
  starting transfers between devices: 19 us -> 55.6 us
  between operations: 14.2 us -> 0.82 us
  matrix products: 28.8 us -> 16.7 us
  waiting for transfers between devices: 140 us -> 129 us
  local copies, waits for them, and re-layouts: 5.04 us -> 13.2 us
    all_gather x2 -> x0, waiting for transfers between devices: 127 us -> none  [on_device(): gathered = lax.all_gather(source, 'col', axis=2, tiled=True)]
    all_to_all x0 -> x2, waiting for transfers between devices: none -> 114 us  [gather_columns(): pieces = lax.all_to_all(copies, 'col', 0, 0, tiled=False)]
    ppermute x8, starting transfers between devices: 19 us -> 38.3 us  [send(): lax.ppermute(cells, 'blk', [(i, (i + shift) % count) for i in range(count)])]
    all_to_all x0 -> x2, starting transfers between devices: none -> 17.3 us  [gather_columns(): pieces = lax.all_to_all(copies, 'col', 0, 0, tiled=False)]
    dot_general x28, matrix products: 28.8 us -> 16.7 us  [contract(): jnp.einsum('ibcs,isr->ibcr', extended[inner_band:inner_band + local_rows,...]
    broadcast_in_dim x0 -> x2, local copies, waits for them, and re-layouts: none -> 6.38 us  [gather_columns(): copies = jnp.broadcast_to(cells[None], (count,) + cells.shape)]
    transpose x0 -> x2, local copies, waits for them, and re-layouts: none -> 6.36 us  [gather_columns(): return jnp.moveaxis(pieces, 0, 2).reshape(rows, bands, count * width, depth)]
    squeeze x12, local copies, waits for them, and re-layouts: 2.98 us -> 0.15 us  [halo_pieces(): head = [cells[k, :2 * W - k] for k in range(W)]]
  transfers between devices with their start and end apart: 10 -> 10, of which waited for: 6 -> 6; matrix products, arithmetic and copies ran while one was open for 4% -> 2% of each run, Pallas kernels for 0% -> 0%
where the time goes in v3:
time: 223 us; the launch traced here: 219 us
  waiting for transfers between devices  129 us (58%)
  starting transfers between devices  55.6 us (25%)
  matrix products  16.7 us (7%)
  local copies, waits for them, and re-layouts  13.2 us (6%)
  other arithmetic  4 us (2%)
    all_to_all x2, waiting for transfers between devices, gather_columns(): pieces = lax.all_to_all(copies, 'col', 0, 0, tiled=False)  114 us
    ppermute x8, starting transfers between devices, send(): lax.ppermute(cells, 'blk', [(i, (i + shift) % count) for i in range(count)])  38.3 us
    all_to_all x2, starting transfers between devices, gather_columns(): pieces = lax.all_to_all(copies, 'col', 0, 0, tiled=False)  17.3 us
    dot_general x28, matrix products, contract(): jnp.einsum('ibcs,isr->ibcr', extended[inner_band:inner_band + local_rows,...  16.7 us
    ppermute x8, waiting for transfers between devices, send(): lax.ppermute(cells, 'blk', [(i, (i + shift) % count) for i in range(count)])  14.1 us
    broadcast_in_dim x2, local copies, waits for them, and re-layouts, gather_columns(): copies = jnp.broadcast_to(cells[None], (count,) + cells.shape)  6.38 us
    transpose x2, local copies, waits for them, and re-layouts, gather_columns(): return jnp.moveaxis(pieces, 0, 2).reshape(rows, bands, count * width, depth)  6.36 us
  transfers between devices with their start and end apart: 10, of which 6 were waited for; matrix products, arithmetic and copies ran while one was open for 2% of the time, Pallas kernels for 0%

profile of v3, /device:TPU:6, one launch (start us, length us, event | category | flops | bytes accessed | tf_op | source)
XLA Modules:
  0.0 218.9 jit_solution(14991938142654924517)
XLA Ops:
  0.0 0.7 compare_convert_fusion
  0.7 1.1 broadcast_multiply_fusion.2
  1.8 3.2 %broadcast_in_dim.4 = f32[16,3,7,16,256]{4,3,1,2,0:T(8,128)} broadcast(f32[3,7,16,256]{3,2,0,1:T(8,128)S(1)} %copy.5), dimensions={1,2,3,4} | broadcast | bytes 5849088 | tf_op jit(solution)/shard_map/broadcast_in_dim | solution.py:69
  5.0 10.3 %all-to-all-start = ((f32[16,3,7,16,256]{4,3,1,2,0:T(8,128)}), f32[16,3,7,16,256]{4,3,1,2,0:T(8,128)}, u32[]{:S(2)}, u32[]{:S(2)}) async-start(f32[16,3,7,16,256]{4,3,1,2,0:T(8,128)} %broadcast_in_dim.4), calls=%async_computation | async-start | bytes 11010048 | tf_op jit(solution)/shard_map/all_to_all | solution.py:70
  15.5 5.6 %collective-permute-start.1 = (f32[15,16,256]{2,1,0:T(8,128)S(1)}, f32[15,16,256]{2,1,0:T(8,128)S(1)}, u32[]{:S(2)}, u32[]{:S(2)}) collective-permute-start(f32[15,16,256]{2,1,0:T(8,128)S(1)} %pad_maximum_fusion.1), channel_id=1, source_target_pairs={{0,496},{16,0},{32,16},{48,32},{64,48},{80,64},{96,80},{112,96},{1... | collective-permute-start | bytes 737288 | tf_op jit(solution)/shard_map/ppermute | solution.py:11
  21.1 3.8 %collective-permute-done = f32[15,16,256]{2,1,0:T(8,128)S(1)} collective-permute-done((f32[15,16,256]{2,1,0:T(8,128)S(1)}, f32[15,16,256]{2,1,0:T(8,128)S(1)}, u32[]{:S(2)}, u32[]{:S(2)}) %collective-permute-start) | collective-permute-done | bytes 245792 | tf_op jit(solution)/shard_map/ppermute | solution.py:11
  25.2 61.2 %all-to-all-done = f32[16,3,7,16,256]{4,3,1,2,0:T(8,128)} async-done(((f32[16,3,7,16,256]{4,3,1,2,0:T(8,128)}), f32[16,3,7,16,256]{4,3,1,2,0:T(8,128)}, u32[]{:S(2)}, u32[]{:S(2)}) %all-to-all-start) | async-done | bytes 5505056 | tf_op jit(solution)/shard_map/all_to_all | solution.py:70
  86.3 3.2 %copy.6 = f32[3,7,16,16,256]{4,3,2,0,1:T(8,128)S(1)} copy(f32[3,7,16,16,256]{4,3,0,1,2:T(8,128)} %bitcast.6) | data formatting | bytes 11010048 | tf_op jit(solution)/shard_map/transpose | solution.py:72
  89.5 0.6 fusion.7
  90.1 0.6 fusion.5
  90.7 0.6 fusion.3
  91.3 0.6 fusion.1
  91.9 0.6 fusion.9
  92.5 0.6 fusion.11
  93.1 0.6 fusion.13
  94.1 14.5 %collective-permute-start.3 = (f32[15,16,256]{2,1,0:T(8,128)S(1)}, f32[15,16,256]{2,1,0:T(8,128)S(1)}, u32[]{:S(2)}, u32[]{:S(2)}) collective-permute-start(f32[15,16,256]{2,1,0:T(8,128)S(1)} %pad_maximum_fusion.3), channel_id=1, source_target_pairs={{0,496},{16,0},{32,16},{48,32},{64,48},{80,64},{96,80},{112,96},{1... | collective-permute-start | bytes 737288 | tf_op jit(solution)/shard_map/ppermute | solution.py:11
  108.6 0.6 fusion.6
  109.2 3.2 %collective-permute-done.2 = f32[15,16,256]{2,1,0:T(8,128)S(1)} collective-permute-done((f32[15,16,256]{2,1,0:T(8,128)S(1)}, f32[15,16,256]{2,1,0:T(8,128)S(1)}, u32[]{:S(2)}, u32[]{:S(2)}) %collective-permute-start.2) | collective-permute-done | bytes 245792 | tf_op jit(solution)/shard_map/ppermute | solution.py:11
  112.5 0.6 fusion.4
  113.1 0.6 fusion.2
  113.7 0.6 fusion
  114.4 0.6 fusion.8
  115.1 0.6 fusion.10
  115.7 0.6 fusion.12
  116.5 0.1 multiply_subtract_fusion.1
  116.7 3.2 %broadcast_in_dim.5 = f32[16,3,7,16,256]{4,3,1,2,0:T(8,128)} broadcast(f32[3,7,16,256]{3,2,0,1:T(8,128)S(1)} %copy.7), dimensions={1,2,3,4} | broadcast | bytes 5849088 | tf_op jit(solution)/shard_map/broadcast_in_dim | solution.py:69
  119.9 7.0 %all-to-all-start.1 = ((f32[16,3,7,16,256]{4,3,1,2,0:T(8,128)}), f32[16,3,7,16,256]{4,3,1,2,0:T(8,128)}, u32[]{:S(2)}, u32[]{:S(2)}) async-start(f32[16,3,7,16,256]{4,3,1,2,0:T(8,128)} %broadcast_in_dim.5), calls=%async_computation.1 | async-start | bytes 11010048 | tf_op jit(solution)/shard_map/all_to_all | solution.py:70
  127.0 2.9 %collective-permute-start.5 = (f32[15,16,256]{2,1,0:T(8,128)S(1)}, f32[15,16,256]{2,1,0:T(8,128)S(1)}, u32[]{:S(2)}, u32[]{:S(2)}) collective-permute-start(f32[15,16,256]{2,1,0:T(8,128)S(1)} %pad_maximum_fusion.5), channel_id=1, source_target_pairs={{0,496},{16,0},{32,16},{48,32},{64,48},{80,64},{96,80},{112,96},{1... | collective-permute-start | bytes 737288 | tf_op jit(solution)/shard_map/ppermute | solution.py:11
  129.9 3.8 %collective-permute-done.4 = f32[15,16,256]{2,1,0:T(8,128)S(1)} collective-permute-done((f32[15,16,256]{2,1,0:T(8,128)S(1)}, f32[15,16,256]{2,1,0:T(8,128)S(1)}, u32[]{:S(2)}, u32[]{:S(2)}) %collective-permute-start.4) | collective-permute-done | bytes 245792 | tf_op jit(solution)/shard_map/ppermute | solution.py:11
  134.0 53.2 %all-to-all-done.1 = f32[16,3,7,16,256]{4,3,1,2,0:T(8,128)} async-done(((f32[16,3,7,16,256]{4,3,1,2,0:T(8,128)}), f32[16,3,7,16,256]{4,3,1,2,0:T(8,128)}, u32[]{:S(2)}, u32[]{:S(2)}) %all-to-all-start.1) | async-done | bytes 5505056 | tf_op jit(solution)/shard_map/all_to_all | solution.py:70
  187.2 3.2 %copy.8 = f32[3,7,16,16,256]{4,3,2,0,1:T(8,128)S(1)} copy(f32[3,7,16,16,256]{4,3,0,1,2:T(8,128)} %bitcast.60) | data formatting | bytes 11010048 | tf_op jit(solution)/shard_map/transpose | solution.py:72
  190.4 0.6 fusion.21
  191.0 0.6 fusion.19
  191.6 0.6 fusion.17
  192.2 0.6 fusion.15
  192.8 0.6 fusion.23
  193.4 0.6 fusion.25
  194.0 0.6 fusion.27
  195.1 15.2 %collective-permute-start.7 = (f32[15,16,256]{2,1,0:T(8,128)S(1)}, f32[15,16,256]{2,1,0:T(8,128)S(1)}, u32[]{:S(2)}, u32[]{:S(2)}) collective-permute-start(f32[15,16,256]{2,1,0:T(8,128)S(1)} %pad_maximum_fusion.7), channel_id=1, source_target_pairs={{0,496},{16,0},{32,16},{48,32},{64,48},{80,64},{96,80},{112,96},{1... | collective-permute-start | bytes 737288 | tf_op jit(solution)/shard_map/ppermute | solution.py:11
  210.2 0.6 fusion.20
  210.8 3.2 %collective-permute-done.6 = f32[15,16,256]{2,1,0:T(8,128)S(1)} collective-permute-done((f32[15,16,256]{2,1,0:T(8,128)S(1)}, f32[15,16,256]{2,1,0:T(8,128)S(1)}, u32[]{:S(2)}, u32[]{:S(2)}) %collective-permute-start.6) | collective-permute-done | bytes 245792 | tf_op jit(solution)/shard_map/ppermute | solution.py:11
  214.1 0.6 fusion.18
  214.7 0.6 fusion.16
  215.3 0.6 fusion.14
  216.0 0.6 fusion.22
  216.6 0.6 fusion.24
  217.3 0.6 fusion.26
  218.1 0.9 multiply_subtract_fusion
  (105 shorter events, 1.8 us)
Async XLA Ops:
  5.0 20.0 %copy-start = (pred[7]{0:T(512)(128)(4,1)S(1)}, pred[7]{0:T(512)(128)(4,1)}, u32[]{:S(2)}) copy-start(pred[7]{0:T(512)(128)(4,1)} %constant.13.clone.1) | copy-start | bytes 25
  5.0 81.3 %all-to-all-start = ((f32[16,3,7,16,256]{4,3,1,2,0:T(8,128)}), f32[16,3,7,16,256]{4,3,1,2,0:T(8,128)}, u32[]{:S(2)}, u32[]{:S(2)}) async-start(f32[16,3,7,16,256]{4,3,1,2,0:T(8,128)} %broadcast_in_dim.4), calls=%async_computation | async-start | bytes 11010048 | tf_op jit(solution)/shard_map/all_to_all | solution.py:70
  15.4 9.5 %collective-permute-start = (f32[15,16,256]{2,1,0:T(8,128)S(1)}, f32[15,16,256]{2,1,0:T(8,128)S(1)}, u32[]{:S(2)}, u32[]{:S(2)}) collective-permute-start(f32[15,16,256]{2,1,0:T(8,128)S(1)} %pad_maximum_fusion), channel_id=1, source_target_pairs={{0,16},{16,32},{32,48},{48,64},{64,80},{80,96},{96,112},{112,128},... | collective-permute-start | bytes 737288 | tf_op jit(solution)/shard_map/ppermute | solution.py:11
  15.5 9.5 %collective-permute-start.1 = (f32[15,16,256]{2,1,0:T(8,128)S(1)}, f32[15,16,256]{2,1,0:T(8,128)S(1)}, u32[]{:S(2)}, u32[]{:S(2)}) collective-permute-start(f32[15,16,256]{2,1,0:T(8,128)S(1)} %pad_maximum_fusion.1), channel_id=1, source_target_pairs={{0,496},{16,0},{32,16},{48,32},{64,48},{80,64},{96,80},{112,96},{1... | collective-permute-start | bytes 737288 | tf_op jit(solution)/shard_map/ppermute | solution.py:11
  94.1 18.4 %collective-permute-start.2 = (f32[15,16,256]{2,1,0:T(8,128)S(1)}, f32[15,16,256]{2,1,0:T(8,128)S(1)}, u32[]{:S(2)}, u32[]{:S(2)}) collective-permute-start(f32[15,16,256]{2,1,0:T(8,128)S(1)} %pad_maximum_fusion.2), channel_id=1, source_target_pairs={{0,16},{16,32},{32,48},{48,64},{64,80},{80,96},{96,112},{112,128},... | collective-permute-start | bytes 737288 | tf_op jit(solution)/shard_map/ppermute | solution.py:11
  94.1 20.2 %collective-permute-start.3 = (f32[15,16,256]{2,1,0:T(8,128)S(1)}, f32[15,16,256]{2,1,0:T(8,128)S(1)}, u32[]{:S(2)}, u32[]{:S(2)}) collective-permute-start(f32[15,16,256]{2,1,0:T(8,128)S(1)} %pad_maximum_fusion.3), channel_id=1, source_target_pairs={{0,496},{16,0},{32,16},{48,32},{64,48},{80,64},{96,80},{112,96},{1... | collective-permute-start | bytes 737288 | tf_op jit(solution)/shard_map/ppermute | solution.py:11
  119.9 67.4 %all-to-all-start.1 = ((f32[16,3,7,16,256]{4,3,1,2,0:T(8,128)}), f32[16,3,7,16,256]{4,3,1,2,0:T(8,128)}, u32[]{:S(2)}, u32[]{:S(2)}) async-start(f32[16,3,7,16,256]{4,3,1,2,0:T(8,128)} %broadcast_in_dim.5), calls=%async_computation.1 | async-start | bytes 11010048 | tf_op jit(solution)/shard_map/all_to_all | solution.py:70
  126.9 6.8 %collective-permute-start.4 = (f32[15,16,256]{2,1,0:T(8,128)S(1)}, f32[15,16,256]{2,1,0:T(8,128)S(1)}, u32[]{:S(2)}, u32[]{:S(2)}) collective-permute-start(f32[15,16,256]{2,1,0:T(8,128)S(1)} %pad_maximum_fusion.4), channel_id=1, source_target_pairs={{0,16},{16,32},{32,48},{48,64},{64,80},{80,96},{96,112},{112,128},... | collective-permute-start | bytes 737288 | tf_op jit(solution)/shard_map/ppermute | solution.py:11
  127.0 6.8 %collective-permute-start.5 = (f32[15,16,256]{2,1,0:T(8,128)S(1)}, f32[15,16,256]{2,1,0:T(8,128)S(1)}, u32[]{:S(2)}, u32[]{:S(2)}) collective-permute-start(f32[15,16,256]{2,1,0:T(8,128)S(1)} %pad_maximum_fusion.5), channel_id=1, source_target_pairs={{0,496},{16,0},{32,16},{48,32},{64,48},{80,64},{96,80},{112,96},{1... | collective-permute-start | bytes 737288 | tf_op jit(solution)/shard_map/ppermute | solution.py:11
  195.0 19.0 %collective-permute-start.6 = (f32[15,16,256]{2,1,0:T(8,128)S(1)}, f32[15,16,256]{2,1,0:T(8,128)S(1)}, u32[]{:S(2)}, u32[]{:S(2)}) collective-permute-start(f32[15,16,256]{2,1,0:T(8,128)S(1)} %pad_maximum_fusion.6), channel_id=1, source_target_pairs={{0,16},{16,32},{32,48},{48,64},{64,80},{80,96},{96,112},{112,128},... | collective-permute-start | bytes 737288 | tf_op jit(solution)/shard_map/ppermute | solution.py:11
  195.1 20.9 %collective-permute-start.7 = (f32[15,16,256]{2,1,0:T(8,128)S(1)}, f32[15,16,256]{2,1,0:T(8,128)S(1)}, u32[]{:S(2)}, u32[]{:S(2)}) collective-permute-start(f32[15,16,256]{2,1,0:T(8,128)S(1)} %pad_maximum_fusion.7), channel_id=1, source_target_pairs={{0,496},{16,0},{32,16},{48,32},{64,48},{80,64},{96,80},{112,96},{1... | collective-permute-start | bytes 737288 | tf_op jit(solution)/shard_map/ppermute | solution.py:11

commit v4 on v2

--- a/solution.py
+++ b/solution.py
@@ -1,6 +1,7 @@
 import jax
 import jax.numpy as jnp
 from jax import lax
+from jax.experimental import pallas as pl
 from jax.sharding import PartitionSpec as P
 
 W = 3
@@ -42,26 +43,27 @@
     return jnp.concatenate([left, right, right_rows], axis=0)
 
 
-def contract(extended, shard_rows, pattern):
-    local_rows = shard_rows.shape[0]
-    summed_bands = [None] * (2 * W + 1)
-    for inner_band in range(2 * W + 1):
-        lowest = max(0, inner_band - W)
-        highest = min(2 * W, inner_band + W)
-        source_low = lowest - inner_band + W
-        source_high = highest - inner_band + W
-        block_terms = jnp.einsum(
-            "ibcs,isr->ibcr",
-            extended[inner_band : inner_band + local_rows, source_low : source_high + 1],
-            shard_rows[:, inner_band] * pattern[:, inner_band],
-            precision=lax.Precision.HIGHEST,
-        )
-        for right_band in range(lowest, highest + 1):
-            term = block_terms[:, right_band - lowest]
-            summed_bands[right_band] = (
-                term if summed_bands[right_band] is None else summed_bands[right_band] + term
-            )
-    return jnp.stack(summed_bands, axis=1)
+def band_kernel(ext_ref, left_ref, out_ref):
+    rows = out_ref.shape[0]
+    width = out_ref.shape[2]
+    for i in range(rows):
+        summed = [None] * (2 * W + 1)
+        for a in range(2 * W + 1):
+            lo, hi = max(0, a - W), min(2 * W, a + W)
+            count = hi - lo + 1
+            lhs = ext_ref[i + a, lo - a + W : hi - a + W + 1].reshape(count * width, -1)
+            res = jnp.dot(lhs, left_ref[i, a], precision=lax.Precision.HIGHEST, preferred_element_type=jnp.float32)
+            for b in range(lo, hi + 1):
+                part = res[(b - lo) * width : (b - lo + 1) * width]
+                summed[b] = part if summed[b] is None else summed[b] + part
+        for b in range(2 * W + 1):
+            out_ref[i, b] = summed[b]
+def contract_kernel(extended, shard_rows):
+    rows, bands, width, depth = extended.shape[0] - 2 * W, extended.shape[1], extended.shape[2], extended.shape[3]
+    flops = 2 * rows * 37 * width * depth * shard_rows.shape[2]
+    nbytes = 4 * (extended.size + shard_rows.size + rows * bands * width * depth)
+    return pl.pallas_call(band_kernel, out_shape=jax.ShapeDtypeStruct((rows, bands, width, depth), jnp.float32),
+        cost_estimate=pl.CostEstimate(flops=flops, transcendentals=0, bytes_accessed=nbytes))(extended, shard_rows)
 
 
 def on_device(density, band_widths):
@@ -69,10 +71,9 @@
     pattern = (offsets[None, :] <= band_widths[:, None]).astype(jnp.float32)[:, :, None, None]
     current = density * pattern
     for purify_step in range(2):
-        source = density if purify_step == 0 else current
-        gathered = lax.all_gather(source, "col", axis=2, tiled=True)
-        square = contract(extend(current), gathered, pattern) * pattern
-        third_power = contract(extend(square), gathered, pattern) * pattern
+        gathered = lax.all_gather(current, "col", axis=2, tiled=True)
+        square = contract_kernel(extend(current), gathered) * pattern
+        third_power = contract_kernel(extend(square), gathered) * pattern
         current = 3.0 * square - 2.0 * third_power
     return current
 

time: 215 us -> 220 us (1.023)
  matrix products: 28.8 us -> 0 us
  Pallas kernels: 0 us -> 26.8 us
  other arithmetic: 6.1 us -> 12.6 us
  local copies, waits for them, and re-layouts: 5.04 us -> 8.98 us
    dot_general x28 -> x0, matrix products: 28.8 us -> none  [contract(): jnp.einsum('ibcs,isr->ibcr', extended[inner_band:inner_band + local_rows,...]
    pallas_call x0 -> x4, Pallas kernels: none -> 26.8 us  [contract_kernel(): pl.pallas_call(band_kernel, out_shape=jax.ShapeDtypeStruct((rows, bands,...]
    all_gather x2, waiting for transfers between devices: 127 us -> 122 us  [on_device(): gathered = lax.all_gather(current, 'col', axis=2, tiled=True)]
    unnamed x24 -> x7, other arithmetic: 0.5 us -> 4.17 us
    squeeze x12, local copies, waits for them, and re-layouts: 2.98 us -> 5.72 us  [halo_pieces(): head = [cells[k, :2 * W - k] for k in range(W)]]
  transfers between devices with their start and end apart: 10 -> 10, of which waited for: 6 -> 6; matrix products, arithmetic and copies ran while one was open for 4% -> 5% of each run, Pallas kernels for 0% -> 0%
where the time goes in v4:
time: 220 us; the launch traced here: 219 us
  waiting for transfers between devices  138 us (63%)
  Pallas kernels  26.8 us (12%)
  starting transfers between devices  19 us (9%)
  between operations  14 us (6%)
  other arithmetic  12.6 us (6%)
  local copies, waits for them, and re-layouts  8.98 us (4%)
    all_gather x2, waiting for transfers between devices, on_device(): gathered = lax.all_gather(current, 'col', axis=2, tiled=True)  122 us
    pallas_call x4, Pallas kernels, contract_kernel(): pl.pallas_call(band_kernel, out_shape=jax.ShapeDtypeStruct((rows, bands,...  26.8 us
    ppermute x8, starting transfers between devices, send(): lax.ppermute(cells, 'blk', [(i, (i + shift) % count) for i in range(count)])  19 us
    ppermute x8, waiting for transfers between devices, send(): lax.ppermute(cells, 'blk', [(i, (i + shift) % count) for i in range(count)])  15.3 us
    squeeze x12, local copies, waits for them, and re-layouts, halo_pieces(): head = [cells[k, :2 * W - k] for k in range(W)]  5.72 us
  transfers between devices with their start and end apart: 10, of which 6 were waited for; matrix products, arithmetic and copies ran while one was open for 5% of the time, Pallas kernels for 0%

profile of v4, /device:TPU:6, one launch (start us, length us, event | category | flops | bytes accessed | tf_op | source)
XLA Modules:
  0.0 219.2 jit_solution(3270132655198544091)
XLA Ops:
  6.5 0.7 compare_convert_fusion
  7.3 1.8 broadcast_multiply_fusion.2
  9.1 0.0 all-gather.3.cloned.1.call-update
  9.1 0.0 all-gather.5.cloned.1.call-start
  9.1 0.9 slice_bitcast_fusion.22
  10.0 1.0 slice_bitcast_fusion.14
  11.0 1.0 slice_bitcast_fusion.6
  12.0 0.0 collective-permute-start
  12.0 8.9 %collective-permute-start.1 = (f32[15,16,256]{2,1,0:T(8,128)S(1)}, f32[15,16,256]{2,1,0:T(8,128)S(1)}, u32[]{:S(2)}, u32[]{:S(2)}) collective-permute-start(f32[15,16,256]{2,1,0:T(8,128)S(1)} %pad_maximum_fusion.1), channel_id=1, source_target_pairs={{0,496},{16,0},{32,16},{48,32},{64,48},{80,64},{96,80},{112,96},{1... | collective-permute-start | bytes 737288 | tf_op jit(solution)/shard_map/ppermute | solution.py:12
  21.0 3.8 %collective-permute-done = f32[15,16,256]{2,1,0:T(8,128)S(1)} collective-permute-done((f32[15,16,256]{2,1,0:T(8,128)S(1)}, f32[15,16,256]{2,1,0:T(8,128)S(1)}, u32[]{:S(2)}, u32[]{:S(2)}) %collective-permute-start) | collective-permute-done | bytes 245792 | tf_op jit(solution)/shard_map/ppermute | solution.py:12
  24.9 0.0 collective-permute-done.1
  24.9 1.1 constant_dynamic-update-slice_fusion
  26.0 0.7 fusion.7
  26.8 0.0 copy-start.6
  26.8 61.0 %all-gather.3.cloned.1.call-done.left_ref = f32[3,7,256,256]{3,2,1,0:T(8,128)} async-done(((f32[3,7,16,256]{3,2,1,0:T(8,128)}), f32[3,7,256,256]{3,2,1,0:T(8,128)}) %all-gather.3.cloned.1.call-update) | async-done | bytes 5505040 | tf_op jit(solution)/shard_map/all_gather | solution.py:74
  87.8 6.7 %shard_map.28 = f32[3,7,16,256]{3,2,1,0:T(8,128)} custom-call(f32[9,7,16,256]{3,2,1,0:T(8,128)} %copy-done.2, f32[3,7,256,256]{3,2,1,0:T(8,128)} %all-gather.3.cloned.1.call-done.left_ref), custom_call_target="tpu_custom_call" | custom-call | flops 232783872 | bytes 6881280 | tf_op jit(solution)/shard_map/pallas_call | solution.py:65
  94.5 1.1 broadcast_multiply_fusion.1
  95.6 0.0 copy-start.1
  95.7 0.0 collective-permute-start.2
  95.7 3.5 %collective-permute-start.3 = (f32[15,16,256]{2,1,0:T(8,128)S(1)}, f32[15,16,256]{2,1,0:T(8,128)S(1)}, u32[]{:S(2)}, u32[]{:S(2)}) collective-permute-start(f32[15,16,256]{2,1,0:T(8,128)S(1)} %pad_maximum_fusion.3), channel_id=1, source_target_pairs={{0,496},{16,0},{32,16},{48,32},{64,48},{80,64},{96,80},{112,96},{1... | collective-permute-start | bytes 737288 | tf_op jit(solution)/shard_map/ppermute | solution.py:12
  99.2 3.8 %collective-permute-done.2 = f32[15,16,256]{2,1,0:T(8,128)S(1)} collective-permute-done((f32[15,16,256]{2,1,0:T(8,128)S(1)}, f32[15,16,256]{2,1,0:T(8,128)S(1)}, u32[]{:S(2)}, u32[]{:S(2)}) %collective-permute-start.2) | collective-permute-done | bytes 245792 | tf_op jit(solution)/shard_map/ppermute | solution.py:12
  103.1 1.1 constant_dynamic-update-slice_fusion.1
  104.2 0.1 fusion.5
  104.4 1.0 copy-done.3
  105.3 6.7 %shard_map.29 = f32[3,7,16,256]{3,2,1,0:T(8,128)} custom-call(f32[9,7,16,256]{3,2,1,0:T(8,128)} %copy-done.3, f32[3,7,256,256]{3,2,1,0:T(8,128)} %all-gather.3.cloned.1.call-done.left_ref), custom_call_target="tpu_custom_call" | custom-call | flops 232783872 | bytes 6881280 | tf_op jit(solution)/shard_map/pallas_call | solution.py:65
  112.0 1.8 multiply_subtract_fusion.1
  113.9 0.0 all-gather.5.cloned.1.call-update
  113.9 0.9 slice_bitcast_fusion.18
  114.8 1.0 slice_bitcast_fusion.10
  115.7 1.0 slice_bitcast_fusion.2
  116.7 0.0 collective-permute-start.4
  116.8 2.9 %collective-permute-start.5 = (f32[15,16,256]{2,1,0:T(8,128)S(1)}, f32[15,16,256]{2,1,0:T(8,128)S(1)}, u32[]{:S(2)}, u32[]{:S(2)}) collective-permute-start(f32[15,16,256]{2,1,0:T(8,128)S(1)} %pad_maximum_fusion.5), channel_id=1, source_target_pairs={{0,496},{16,0},{32,16},{48,32},{64,48},{80,64},{96,80},{112,96},{1... | collective-permute-start | bytes 737288 | tf_op jit(solution)/shard_map/ppermute | solution.py:12
  119.7 3.8 %collective-permute-done.4 = f32[15,16,256]{2,1,0:T(8,128)S(1)} collective-permute-done((f32[15,16,256]{2,1,0:T(8,128)S(1)}, f32[15,16,256]{2,1,0:T(8,128)S(1)}, u32[]{:S(2)}, u32[]{:S(2)}) %collective-permute-start.4) | collective-permute-done | bytes 245792 | tf_op jit(solution)/shard_map/ppermute | solution.py:12
  123.6 0.0 collective-permute-done.5
  123.7 1.0 constant_dynamic-update-slice_fusion.2
  124.7 0.1 fusion.3
  124.8 61.4 %all-gather.5.cloned.1.call-done.left_ref = f32[3,7,256,256]{3,2,1,0:T(8,128)} async-done(((f32[3,7,16,256]{3,2,1,0:T(8,128)}), f32[3,7,256,256]{3,2,1,0:T(8,128)}) %all-gather.5.cloned.1.call-update) | async-done | bytes 5505040 | tf_op jit(solution)/shard_map/all_gather | solution.py:74
  186.3 6.7 %shard_map.30 = f32[3,7,16,256]{3,2,1,0:T(8,128)} custom-call(f32[9,7,16,256]{3,2,1,0:T(8,128)} %copy-done.4, f32[3,7,256,256]{3,2,1,0:T(8,128)} %all-gather.5.cloned.1.call-done.left_ref), custom_call_target="tpu_custom_call" | custom-call | flops 232783872 | bytes 6881280 | tf_op jit(solution)/shard_map/pallas_call | solution.py:65
  192.9 1.1 broadcast_multiply_fusion
  194.1 0.0 copy-start
  194.1 0.0 collective-permute-start.6
  194.2 3.5 %collective-permute-start.7 = (f32[15,16,256]{2,1,0:T(8,128)S(1)}, f32[15,16,256]{2,1,0:T(8,128)S(1)}, u32[]{:S(2)}, u32[]{:S(2)}) collective-permute-start(f32[15,16,256]{2,1,0:T(8,128)S(1)} %pad_maximum_fusion.7), channel_id=1, source_target_pairs={{0,496},{16,0},{32,16},{48,32},{64,48},{80,64},{96,80},{112,96},{1... | collective-permute-start | bytes 737288 | tf_op jit(solution)/shard_map/ppermute | solution.py:12
  197.7 3.8 %collective-permute-done.6 = f32[15,16,256]{2,1,0:T(8,128)S(1)} collective-permute-done((f32[15,16,256]{2,1,0:T(8,128)S(1)}, f32[15,16,256]{2,1,0:T(8,128)S(1)}, u32[]{:S(2)}, u32[]{:S(2)}) %collective-permute-start.6) | collective-permute-done | bytes 245792 | tf_op jit(solution)/shard_map/ppermute | solution.py:12
  201.6 1.1 constant_dynamic-update-slice_fusion.3
  202.7 0.1 fusion.1
  202.8 1.0 copy-done.5
  203.8 6.7 %shard_map.31 = f32[3,7,16,256]{3,2,1,0:T(8,128)} custom-call(f32[9,7,16,256]{3,2,1,0:T(8,128)} %copy-done.5, f32[3,7,256,256]{3,2,1,0:T(8,128)} %all-gather.5.cloned.1.call-done.left_ref), custom_call_target="tpu_custom_call" | custom-call | flops 232783872 | bytes 6881280 | tf_op jit(solution)/shard_map/pallas_call | solution.py:65
  210.5 1.8 multiply_subtract_fusion
  (67 shorter events, 0.6 us)
Async XLA Ops:
  6.5 81.3 %all-gather.3.cloned.1.call-start = ((), (), s32[]{:S(2)}) async-start(), calls=%async_computation | async-start | bytes 5849088 | tf_op jit(solution)/shard_map/all_gather | solution.py:74
  9.1 177.2 %all-gather.5.cloned.1.call-start = ((), (), s32[]{:S(2)}) async-start(), calls=%async_computation.1 | async-start | bytes 5849088 | tf_op jit(solution)/shard_map/all_gather | solution.py:74
  12.0 12.8 %collective-permute-start = (f32[15,16,256]{2,1,0:T(8,128)S(1)}, f32[15,16,256]{2,1,0:T(8,128)S(1)}, u32[]{:S(2)}, u32[]{:S(2)}) collective-permute-start(f32[15,16,256]{2,1,0:T(8,128)S(1)} %pad_maximum_fusion), channel_id=1, source_target_pairs={{0,16},{16,32},{32,48},{48,64},{64,80},{80,96},{96,112},{112,128},... | collective-permute-start | bytes 737288 | tf_op jit(solution)/shard_map/ppermute | solution.py:12
  12.0 12.8 %collective-permute-start.1 = (f32[15,16,256]{2,1,0:T(8,128)S(1)}, f32[15,16,256]{2,1,0:T(8,128)S(1)}, u32[]{:S(2)}, u32[]{:S(2)}) collective-permute-start(f32[15,16,256]{2,1,0:T(8,128)S(1)} %pad_maximum_fusion.1), channel_id=1, source_target_pairs={{0,496},{16,0},{32,16},{48,32},{64,48},{80,64},{96,80},{112,96},{1... | collective-permute-start | bytes 737288 | tf_op jit(solution)/shard_map/ppermute | solution.py:12
  26.8 61.0 %copy-start.2 = (f32[9,7,16,256]{3,2,1,0:T(8,128)}, f32[9,7,16,256]{3,2,1,0:T(8,128)S(1)}, u32[]{:S(2)}) copy-start(f32[9,7,16,256]{3,2,1,0:T(8,128)S(1)} %bitcast_dynamic-update-slice_fusion.15.ext_ref) | copy-start | bytes 3096580
  26.8 77.4 %copy-start.6 = (pred[7]{0:T(512)(128)(4,1)S(1)}, pred[7]{0:T(512)(128)(4,1)}, u32[]{:S(2)}) copy-start(pred[7]{0:T(512)(128)(4,1)} %constant.13.clone.1) | copy-start | bytes 25
  95.6 16.4 %copy-start.1 = (f32[3,7,16,256]{3,2,1,0:T(8,128)S(1)}, f32[3,7,16,256]{3,2,1,0:T(8,128)}, u32[]{:S(2)}) copy-start(f32[3,7,16,256]{3,2,1,0:T(8,128)} %shard_map.28) | copy-start | bytes 1032196
  95.7 7.4 %collective-permute-start.2 = (f32[15,16,256]{2,1,0:T(8,128)S(1)}, f32[15,16,256]{2,1,0:T(8,128)S(1)}, u32[]{:S(2)}, u32[]{:S(2)}) collective-permute-start(f32[15,16,256]{2,1,0:T(8,128)S(1)} %pad_maximum_fusion.2), channel_id=1, source_target_pairs={{0,16},{16,32},{32,48},{48,64},{64,80},{80,96},{96,112},{112,128},... | collective-permute-start | bytes 737288 | tf_op jit(solution)/shard_map/ppermute | solution.py:12
  95.7 8.5 %collective-permute-start.3 = (f32[15,16,256]{2,1,0:T(8,128)S(1)}, f32[15,16,256]{2,1,0:T(8,128)S(1)}, u32[]{:S(2)}, u32[]{:S(2)}) collective-permute-start(f32[15,16,256]{2,1,0:T(8,128)S(1)} %pad_maximum_fusion.3), channel_id=1, source_target_pairs={{0,496},{16,0},{32,16},{48,32},{64,48},{80,64},{96,80},{112,96},{1... | collective-permute-start | bytes 737288 | tf_op jit(solution)/shard_map/ppermute | solution.py:12
  104.4 1.0 copy-start.3
  116.7 6.8 %collective-permute-start.4 = (f32[15,16,256]{2,1,0:T(8,128)S(1)}, f32[15,16,256]{2,1,0:T(8,128)S(1)}, u32[]{:S(2)}, u32[]{:S(2)}) collective-permute-start(f32[15,16,256]{2,1,0:T(8,128)S(1)} %pad_maximum_fusion.4), channel_id=1, source_target_pairs={{0,16},{16,32},{32,48},{48,64},{64,80},{80,96},{96,112},{112,128},... | collective-permute-start | bytes 737288 | tf_op jit(solution)/shard_map/ppermute | solution.py:12
  116.8 6.8 %collective-permute-start.5 = (f32[15,16,256]{2,1,0:T(8,128)S(1)}, f32[15,16,256]{2,1,0:T(8,128)S(1)}, u32[]{:S(2)}, u32[]{:S(2)}) collective-permute-start(f32[15,16,256]{2,1,0:T(8,128)S(1)} %pad_maximum_fusion.5), channel_id=1, source_target_pairs={{0,496},{16,0},{32,16},{48,32},{64,48},{80,64},{96,80},{112,96},{1... | collective-permute-start | bytes 737288 | tf_op jit(solution)/shard_map/ppermute | solution.py:12
  124.8 61.4 %copy-start.4 = (f32[9,7,16,256]{3,2,1,0:T(8,128)}, f32[9,7,16,256]{3,2,1,0:T(8,128)S(1)}, u32[]{:S(2)}) copy-start(f32[9,7,16,256]{3,2,1,0:T(8,128)S(1)} %bitcast_dynamic-update-slice_fusion.5.ext_ref) | copy-start | bytes 3096580
  194.1 16.4 %copy-start = (f32[3,7,16,256]{3,2,1,0:T(8,128)S(1)}, f32[3,7,16,256]{3,2,1,0:T(8,128)}, u32[]{:S(2)}) copy-start(f32[3,7,16,256]{3,2,1,0:T(8,128)} %shard_map.30) | copy-start | bytes 1032196
  194.1 7.4 %collective-permute-start.6 = (f32[15,16,256]{2,1,0:T(8,128)S(1)}, f32[15,16,256]{2,1,0:T(8,128)S(1)}, u32[]{:S(2)}, u32[]{:S(2)}) collective-permute-start(f32[15,16,256]{2,1,0:T(8,128)S(1)} %pad_maximum_fusion.6), channel_id=1, source_target_pairs={{0,16},{16,32},{32,48},{48,64},{64,80},{80,96},{96,112},{112,128},... | collective-permute-start | bytes 737288 | tf_op jit(solution)/shard_map/ppermute | solution.py:12
  194.2 8.5 %collective-permute-start.7 = (f32[15,16,256]{2,1,0:T(8,128)S(1)}, f32[15,16,256]{2,1,0:T(8,128)S(1)}, u32[]{:S(2)}, u32[]{:S(2)}) collective-permute-start(f32[15,16,256]{2,1,0:T(8,128)S(1)} %pad_maximum_fusion.7), channel_id=1, source_target_pairs={{0,496},{16,0},{32,16},{48,32},{64,48},{80,64},{96,80},{112,96},{1... | collective-permute-start | bytes 737288 | tf_op jit(solution)/shard_map/ppermute | solution.py:12
  202.8 1.0 copy-start.5
Sparse Core Ops, SparseCore 0:
  10.4 77.3 all-gather.2
  114.0 72.2 all-gather.4

commit v5 on v4

--- a/solution.py
+++ b/solution.py
@@ -1,7 +1,10 @@
+import functools
+
 import jax
 import jax.numpy as jnp
 from jax import lax
 from jax.experimental import pallas as pl
+from jax.experimental.pallas import tpu as pltpu
 from jax.sharding import PartitionSpec as P
 
 W = 3
@@ -43,7 +46,7 @@
     return jnp.concatenate([left, right, right_rows], axis=0)
 
 
-def band_kernel(ext_ref, left_ref, out_ref):
+def band_kernel(ext_ref, left_ref, keep_ref, out_ref, *, combine):
     rows = out_ref.shape[0]
     width = out_ref.shape[2]
     for i in range(rows):
@@ -57,24 +60,35 @@
                 part = res[(b - lo) * width : (b - lo + 1) * width]
                 summed[b] = part if summed[b] is None else summed[b] + part
         for b in range(2 * W + 1):
-            out_ref[i, b] = summed[b]
-def contract_kernel(extended, shard_rows):
+            masked = summed[b] * keep_ref[i, b]
+            if combine:
+                masked = 3.0 * ext_ref[W + i, b] - 2.0 * masked
+            out_ref[i, b] = masked
+
+
+def contract_kernel(extended, shard_rows, keep, combine):
     rows, bands, width, depth = extended.shape[0] - 2 * W, extended.shape[1], extended.shape[2], extended.shape[3]
     flops = 2 * rows * 37 * width * depth * shard_rows.shape[2]
     nbytes = 4 * (extended.size + shard_rows.size + rows * bands * width * depth)
-    return pl.pallas_call(band_kernel, out_shape=jax.ShapeDtypeStruct((rows, bands, width, depth), jnp.float32),
-        cost_estimate=pl.CostEstimate(flops=flops, transcendentals=0, bytes_accessed=nbytes))(extended, shard_rows)
+    vmem = pl.BlockSpec(memory_space=pltpu.VMEM)
+    return pl.pallas_call(
+        functools.partial(band_kernel, combine=combine),
+        out_shape=jax.ShapeDtypeStruct((rows, bands, width, depth), jnp.float32),
+        in_specs=[vmem, vmem, pl.BlockSpec(memory_space=pltpu.SMEM)],
+        out_specs=vmem,
+        cost_estimate=pl.CostEstimate(flops=flops, transcendentals=0, bytes_accessed=nbytes),
+    )(extended, shard_rows, keep)
 
 
 def on_device(density, band_widths):
     offsets = jnp.abs(jnp.arange(2 * W + 1, dtype=jnp.int32) - W)
     pattern = (offsets[None, :] <= band_widths[:, None]).astype(jnp.float32)[:, :, None, None]
     current = density * pattern
+    keep = pattern[:, :, 0, 0]
     for purify_step in range(2):
         gathered = lax.all_gather(current, "col", axis=2, tiled=True)
-        square = contract_kernel(extend(current), gathered) * pattern
-        third_power = contract_kernel(extend(square), gathered) * pattern
-        current = 3.0 * square - 2.0 * third_power
+        square = contract_kernel(extend(current), gathered, keep, False)
+        current = contract_kernel(extend(square), gathered, keep, True)
     return current
 
 

time: 220 us -> 220 us (level)
  other arithmetic: 12.6 us -> 4.71 us
  local copies, waits for them, and re-layouts: 8.98 us -> 16.5 us
    squeeze x12, local copies, waits for them, and re-layouts: 5.72 us -> 11.3 us  [halo_pieces(): head = [cells[k, :2 * W - k] for k in range(W)]]
    sub x2 -> x0, other arithmetic: 3.67 us -> none  [on_device(): current = 3.0 * square - 2.0 * third_power]
where the time goes in v5:
time: 220 us; the launch traced here: 219 us
  waiting for transfers between devices  138 us (63%)
  Pallas kernels  26.7 us (12%)
  starting transfers between devices  19 us (9%)
  local copies, waits for them, and re-layouts  16.5 us (8%)
  between operations  13.9 us (6%)
  other arithmetic  4.71 us (2%)
    all_gather x2, waiting for transfers between devices, on_device(): gathered = lax.all_gather(current, 'col', axis=2, tiled=True)  122 us
    pallas_call x4, Pallas kernels, contract_kernel(): pl.pallas_call(functools.partial(band_kernel, combine=combine), out_shape...  26.7 us
    ppermute x8, starting transfers between devices, send(): lax.ppermute(cells, 'blk', [(i, (i + shift) % count) for i in range(count)])  19 us
    ppermute x8, waiting for transfers between devices, send(): lax.ppermute(cells, 'blk', [(i, (i + shift) % count) for i in range(count)])  15.3 us
    squeeze x12, local copies, waits for them, and re-layouts, halo_pieces(): head = [cells[k, :2 * W - k] for k in range(W)]  11.3 us
    unnamed x31, local copies, waits for them, and re-layouts  5.1 us
  transfers between devices with their start and end apart: 10, of which 6 were waited for; matrix products, arithmetic and copies ran while one was open for 5% of the time, Pallas kernels for 0%

profile of v5, /device:TPU:6, one launch (start us, length us, event | category | flops | bytes accessed | tf_op | source)
XLA Modules:
  0.0 218.7 jit_solution(653443451071538027)
XLA Ops:
  6.5 0.7 compare_convert_fusion.keep_ref
  7.3 1.8 broadcast_multiply_fusion
  9.1 0.0 all-gather.3.cloned.1.call-update
  9.1 0.0 all-gather.5.cloned.1.call-start
  9.1 0.9 slice_bitcast_fusion.22
  10.0 1.0 slice_bitcast_fusion.14
  11.0 1.0 slice_bitcast_fusion.6
  12.0 0.0 collective-permute-start
  12.1 8.9 %collective-permute-start.1 = (f32[15,16,256]{2,1,0:T(8,128)S(1)}, f32[15,16,256]{2,1,0:T(8,128)S(1)}, u32[]{:S(2)}, u32[]{:S(2)}) collective-permute-start(f32[15,16,256]{2,1,0:T(8,128)S(1)} %pad_maximum_fusion.1), channel_id=1, source_target_pairs={{0,496},{16,0},{32,16},{48,32},{64,48},{80,64},{96,80},{112,96},{1... | collective-permute-start | bytes 737288 | tf_op jit(solution)/shard_map/ppermute | solution.py:15
  21.0 3.8 %collective-permute-done = f32[15,16,256]{2,1,0:T(8,128)S(1)} collective-permute-done((f32[15,16,256]{2,1,0:T(8,128)S(1)}, f32[15,16,256]{2,1,0:T(8,128)S(1)}, u32[]{:S(2)}, u32[]{:S(2)}) %collective-permute-start) | collective-permute-done | bytes 245792 | tf_op jit(solution)/shard_map/ppermute | solution.py:15
  24.9 0.0 collective-permute-done.1
  25.0 1.1 constant_dynamic-update-slice_fusion
  26.0 0.7 fusion.7
  26.8 0.0 copy-start.5
  26.8 61.0 %all-gather.3.cloned.1.call-done.left_ref = f32[3,7,256,256]{3,2,1,0:T(8,128)} async-done(((f32[3,7,16,256]{3,2,1,0:T(8,128)}), f32[3,7,256,256]{3,2,1,0:T(8,128)}) %all-gather.3.cloned.1.call-update) | async-done | bytes 5505040 | tf_op jit(solution)/shard_map/all_gather | solution.py:89
  87.8 6.7 %shard_map.28 = f32[3,7,16,256]{3,2,1,0:T(8,128)} custom-call(f32[9,7,16,256]{3,2,1,0:T(8,128)} %copy-done, f32[3,7,256,256]{3,2,1,0:T(8,128)} %all-gather.3.cloned.1.call-done.left_ref, f32[3,7]{1,0:T(4,128)} %copy-done.4), custom_call_target="tpu_custom_call" | custom-call | flops 232783872 | bytes 6881280 | tf_op jit(solution)/shard_map/pallas_call | solution.py:74
  94.5 0.9 slice_bitcast_fusion.20
  95.4 1.0 slice_bitcast_fusion.12
  96.3 1.0 slice_bitcast_fusion.4
  97.3 0.0 collective-permute-start.2
  97.4 3.5 %collective-permute-start.3 = (f32[15,16,256]{2,1,0:T(8,128)S(1)}, f32[15,16,256]{2,1,0:T(8,128)S(1)}, u32[]{:S(2)}, u32[]{:S(2)}) collective-permute-start(f32[15,16,256]{2,1,0:T(8,128)S(1)} %pad_maximum_fusion.3), channel_id=1, source_target_pairs={{0,496},{16,0},{32,16},{48,32},{64,48},{80,64},{96,80},{112,96},{1... | collective-permute-start | bytes 737288 | tf_op jit(solution)/shard_map/ppermute | solution.py:15
  100.9 3.8 %collective-permute-done.2 = f32[15,16,256]{2,1,0:T(8,128)S(1)} collective-permute-done((f32[15,16,256]{2,1,0:T(8,128)S(1)}, f32[15,16,256]{2,1,0:T(8,128)S(1)}, u32[]{:S(2)}, u32[]{:S(2)}) %collective-permute-start.2) | collective-permute-done | bytes 245792 | tf_op jit(solution)/shard_map/ppermute | solution.py:15
  104.8 1.0 constant_dynamic-update-slice_fusion.1
  105.8 0.1 fusion.5
  106.0 1.0 copy-done.1
  106.9 6.7 %shard_map.29 = f32[3,7,16,256]{3,2,1,0:T(8,128)} custom-call(f32[9,7,16,256]{3,2,1,0:T(8,128)} %copy-done.1, f32[3,7,256,256]{3,2,1,0:T(8,128)} %all-gather.3.cloned.1.call-done.left_ref, f32[3,7]{1,0:T(4,128)} %copy-done.4), custom_call_target="tpu_custom_call" | custom-call | flops 232783872 | bytes 6881280 | tf_op jit(solution)/shard_map/pallas_call | solution.py:74
  113.6 0.0 all-gather.5.cloned.1.call-update
  113.6 0.9 slice_bitcast_fusion.18
  114.5 1.0 slice_bitcast_fusion.10
  115.5 1.0 slice_bitcast_fusion.2
  116.5 0.0 collective-permute-start.4
  116.5 2.9 %collective-permute-start.5 = (f32[15,16,256]{2,1,0:T(8,128)S(1)}, f32[15,16,256]{2,1,0:T(8,128)S(1)}, u32[]{:S(2)}, u32[]{:S(2)}) collective-permute-start(f32[15,16,256]{2,1,0:T(8,128)S(1)} %pad_maximum_fusion.5), channel_id=1, source_target_pairs={{0,496},{16,0},{32,16},{48,32},{64,48},{80,64},{96,80},{112,96},{1... | collective-permute-start | bytes 737288 | tf_op jit(solution)/shard_map/ppermute | solution.py:15
  119.5 3.8 %collective-permute-done.4 = f32[15,16,256]{2,1,0:T(8,128)S(1)} collective-permute-done((f32[15,16,256]{2,1,0:T(8,128)S(1)}, f32[15,16,256]{2,1,0:T(8,128)S(1)}, u32[]{:S(2)}, u32[]{:S(2)}) %collective-permute-start.4) | collective-permute-done | bytes 245792 | tf_op jit(solution)/shard_map/ppermute | solution.py:15
  123.4 0.0 collective-permute-done.5
  123.5 1.0 constant_dynamic-update-slice_fusion.2
  124.5 0.1 fusion.3
  124.6 61.4 %all-gather.5.cloned.1.call-done.left_ref = f32[3,7,256,256]{3,2,1,0:T(8,128)} async-done(((f32[3,7,16,256]{3,2,1,0:T(8,128)}), f32[3,7,256,256]{3,2,1,0:T(8,128)}) %all-gather.5.cloned.1.call-update) | async-done | bytes 5505040 | tf_op jit(solution)/shard_map/all_gather | solution.py:89
  186.0 6.7 %shard_map.30 = f32[3,7,16,256]{3,2,1,0:T(8,128)} custom-call(f32[9,7,16,256]{3,2,1,0:T(8,128)} %copy-done.2, f32[3,7,256,256]{3,2,1,0:T(8,128)} %all-gather.5.cloned.1.call-done.left_ref, f32[3,7]{1,0:T(4,128)} %copy-done.4), custom_call_target="tpu_custom_call" | custom-call | flops 232783872 | bytes 6881280 | tf_op jit(solution)/shard_map/pallas_call | solution.py:74
  192.7 0.9 slice_bitcast_fusion.16
  193.6 1.0 slice_bitcast_fusion.8
  194.6 1.0 slice_bitcast_fusion
  195.6 0.0 collective-permute-start.6
  195.6 3.5 %collective-permute-start.7 = (f32[15,16,256]{2,1,0:T(8,128)S(1)}, f32[15,16,256]{2,1,0:T(8,128)S(1)}, u32[]{:S(2)}, u32[]{:S(2)}) collective-permute-start(f32[15,16,256]{2,1,0:T(8,128)S(1)} %pad_maximum_fusion.7), channel_id=1, source_target_pairs={{0,496},{16,0},{32,16},{48,32},{64,48},{80,64},{96,80},{112,96},{1... | collective-permute-start | bytes 737288 | tf_op jit(solution)/shard_map/ppermute | solution.py:15
  199.1 3.8 %collective-permute-done.6 = f32[15,16,256]{2,1,0:T(8,128)S(1)} collective-permute-done((f32[15,16,256]{2,1,0:T(8,128)S(1)}, f32[15,16,256]{2,1,0:T(8,128)S(1)}, u32[]{:S(2)}, u32[]{:S(2)}) %collective-permute-start.6) | collective-permute-done | bytes 245792 | tf_op jit(solution)/shard_map/ppermute | solution.py:15
  203.0 1.0 constant_dynamic-update-slice_fusion.3
  204.1 0.1 fusion.1
  204.2 1.0 copy-done.3
  205.2 6.7 %shard_map.31 = f32[3,7,16,256]{3,2,1,0:T(8,128)} custom-call(f32[9,7,16,256]{3,2,1,0:T(8,128)} %copy-done.3, f32[3,7,256,256]{3,2,1,0:T(8,128)} %all-gather.5.cloned.1.call-done.left_ref, f32[3,7]{1,0:T(4,128)} %copy-done.4), custom_call_target="tpu_custom_call" | custom-call | flops 232783872 | bytes 6881280 | tf_op jit(solution)/shard_map/pallas_call | solution.py:74
  (61 shorter events, 0.5 us)
Async XLA Ops:
  6.5 81.3 %all-gather.3.cloned.1.call-start = ((), (), s32[]{:S(2)}) async-start(), calls=%async_computation | async-start | bytes 5849088 | tf_op jit(solution)/shard_map/all_gather | solution.py:89
  7.3 80.5 %copy-start.4 = (f32[3,7]{1,0:T(4,128)}, f32[3,7]{1,0:T(4,128)S(1)}, u32[]{:S(2)}) copy-start(f32[3,7]{1,0:T(4,128)S(1)} %compare_convert_fusion.keep_ref) | copy-start | bytes 256
  9.1 176.9 %all-gather.5.cloned.1.call-start = ((), (), s32[]{:S(2)}) async-start(), calls=%async_computation.1 | async-start | bytes 5849088 | tf_op jit(solution)/shard_map/all_gather | solution.py:89
  12.0 12.8 %collective-permute-start = (f32[15,16,256]{2,1,0:T(8,128)S(1)}, f32[15,16,256]{2,1,0:T(8,128)S(1)}, u32[]{:S(2)}, u32[]{:S(2)}) collective-permute-start(f32[15,16,256]{2,1,0:T(8,128)S(1)} %pad_maximum_fusion), channel_id=1, source_target_pairs={{0,16},{16,32},{32,48},{48,64},{64,80},{80,96},{96,112},{112,128},... | collective-permute-start | bytes 737288 | tf_op jit(solution)/shard_map/ppermute | solution.py:15
  12.1 12.8 %collective-permute-start.1 = (f32[15,16,256]{2,1,0:T(8,128)S(1)}, f32[15,16,256]{2,1,0:T(8,128)S(1)}, u32[]{:S(2)}, u32[]{:S(2)}) collective-permute-start(f32[15,16,256]{2,1,0:T(8,128)S(1)} %pad_maximum_fusion.1), channel_id=1, source_target_pairs={{0,496},{16,0},{32,16},{48,32},{64,48},{80,64},{96,80},{112,96},{1... | collective-permute-start | bytes 737288 | tf_op jit(solution)/shard_map/ppermute | solution.py:15
  26.8 79.0 %copy-start.5 = (pred[7]{0:T(512)(128)(4,1)S(1)}, pred[7]{0:T(512)(128)(4,1)}, u32[]{:S(2)}) copy-start(pred[7]{0:T(512)(128)(4,1)} %constant.11.clone.1) | copy-start | bytes 25
  26.8 61.0 %copy-start = (f32[9,7,16,256]{3,2,1,0:T(8,128)}, f32[9,7,16,256]{3,2,1,0:T(8,128)S(1)}, u32[]{:S(2)}) copy-start(f32[9,7,16,256]{3,2,1,0:T(8,128)S(1)} %bitcast_dynamic-update-slice_fusion.15.ext_ref) | copy-start | bytes 3096580
  97.3 7.4 %collective-permute-start.2 = (f32[15,16,256]{2,1,0:T(8,128)S(1)}, f32[15,16,256]{2,1,0:T(8,128)S(1)}, u32[]{:S(2)}, u32[]{:S(2)}) collective-permute-start(f32[15,16,256]{2,1,0:T(8,128)S(1)} %pad_maximum_fusion.2), channel_id=1, source_target_pairs={{0,16},{16,32},{32,48},{48,64},{64,80},{80,96},{96,112},{112,128},... | collective-permute-start | bytes 737288 | tf_op jit(solution)/shard_map/ppermute | solution.py:15
  97.4 8.4 %collective-permute-start.3 = (f32[15,16,256]{2,1,0:T(8,128)S(1)}, f32[15,16,256]{2,1,0:T(8,128)S(1)}, u32[]{:S(2)}, u32[]{:S(2)}) collective-permute-start(f32[15,16,256]{2,1,0:T(8,128)S(1)} %pad_maximum_fusion.3), channel_id=1, source_target_pairs={{0,496},{16,0},{32,16},{48,32},{64,48},{80,64},{96,80},{112,96},{1... | collective-permute-start | bytes 737288 | tf_op jit(solution)/shard_map/ppermute | solution.py:15
  106.0 1.0 copy-start.1
  116.5 6.8 %collective-permute-start.4 = (f32[15,16,256]{2,1,0:T(8,128)S(1)}, f32[15,16,256]{2,1,0:T(8,128)S(1)}, u32[]{:S(2)}, u32[]{:S(2)}) collective-permute-start(f32[15,16,256]{2,1,0:T(8,128)S(1)} %pad_maximum_fusion.4), channel_id=1, source_target_pairs={{0,16},{16,32},{32,48},{48,64},{64,80},{80,96},{96,112},{112,128},... | collective-permute-start | bytes 737288 | tf_op jit(solution)/shard_map/ppermute | solution.py:15
  116.5 6.8 %collective-permute-start.5 = (f32[15,16,256]{2,1,0:T(8,128)S(1)}, f32[15,16,256]{2,1,0:T(8,128)S(1)}, u32[]{:S(2)}, u32[]{:S(2)}) collective-permute-start(f32[15,16,256]{2,1,0:T(8,128)S(1)} %pad_maximum_fusion.5), channel_id=1, source_target_pairs={{0,496},{16,0},{32,16},{48,32},{64,48},{80,64},{96,80},{112,96},{1... | collective-permute-start | bytes 737288 | tf_op jit(solution)/shard_map/ppermute | solution.py:15
  124.6 61.5 %copy-start.2 = (f32[9,7,16,256]{3,2,1,0:T(8,128)}, f32[9,7,16,256]{3,2,1,0:T(8,128)S(1)}, u32[]{:S(2)}) copy-start(f32[9,7,16,256]{3,2,1,0:T(8,128)S(1)} %bitcast_dynamic-update-slice_fusion.5.ext_ref) | copy-start | bytes 3096580
  195.6 7.4 %collective-permute-start.6 = (f32[15,16,256]{2,1,0:T(8,128)S(1)}, f32[15,16,256]{2,1,0:T(8,128)S(1)}, u32[]{:S(2)}, u32[]{:S(2)}) collective-permute-start(f32[15,16,256]{2,1,0:T(8,128)S(1)} %pad_maximum_fusion.6), channel_id=1, source_target_pairs={{0,16},{16,32},{32,48},{48,64},{64,80},{80,96},{96,112},{112,128},... | collective-permute-start | bytes 737288 | tf_op jit(solution)/shard_map/ppermute | solution.py:15
  195.6 8.4 %collective-permute-start.7 = (f32[15,16,256]{2,1,0:T(8,128)S(1)}, f32[15,16,256]{2,1,0:T(8,128)S(1)}, u32[]{:S(2)}, u32[]{:S(2)}) collective-permute-start(f32[15,16,256]{2,1,0:T(8,128)S(1)} %pad_maximum_fusion.7), channel_id=1, source_target_pairs={{0,496},{16,0},{32,16},{48,32},{64,48},{80,64},{96,80},{112,96},{1... | collective-permute-start | bytes 737288 | tf_op jit(solution)/shard_map/ppermute | solution.py:15
  204.2 1.0 copy-start.3
Sparse Core Ops, SparseCore 0:
  10.4 77.3 all-gather.2
  113.8 72.2 all-gather.4

commit v6 on v0

--- a/solution.py
+++ b/solution.py
@@ -28,24 +28,19 @@
 
 def contract(extended, shard_rows):
     local_rows = shard_rows.shape[0]
-    summed_bands = [None] * (2 * W + 1)
-    for inner_band in range(2 * W + 1):
-        lowest = max(0, inner_band - W)
-        highest = min(2 * W, inner_band + W)
-        source_low = lowest - inner_band + W
-        source_high = highest - inner_band + W
-        block_terms = jnp.einsum(
-            "ibcs,isr->ibcr",
-            extended[inner_band : inner_band + local_rows, source_low : source_high + 1],
-            shard_rows[:, inner_band],
-            precision=lax.Precision.HIGHEST,
-        )
-        for right_band in range(lowest, highest + 1):
-            term = block_terms[:, right_band - lowest]
-            summed_bands[right_band] = (
-                term if summed_bands[right_band] is None else summed_bands[right_band] + term
-            )
-    return jnp.stack(summed_bands, axis=1)
+    span = 2 * W + 1
+    zeros = jnp.zeros_like(extended[:local_rows, :1])
+    shifted = []
+    for inner_band in range(span):
+        window = extended[inner_band : inner_band + local_rows]
+        shift = inner_band - W
+        if shift > 0:
+            window = jnp.concatenate([zeros] * shift + [window[:, : span - shift]], axis=1)
+        elif shift < 0:
+            window = jnp.concatenate([window[:, -shift:]] + [zeros] * (-shift), axis=1)
+        shifted.append(window)
+    stacked = jnp.stack(shifted, axis=3)
+    return jnp.einsum("ibcas,iasr->ibcr", stacked, shard_rows, precision=lax.Precision.HIGHEST)
 
 
 def on_device(density, band_widths):

time: 212 us -> 209 us (0.986)
  matrix products: 26.7 us -> 17.8 us
  local copies, waits for them, and re-layouts: 0.77 us -> 4.87 us
  other arithmetic: 4.26 us -> 6.91 us
    all_gather x2, waiting for transfers between devices: 139 us -> 126 us  [on_device(): gathered = lax.all_gather(current, 'col', axis=2, tiled=True)]
    ppermute x4, waiting for transfers between devices: 8.44 us -> 20.1 us  [padded(): lax.ppermute(tail, axis, [(i, (i + 1) % count) for i in range(count)])]
    dot_general x28 -> x4, matrix products: 26.7 us -> 17.8 us  [contract(): jnp.einsum('ibcas,iasr->ibcr', stacked, shard_rows, precision=lax.Precisi...]
    unnamed x8 -> x15, local copies, waits for them, and re-layouts: 0.01 us -> 4.66 us
  transfers between devices with their start and end apart: 10 -> 10, of which waited for: 4 -> 6; matrix products, arithmetic and copies ran while one was open for 9% -> 1% of each run, Pallas kernels for 0% -> 0%
where the time goes in v6:
time: 209 us
  waiting for transfers between devices  146 us (70%)
  starting transfers between devices  19 us (9%)
  matrix products  17.8 us (9%)
  between operations  13.8 us (7%)
  other arithmetic  6.91 us (3%)
  local copies, waits for them, and re-layouts  4.87 us (2%)
    all_gather x2, waiting for transfers between devices, on_device(): gathered = lax.all_gather(current, 'col', axis=2, tiled=True)  126 us
    ppermute x4, waiting for transfers between devices, padded(): lax.ppermute(tail, axis, [(i, (i + 1) % count) for i in range(count)])  20.1 us
    ppermute x4, starting transfers between devices, padded(): lax.ppermute(head, axis, [((i + 1) % count, i) for i in range(count)])  18.9 us
    dot_general x4, matrix products, contract(): jnp.einsum('ibcas,iasr->ibcr', stacked, shard_rows, precision=lax.Precisi...  17.8 us
    unnamed x15, local copies, waits for them, and re-layouts  4.66 us
  transfers between devices with their start and end apart: 10, of which 6 were waited for; matrix products, arithmetic and copies ran while one was open for 1% of the time, Pallas kernels for 0%

profile of v6, /device:TPU:6, one launch (start us, length us, event | category | flops | bytes accessed | tf_op | source)
XLA Modules:
  0.0 208.9 jit_solution(3460034582957429222)
XLA Ops:
  6.5 0.0 copy-start.4
  6.5 0.0 all-gather.3.cloned.1.call-start
  6.5 0.8 compare_convert_fusion
  7.3 1.8 broadcast_multiply_fusion
  9.1 0.0 copy-start.3
  9.1 0.0 all-gather.3.cloned.1.call-update
  9.1 0.0 all-gather.5.cloned.1.call-start
  9.2 0.0 collective-permute-start
  9.2 8.9 %collective-permute-start.1 = (f32[3,7,16,256]{3,2,1,0:T(8,128)}, f32[3,7,16,256]{3,2,1,0:T(8,128)S(1)}, u32[]{:S(2)}, u32[]{:S(2)}) collective-permute-start(f32[3,7,16,256]{3,2,1,0:T(8,128)} %broadcast_multiply_fusion), channel_id=1, source_target_pairs={{16,0},{32,16},{48,32},{64,48},{80,64},{96,80},{112,96},{128,112},... | collective-permute-start | bytes 1032200 | tf_op jit(solution)/shard_map/ppermute | solution.py:18
  18.2 5.1 %collective-permute-done = f32[3,7,16,256]{3,2,1,0:T(8,128)S(1)} collective-permute-done((f32[3,7,16,256]{3,2,1,0:T(8,128)}, f32[3,7,16,256]{3,2,1,0:T(8,128)S(1)}, u32[]{:S(2)}, u32[]{:S(2)}) %collective-permute-start) | collective-permute-done | bytes 344096 | tf_op jit(solution)/shard_map/ppermute | solution.py:16
  23.3 0.0 collective-permute-done.1
  23.4 0.9 fusion.43
  24.3 0.0 copy-done.3
  24.3 0.0 copy-done.4
  24.3 0.1 bitcast_dynamic-update-slice_fusion.10
  24.5 63.3 %all-gather.3.cloned.1.call-done = f32[3,7,256,256]{3,2,1,0:T(8,128)} async-done(((f32[3,7,16,256]{3,2,1,0:T(8,128)}), f32[3,7,256,256]{3,2,1,0:T(8,128)}) %all-gather.3.cloned.1.call-update) | async-done | bytes 5505040 | tf_op jit(solution)/shard_map/all_gather | solution.py:51
  87.8 5.7 %fusion.6 = f32[3,7,16,256,1]{3,2,0,1,4:T(8,128)S(1)} fusion(f32[3,7,16,7,256]{4,2,1,0,3:T(8,128)S(1)} %bitcast_dynamic-update-slice_fusion.9, f32[3,7,256,256]{3,2,1,0:T(8,128)} %all-gather.3.cloned.1.call-done), kind=kOutput, calls=%fused_computation.6 | convolution fusion | flops 1849688064 | bytes 8257536 | tf_op jit(solution)/shard_map/ibcas,iasr->ibcr/dot_general | solution.py:43
  93.5 0.1 bitcast_multiply_fusion.3
  93.6 0.0 collective-permute-start.2
  93.7 3.5 %collective-permute-start.3 = (f32[3,7,16,256]{3,2,1,0:T(8,128)S(1)}, f32[3,7,16,256]{3,2,1,0:T(8,128)S(1)}, u32[]{:S(2)}, u32[]{:S(2)}) collective-permute-start(f32[3,7,16,256]{3,2,1,0:T(8,128)S(1)} %bitcast_multiply_fusion.3), channel_id=1, source_target_pairs={{16,0},{32,16},{48,32},{64,48},{80,64},{96,80},{112,96},{128,112},... | collective-permute-start | bytes 1032200 | tf_op jit(solution)/shard_map/ppermute | solution.py:18
  97.2 4.9 %collective-permute-done.2 = f32[3,7,16,256]{3,2,1,0:T(8,128)S(1)} collective-permute-done((f32[3,7,16,256]{3,2,1,0:T(8,128)S(1)}, f32[3,7,16,256]{3,2,1,0:T(8,128)S(1)}, u32[]{:S(2)}, u32[]{:S(2)}) %collective-permute-start.2) | collective-permute-done | bytes 344096 | tf_op jit(solution)/shard_map/ppermute | solution.py:16
  102.1 0.0 copy-start
  102.2 0.1 bitcast_dynamic-update-slice_fusion.7
  102.3 0.0 collective-permute-done.3
  102.4 2.3 %copy-done = f32[3,7,256,256]{3,2,1,0:T(8,128)S(1)} copy-done((f32[3,7,256,256]{3,2,1,0:T(8,128)S(1)}, f32[3,7,256,256]{3,2,1,0:T(8,128)}, u32[]{:S(2)}) %copy-start) | copy-done | bytes 5505048
  104.7 3.2 %fusion.4 = f32[3,7,16,256,1]{3,2,0,1,4:T(8,128)S(1)} fusion(f32[3,7,16,7,256]{4,2,1,0,3:T(8,128)S(1)} %bitcast_dynamic-update-slice_fusion.6, f32[3,7,256,256]{3,2,1,0:T(8,128)S(1)} %copy-done), kind=kOutput, calls=%fused_computation.4 | convolution fusion | flops 1849688064 | bytes 8257536 | tf_op jit(solution)/shard_map/ibcas,iasr->ibcr/dot_general | solution.py:43
  107.9 0.9 fusion.47
  108.7 0.0 copy-start.2
  108.7 0.0 all-gather.5.cloned.1.call-update
  108.8 0.0 collective-permute-start.4
  108.8 2.9 %collective-permute-start.5 = (f32[3,7,16,256]{3,2,1,0:T(8,128)}, f32[3,7,16,256]{3,2,1,0:T(8,128)S(1)}, u32[]{:S(2)}, u32[]{:S(2)}) collective-permute-start(f32[3,7,16,256]{3,2,1,0:T(8,128)} %fusion.47), channel_id=1, source_target_pairs={{16,0},{32,16},{48,32},{64,48},{80,64},{96,80},{112,96},{128,112},... | collective-permute-start | bytes 1032200 | tf_op jit(solution)/shard_map/ppermute | solution.py:18
  111.7 5.1 %collective-permute-done.4 = f32[3,7,16,256]{3,2,1,0:T(8,128)S(1)} collective-permute-done((f32[3,7,16,256]{3,2,1,0:T(8,128)}, f32[3,7,16,256]{3,2,1,0:T(8,128)S(1)}, u32[]{:S(2)}, u32[]{:S(2)}) %collective-permute-start.4) | collective-permute-done | bytes 344096 | tf_op jit(solution)/shard_map/ppermute | solution.py:16
  116.9 0.0 collective-permute-done.5
  116.9 0.9 fusion.27
  117.9 0.0 copy-done.2
  118.0 63.1 %all-gather.5.cloned.1.call-done = f32[3,7,256,256]{3,2,1,0:T(8,128)} async-done(((f32[3,7,16,256]{3,2,1,0:T(8,128)}), f32[3,7,256,256]{3,2,1,0:T(8,128)}) %all-gather.5.cloned.1.call-update) | async-done | bytes 5505040 | tf_op jit(solution)/shard_map/all_gather | solution.py:51
  181.2 5.7 %fusion.2 = f32[3,7,16,256,1]{3,2,0,1,4:T(8,128)S(1)} fusion(f32[3,7,16,7,256]{4,2,1,0,3:T(8,128)S(1)} %bitcast_dynamic-update-slice_fusion.3, f32[3,7,256,256]{3,2,1,0:T(8,128)} %all-gather.5.cloned.1.call-done), kind=kOutput, calls=%fused_computation.2 | convolution fusion | flops 1849688064 | bytes 8257536 | tf_op jit(solution)/shard_map/ibcas,iasr->ibcr/dot_general | solution.py:43
  186.9 0.1 bitcast_multiply_fusion.1
  187.0 0.0 collective-permute-start.6
  187.0 3.5 %collective-permute-start.7 = (f32[3,7,16,256]{3,2,1,0:T(8,128)S(1)}, f32[3,7,16,256]{3,2,1,0:T(8,128)S(1)}, u32[]{:S(2)}, u32[]{:S(2)}) collective-permute-start(f32[3,7,16,256]{3,2,1,0:T(8,128)S(1)} %bitcast_multiply_fusion.1), channel_id=1, source_target_pairs={{16,0},{32,16},{48,32},{64,48},{80,64},{96,80},{112,96},{128,112},... | collective-permute-start | bytes 1032200 | tf_op jit(solution)/shard_map/ppermute | solution.py:18
  190.5 4.9 %collective-permute-done.6 = f32[3,7,16,256]{3,2,1,0:T(8,128)S(1)} collective-permute-done((f32[3,7,16,256]{3,2,1,0:T(8,128)S(1)}, f32[3,7,16,256]{3,2,1,0:T(8,128)S(1)}, u32[]{:S(2)}, u32[]{:S(2)}) %collective-permute-start.6) | collective-permute-done | bytes 344096 | tf_op jit(solution)/shard_map/ppermute | solution.py:16
  195.5 0.0 copy-start.1
  195.6 0.1 bitcast_dynamic-update-slice_fusion.1
  195.7 0.0 collective-permute-done.7
  195.8 2.3 %copy-done.1 = f32[3,7,256,256]{3,2,1,0:T(8,128)S(1)} copy-done((f32[3,7,256,256]{3,2,1,0:T(8,128)S(1)}, f32[3,7,256,256]{3,2,1,0:T(8,128)}, u32[]{:S(2)}) %copy-start.1) | copy-done | bytes 5505048
  198.0 3.2 %fusion = f32[3,7,16,256,1]{3,2,0,1,4:T(8,128)S(1)} fusion(f32[3,7,16,7,256]{4,2,1,0,3:T(8,128)S(1)} %bitcast_dynamic-update-slice_fusion, f32[3,7,256,256]{3,2,1,0:T(8,128)S(1)} %copy-done.1), kind=kOutput, calls=%fused_computation | convolution fusion | flops 1849688064 | bytes 8257536 | tf_op jit(solution)/shard_map/ibcas,iasr->ibcr/dot_general | solution.py:43
  201.2 0.9 fusion.45
  (32 shorter events, 0.7 us)
Async XLA Ops:
  6.5 17.8 %copy-start.4 = (f32[3,7,16,256]{3,2,1,0:T(8,128)S(1)}, f32[3,7,16,256]{3,2,1,0:T(8,128)}, u32[]{:S(2)}) copy-start(f32[3,7,16,256]{3,2,1,0:T(8,128)} %param.2) | copy-start | bytes 1032196
  6.5 81.3 %all-gather.3.cloned.1.call-start = ((), (), s32[]{:S(2)}) async-start(), calls=%async_computation | async-start | bytes 5849088 | tf_op jit(solution)/shard_map/all_gather | solution.py:51
  9.1 15.2 %copy-start.3 = (f32[3,7,16,256]{3,2,1,0:T(8,128)S(1)}, f32[3,7,16,256]{3,2,1,0:T(8,128)}, u32[]{:S(2)}) copy-start(f32[3,7,16,256]{3,2,1,0:T(8,128)} %broadcast_multiply_fusion) | copy-start | bytes 1032196
  9.1 172.0 %all-gather.5.cloned.1.call-start = ((), (), s32[]{:S(2)}) async-start(), calls=%async_computation.1 | async-start | bytes 5849088 | tf_op jit(solution)/shard_map/all_gather | solution.py:51
  9.2 14.1 %collective-permute-start = (f32[3,7,16,256]{3,2,1,0:T(8,128)}, f32[3,7,16,256]{3,2,1,0:T(8,128)S(1)}, u32[]{:S(2)}, u32[]{:S(2)}) collective-permute-start(f32[3,7,16,256]{3,2,1,0:T(8,128)} %broadcast_multiply_fusion), channel_id=1, source_target_pairs={{0,16},{16,32},{32,48},{48,64},{64,80},{80,96},{96,112},{112,128},... | collective-permute-start | bytes 1032200 | tf_op jit(solution)/shard_map/ppermute | solution.py:16
  9.2 14.1 %collective-permute-start.1 = (f32[3,7,16,256]{3,2,1,0:T(8,128)}, f32[3,7,16,256]{3,2,1,0:T(8,128)S(1)}, u32[]{:S(2)}, u32[]{:S(2)}) collective-permute-start(f32[3,7,16,256]{3,2,1,0:T(8,128)} %broadcast_multiply_fusion), channel_id=1, source_target_pairs={{16,0},{32,16},{48,32},{64,48},{80,64},{96,80},{112,96},{128,112},... | collective-permute-start | bytes 1032200 | tf_op jit(solution)/shard_map/ppermute | solution.py:18
  93.6 8.4 %collective-permute-start.2 = (f32[3,7,16,256]{3,2,1,0:T(8,128)S(1)}, f32[3,7,16,256]{3,2,1,0:T(8,128)S(1)}, u32[]{:S(2)}, u32[]{:S(2)}) collective-permute-start(f32[3,7,16,256]{3,2,1,0:T(8,128)S(1)} %bitcast_multiply_fusion.3), channel_id=1, source_target_pairs={{0,16},{16,32},{32,48},{48,64},{64,80},{80,96},{96,112},{112,128},... | collective-permute-start | bytes 1032200 | tf_op jit(solution)/shard_map/ppermute | solution.py:16
  93.7 8.6 %collective-permute-start.3 = (f32[3,7,16,256]{3,2,1,0:T(8,128)S(1)}, f32[3,7,16,256]{3,2,1,0:T(8,128)S(1)}, u32[]{:S(2)}, u32[]{:S(2)}) collective-permute-start(f32[3,7,16,256]{3,2,1,0:T(8,128)S(1)} %bitcast_multiply_fusion.3), channel_id=1, source_target_pairs={{16,0},{32,16},{48,32},{64,48},{80,64},{96,80},{112,96},{128,112},... | collective-permute-start | bytes 1032200 | tf_op jit(solution)/shard_map/ppermute | solution.py:18
  102.1 2.6 %copy-start = (f32[3,7,256,256]{3,2,1,0:T(8,128)S(1)}, f32[3,7,256,256]{3,2,1,0:T(8,128)}, u32[]{:S(2)}) copy-start(f32[3,7,256,256]{3,2,1,0:T(8,128)} %all-gather.3.cloned.1.call-done) | copy-start | bytes 16515076
  108.7 9.1 %copy-start.2 = (f32[3,7,16,256]{3,2,1,0:T(8,128)S(1)}, f32[3,7,16,256]{3,2,1,0:T(8,128)}, u32[]{:S(2)}) copy-start(f32[3,7,16,256]{3,2,1,0:T(8,128)} %fusion.47) | copy-start | bytes 1032196
  108.8 8.1 %collective-permute-start.4 = (f32[3,7,16,256]{3,2,1,0:T(8,128)}, f32[3,7,16,256]{3,2,1,0:T(8,128)S(1)}, u32[]{:S(2)}, u32[]{:S(2)}) collective-permute-start(f32[3,7,16,256]{3,2,1,0:T(8,128)} %fusion.47), channel_id=1, source_target_pairs={{0,16},{16,32},{32,48},{48,64},{64,80},{80,96},{96,112},{112,128},... | collective-permute-start | bytes 1032200 | tf_op jit(solution)/shard_map/ppermute | solution.py:16
  108.8 8.1 %collective-permute-start.5 = (f32[3,7,16,256]{3,2,1,0:T(8,128)}, f32[3,7,16,256]{3,2,1,0:T(8,128)S(1)}, u32[]{:S(2)}, u32[]{:S(2)}) collective-permute-start(f32[3,7,16,256]{3,2,1,0:T(8,128)} %fusion.47), channel_id=1, source_target_pairs={{16,0},{32,16},{48,32},{64,48},{80,64},{96,80},{112,96},{128,112},... | collective-permute-start | bytes 1032200 | tf_op jit(solution)/shard_map/ppermute | solution.py:18
  187.0 8.4 %collective-permute-start.6 = (f32[3,7,16,256]{3,2,1,0:T(8,128)S(1)}, f32[3,7,16,256]{3,2,1,0:T(8,128)S(1)}, u32[]{:S(2)}, u32[]{:S(2)}) collective-permute-start(f32[3,7,16,256]{3,2,1,0:T(8,128)S(1)} %bitcast_multiply_fusion.1), channel_id=1, source_target_pairs={{0,16},{16,32},{32,48},{48,64},{64,80},{80,96},{96,112},{112,128},... | collective-permute-start | bytes 1032200 | tf_op jit(solution)/shard_map/ppermute | solution.py:16
  187.0 8.6 %collective-permute-start.7 = (f32[3,7,16,256]{3,2,1,0:T(8,128)S(1)}, f32[3,7,16,256]{3,2,1,0:T(8,128)S(1)}, u32[]{:S(2)}, u32[]{:S(2)}) collective-permute-start(f32[3,7,16,256]{3,2,1,0:T(8,128)S(1)} %bitcast_multiply_fusion.1), channel_id=1, source_target_pairs={{16,0},{32,16},{48,32},{64,48},{80,64},{96,80},{112,96},{128,112},... | collective-permute-start | bytes 1032200 | tf_op jit(solution)/shard_map/ppermute | solution.py:18
  195.5 2.6 %copy-start.1 = (f32[3,7,256,256]{3,2,1,0:T(8,128)S(1)}, f32[3,7,256,256]{3,2,1,0:T(8,128)}, u32[]{:S(2)}) copy-start(f32[3,7,256,256]{3,2,1,0:T(8,128)} %all-gather.5.cloned.1.call-done) | copy-start | bytes 16515076
Sparse Core Ops, SparseCore 0:
  10.4 77.3 all-gather.2
  108.9 72.2 all-gather.4

commit v7 on v3

--- a/solution.py
+++ b/solution.py
@@ -44,32 +44,19 @@
 
 def contract(extended, shard_rows):
     local_rows = shard_rows.shape[0]
-    summed_bands = [None] * (2 * W + 1)
-    for inner_band in range(2 * W + 1):
-        lowest = max(0, inner_band - W)
-        highest = min(2 * W, inner_band + W)
-        source_low = lowest - inner_band + W
-        source_high = highest - inner_band + W
-        block_terms = jnp.einsum(
-            "ibcs,isr->ibcr",
-            extended[inner_band : inner_band + local_rows, source_low : source_high + 1],
-            shard_rows[:, inner_band],
-            precision=lax.Precision.HIGHEST,
-        )
-        for right_band in range(lowest, highest + 1):
-            term = block_terms[:, right_band - lowest]
-            summed_bands[right_band] = (
-                term if summed_bands[right_band] is None else summed_bands[right_band] + term
-            )
-    return jnp.stack(summed_bands, axis=1)
-
-
-def gather_columns(cells):
-    count = lax.axis_size("col")
-    copies = jnp.broadcast_to(cells[None], (count,) + cells.shape)
-    pieces = lax.all_to_all(copies, "col", 0, 0, tiled=False)
-    rows, bands, width, depth = cells.shape
-    return jnp.moveaxis(pieces, 0, 2).reshape(rows, bands, count * width, depth)
+    span = 2 * W + 1
+    zeros = jnp.zeros_like(extended[:local_rows, :1])
+    shifted = []
+    for inner_band in range(span):
+        window = extended[inner_band : inner_band + local_rows]
+        shift = inner_band - W
+        if shift > 0:
+            window = jnp.concatenate([zeros] * shift + [window[:, : span - shift]], axis=1)
+        elif shift < 0:
+            window = jnp.concatenate([window[:, -shift:]] + [zeros] * (-shift), axis=1)
+        shifted.append(window)
+    stacked = jnp.stack(shifted, axis=3)
+    return jnp.einsum("ibcas,iasr->ibcr", stacked, shard_rows, precision=lax.Precision.HIGHEST)
 
 
 def on_device(density, band_widths):
@@ -77,7 +64,7 @@
     pattern = (offsets[None, :] <= band_widths[:, None]).astype(jnp.float32)[:, :, None, None]
     current = density * pattern
     for purify_step in range(2):
-        gathered = gather_columns(current)
+        gathered = lax.all_gather(current, "col", axis=2, tiled=True)
         square = contract(extend(current), gathered) * pattern
         third_power = contract(extend(square), gathered) * pattern
         current = 3.0 * square - 2.0 * third_power

time: 223 us -> 205 us (0.919); the launches traced: 219 us -> 203 us
  starting transfers between devices: 55.6 us -> 19 us
  between operations: 0.82 us -> 14.3 us
  waiting for transfers between devices: 129 us -> 140 us
  local copies, waits for them, and re-layouts: 13.2 us -> 6.16 us
    all_gather x0 -> x2, waiting for transfers between devices: none -> 125 us  [on_device(): gathered = lax.all_gather(current, 'col', axis=2, tiled=True)]
    all_to_all x2 -> x0, waiting for transfers between devices: 114 us -> none  [gather_columns(): pieces = lax.all_to_all(copies, 'col', 0, 0, tiled=False)]
    ppermute x8, starting transfers between devices: 38.3 us -> 19 us  [send(): lax.ppermute(cells, 'blk', [(i, (i + shift) % count) for i in range(count)])]
    all_to_all x2 -> x0, starting transfers between devices: 17.3 us -> none  [gather_columns(): pieces = lax.all_to_all(copies, 'col', 0, 0, tiled=False)]
    broadcast_in_dim x2 -> x0, local copies, waits for them, and re-layouts: 6.38 us -> none  [gather_columns(): copies = jnp.broadcast_to(cells[None], (count,) + cells.shape)]
    transpose x2 -> x0, local copies, waits for them, and re-layouts: 6.36 us -> none  [gather_columns(): return jnp.moveaxis(pieces, 0, 2).reshape(rows, bands, count * width, depth)]
    squeeze x12, local copies, waits for them, and re-layouts: 0.15 us -> 5.79 us  [halo_pieces(): head = [cells[k, :2 * W - k] for k in range(W)]]
    dot_general x28 -> x4, matrix products: 16.7 us -> 18.3 us  [contract(): jnp.einsum('ibcas,iasr->ibcr', stacked, shard_rows, precision=lax.Precisi...]
  transfers between devices with their start and end apart: 10 -> 10, of which waited for: 6 -> 6; matrix products, arithmetic and copies ran while one was open for 2% -> 3% of each run, Pallas kernels for 0% -> 0%
where the time goes in v7:
time: 205 us; the launch traced here: 203 us
  waiting for transfers between devices  140 us (68%)
  starting transfers between devices  19 us (9%)
  matrix products  18.3 us (9%)
  between operations  14.3 us (7%)
  local copies, waits for them, and re-layouts  6.16 us (3%)
  other arithmetic  5.74 us (3%)
    all_gather x2, waiting for transfers between devices, on_device(): gathered = lax.all_gather(current, 'col', axis=2, tiled=True)  125 us
    ppermute x8, starting transfers between devices, send(): lax.ppermute(cells, 'blk', [(i, (i + shift) % count) for i in range(count)])  19 us
    dot_general x4, matrix products, contract(): jnp.einsum('ibcas,iasr->ibcr', stacked, shard_rows, precision=lax.Precisi...  18.3 us
    ppermute x8, waiting for transfers between devices, send(): lax.ppermute(cells, 'blk', [(i, (i + shift) % count) for i in range(count)])  15.3 us
    squeeze x12, local copies, waits for them, and re-layouts, halo_pieces(): head = [cells[k, :2 * W - k] for k in range(W)]  5.79 us
  transfers between devices with their start and end apart: 10, of which 6 were waited for; matrix products, arithmetic and copies ran while one was open for 3% of the time, Pallas kernels for 0%

profile of v7, /device:TPU:6, one launch (start us, length us, event | category | flops | bytes accessed | tf_op | source)
XLA Modules:
  0.0 203.5 jit_solution(13987754492203790641)
XLA Ops:
  6.5 0.7 compare_convert_fusion
  7.3 1.8 broadcast_multiply_fusion
  9.1 0.0 all-gather.3.cloned.1.call-update
  9.1 0.0 all-gather.5.cloned.1.call-start
  9.1 0.9 slice_bitcast_fusion.22
  10.1 1.0 slice_bitcast_fusion.14
  11.0 1.0 slice_bitcast_fusion.6
  12.0 0.0 copy-start.3
  12.0 0.0 collective-permute-start
  12.1 0.0 copy-start.2
  12.1 8.9 %collective-permute-start.1 = (f32[15,16,256]{2,1,0:T(8,128)S(1)}, f32[15,16,256]{2,1,0:T(8,128)S(1)}, u32[]{:S(2)}, u32[]{:S(2)}) collective-permute-start(f32[15,16,256]{2,1,0:T(8,128)S(1)} %pad_maximum_fusion.1), channel_id=1, source_target_pairs={{0,496},{16,0},{32,16},{48,32},{64,48},{80,64},{96,80},{112,96},{1... | collective-permute-start | bytes 737288 | tf_op jit(solution)/shard_map/ppermute | solution.py:11
  21.1 3.8 %collective-permute-done = f32[15,16,256]{2,1,0:T(8,128)S(1)} collective-permute-done((f32[15,16,256]{2,1,0:T(8,128)S(1)}, f32[15,16,256]{2,1,0:T(8,128)S(1)}, u32[]{:S(2)}, u32[]{:S(2)}) %collective-permute-start) | collective-permute-done | bytes 245792 | tf_op jit(solution)/shard_map/ppermute | solution.py:11
  24.9 0.0 collective-permute-done.1
  25.1 0.1 fusion.77
  25.2 0.1 bitcast_dynamic-update-slice_fusion.3
  25.4 62.4 %all-gather.3.cloned.1.call-done = f32[3,7,256,256]{3,2,1,0:T(8,128)} async-done(((f32[3,7,16,256]{3,2,1,0:T(8,128)}), f32[3,7,256,256]{3,2,1,0:T(8,128)}) %all-gather.3.cloned.1.call-update) | async-done | bytes 5505040 | tf_op jit(solution)/shard_map/all_gather | solution.py:67
  87.8 5.9 %fusion.6 = f32[3,7,16,256,1]{3,2,0,1,4:T(8,128)S(1)} fusion(f32[3,7,16,7,256]{4,2,1,0,3:T(8,128)S(1)} %fusion.61, f32[3,7,256,256]{3,2,1,0:T(8,128)} %all-gather.3.cloned.1.call-done), kind=kOutput, calls=%fused_computation.6 | convolution fusion | flops 1849688064 | bytes 8257536 | tf_op jit(solution)/shard_map/ibcas,iasr->ibcr/dot_general | solution.py:59
  93.7 0.1 bitcast_multiply_fusion.3
  93.8 0.0 slice-start.1
  93.9 0.0 collective-permute-start.2
  93.9 3.5 %collective-permute-start.3 = (f32[15,16,256]{2,1,0:T(8,128)S(1)}, f32[15,16,256]{2,1,0:T(8,128)S(1)}, u32[]{:S(2)}, u32[]{:S(2)}) collective-permute-start(f32[15,16,256]{2,1,0:T(8,128)S(1)} %pad_maximum_fusion.3), channel_id=1, source_target_pairs={{0,496},{16,0},{32,16},{48,32},{64,48},{80,64},{96,80},{112,96},{1... | collective-permute-start | bytes 737288 | tf_op jit(solution)/shard_map/ppermute | solution.py:11
  97.4 3.8 %collective-permute-done.2 = f32[15,16,256]{2,1,0:T(8,128)S(1)} collective-permute-done((f32[15,16,256]{2,1,0:T(8,128)S(1)}, f32[15,16,256]{2,1,0:T(8,128)S(1)}, u32[]{:S(2)}, u32[]{:S(2)}) %collective-permute-start.2) | collective-permute-done | bytes 245792 | tf_op jit(solution)/shard_map/ppermute | solution.py:11
  101.4 0.1 bitcast_dynamic-update-slice_fusion.2
  101.5 0.0 collective-permute-done.3
  101.6 0.1 fusion.76
  101.8 3.2 %fusion.4 = f32[3,7,16,256,1]{3,2,0,1,4:T(8,128)S(1)} fusion(f32[3,7,16,7,256]{4,2,1,0,3:T(8,128)S(1)} %fusion.51, f32[3,7,256,256]{3,2,1,0:T(8,128)S(1)} %bitcast.239), kind=kOutput, calls=%fused_computation.4 | convolution fusion | flops 1849688064 | bytes 8257536 | tf_op jit(solution)/shard_map/ibcas,iasr->ibcr/dot_general | solution.py:59
  105.0 0.9 fusion.73
  105.9 0.0 all-gather.5.cloned.1.call-update
  105.9 0.9 slice_bitcast_fusion.18
  106.8 1.0 slice_bitcast_fusion.10
  107.8 1.0 slice_bitcast_fusion.2
  108.8 0.0 collective-permute-start.4
  108.8 2.9 %collective-permute-start.5 = (f32[15,16,256]{2,1,0:T(8,128)S(1)}, f32[15,16,256]{2,1,0:T(8,128)S(1)}, u32[]{:S(2)}, u32[]{:S(2)}) collective-permute-start(f32[15,16,256]{2,1,0:T(8,128)S(1)} %pad_maximum_fusion.5), channel_id=1, source_target_pairs={{0,496},{16,0},{32,16},{48,32},{64,48},{80,64},{96,80},{112,96},{1... | collective-permute-start | bytes 737288 | tf_op jit(solution)/shard_map/ppermute | solution.py:11
  111.8 3.8 %collective-permute-done.4 = f32[15,16,256]{2,1,0:T(8,128)S(1)} collective-permute-done((f32[15,16,256]{2,1,0:T(8,128)S(1)}, f32[15,16,256]{2,1,0:T(8,128)S(1)}, u32[]{:S(2)}, u32[]{:S(2)}) %collective-permute-start.4) | collective-permute-done | bytes 245792 | tf_op jit(solution)/shard_map/ppermute | solution.py:11
  115.7 0.0 collective-permute-done.5
  115.9 0.1 fusion.75
  116.1 62.2 %all-gather.5.cloned.1.call-done = f32[3,7,256,256]{3,2,1,0:T(8,128)} async-done(((f32[3,7,16,256]{3,2,1,0:T(8,128)}), f32[3,7,256,256]{3,2,1,0:T(8,128)}) %all-gather.5.cloned.1.call-update) | async-done | bytes 5505040 | tf_op jit(solution)/shard_map/all_gather | solution.py:67
  178.4 5.9 %fusion.2 = f32[3,7,16,256,1]{3,2,0,1,4:T(8,128)S(1)} fusion(f32[3,7,16,7,256]{4,2,1,0,3:T(8,128)S(1)} %fusion.25, f32[3,7,256,256]{3,2,1,0:T(8,128)} %all-gather.5.cloned.1.call-done), kind=kOutput, calls=%fused_computation.2 | convolution fusion | flops 1849688064 | bytes 8257536 | tf_op jit(solution)/shard_map/ibcas,iasr->ibcr/dot_general | solution.py:59
  184.2 0.1 bitcast_multiply_fusion.1
  184.3 0.0 slice-start.3
  184.4 0.0 collective-permute-start.6
  184.5 3.5 %collective-permute-start.7 = (f32[15,16,256]{2,1,0:T(8,128)S(1)}, f32[15,16,256]{2,1,0:T(8,128)S(1)}, u32[]{:S(2)}, u32[]{:S(2)}) collective-permute-start(f32[15,16,256]{2,1,0:T(8,128)S(1)} %pad_maximum_fusion.7), channel_id=1, source_target_pairs={{0,496},{16,0},{32,16},{48,32},{64,48},{80,64},{96,80},{112,96},{1... | collective-permute-start | bytes 737288 | tf_op jit(solution)/shard_map/ppermute | solution.py:11
  188.0 3.8 %collective-permute-done.6 = f32[15,16,256]{2,1,0:T(8,128)S(1)} collective-permute-done((f32[15,16,256]{2,1,0:T(8,128)S(1)}, f32[15,16,256]{2,1,0:T(8,128)S(1)}, u32[]{:S(2)}, u32[]{:S(2)}) %collective-permute-start.6) | collective-permute-done | bytes 245792 | tf_op jit(solution)/shard_map/ppermute | solution.py:11
  192.0 0.1 bitcast_dynamic-update-slice_fusion
  192.1 0.0 collective-permute-done.7
  192.2 0.1 fusion.74
  192.4 3.4 %fusion = f32[3,7,16,256,1]{3,2,0,1,4:T(8,128)S(1)} fusion(f32[3,7,16,7,256]{4,2,1,0,3:T(8,128)S(1)} %fusion.13, f32[3,7,256,256]{3,2,1,0:T(8,128)S(1)} %bitcast.241), kind=kOutput, calls=%fused_computation | convolution fusion | flops 1849688064 | bytes 8257536 | tf_op jit(solution)/shard_map/ibcas,iasr->ibcr/dot_general | solution.py:59
  195.8 0.9 fusion.71
  (93 shorter events, 1.2 us)
Async XLA Ops:
  6.5 81.3 %all-gather.3.cloned.1.call-start = ((), (), s32[]{:S(2)}) async-start(), calls=%async_computation | async-start | bytes 5849088 | tf_op jit(solution)/shard_map/all_gather | solution.py:67
  9.1 16.0 %copy-start.1 = (f32[3,7,16,256]{3,2,1,0:T(8,128)S(1)}, f32[3,7,16,256]{3,2,1,0:T(8,128)}, u32[]{:S(2)}) copy-start(f32[3,7,16,256]{3,2,1,0:T(8,128)} %broadcast_multiply_fusion) | copy-start | bytes 1032196
  9.1 169.3 %all-gather.5.cloned.1.call-start = ((), (), s32[]{:S(2)}) async-start(), calls=%async_computation.1 | async-start | bytes 5849088 | tf_op jit(solution)/shard_map/all_gather | solution.py:67
  12.0 13.1 %copy-start.3 = (pred[7]{0:T(512)(128)(4,1)S(1)}, pred[7]{0:T(512)(128)(4,1)}, u32[]{:S(2)}) copy-start(pred[7]{0:T(512)(128)(4,1)} %constant.7.clone.1) | copy-start | bytes 25
  12.0 12.8 %collective-permute-start = (f32[15,16,256]{2,1,0:T(8,128)S(1)}, f32[15,16,256]{2,1,0:T(8,128)S(1)}, u32[]{:S(2)}, u32[]{:S(2)}) collective-permute-start(f32[15,16,256]{2,1,0:T(8,128)S(1)} %pad_maximum_fusion), channel_id=1, source_target_pairs={{0,16},{16,32},{32,48},{48,64},{64,80},{80,96},{96,112},{112,128},... | collective-permute-start | bytes 737288 | tf_op jit(solution)/shard_map/ppermute | solution.py:11
  12.1 13.1 %copy-start.2 = (f32[3,7,16,256]{3,2,1,0:T(8,128)S(1)}, f32[3,7,16,256]{3,2,1,0:T(8,128)}, u32[]{:S(2)}) copy-start(f32[3,7,16,256]{3,2,1,0:T(8,128)} %param.2) | copy-start | bytes 1032196
  12.1 12.8 %collective-permute-start.1 = (f32[15,16,256]{2,1,0:T(8,128)S(1)}, f32[15,16,256]{2,1,0:T(8,128)S(1)}, u32[]{:S(2)}, u32[]{:S(2)}) collective-permute-start(f32[15,16,256]{2,1,0:T(8,128)S(1)} %pad_maximum_fusion.1), channel_id=1, source_target_pairs={{0,496},{16,0},{32,16},{48,32},{64,48},{80,64},{96,80},{112,96},{1... | collective-permute-start | bytes 737288 | tf_op jit(solution)/shard_map/ppermute | solution.py:11
  87.8 14.0 %slice-start = ((s8[5505024]{0:T(1024)(128)(4,1)}), s8[4194304]{0:T(1024)(128)(4,1)S(1)}, s32[]{:S(2)}) async-start(s8[5505024]{0:T(1024)(128)(4,1)} %bitcast.238), calls=%async_computation.2 | async-start | bytes 8388608
  93.8 8.0 %slice-start.1 = ((s8[5505024]{0:T(1024)(128)(4,1)}), s8[1310720]{0:T(1024)(128)(4,1)S(1)}, s32[]{:S(2)}) async-start(s8[5505024]{0:T(1024)(128)(4,1)} %bitcast.238), calls=%async_computation.3 | async-start | bytes 2621440
  93.9 7.4 %collective-permute-start.2 = (f32[15,16,256]{2,1,0:T(8,128)S(1)}, f32[15,16,256]{2,1,0:T(8,128)S(1)}, u32[]{:S(2)}, u32[]{:S(2)}) collective-permute-start(f32[15,16,256]{2,1,0:T(8,128)S(1)} %pad_maximum_fusion.2), channel_id=1, source_target_pairs={{0,16},{16,32},{32,48},{48,64},{64,80},{80,96},{96,112},{112,128},... | collective-permute-start | bytes 737288 | tf_op jit(solution)/shard_map/ppermute | solution.py:11
  93.9 7.6 %collective-permute-start.3 = (f32[15,16,256]{2,1,0:T(8,128)S(1)}, f32[15,16,256]{2,1,0:T(8,128)S(1)}, u32[]{:S(2)}, u32[]{:S(2)}) collective-permute-start(f32[15,16,256]{2,1,0:T(8,128)S(1)} %pad_maximum_fusion.3), channel_id=1, source_target_pairs={{0,496},{16,0},{32,16},{48,32},{64,48},{80,64},{96,80},{112,96},{1... | collective-permute-start | bytes 737288 | tf_op jit(solution)/shard_map/ppermute | solution.py:11
  105.9 10.0 %copy-start = (f32[3,7,16,256]{3,2,1,0:T(8,128)S(1)}, f32[3,7,16,256]{3,2,1,0:T(8,128)}, u32[]{:S(2)}) copy-start(f32[3,7,16,256]{3,2,1,0:T(8,128)} %fusion.73) | copy-start | bytes 1032196
  108.8 6.8 %collective-permute-start.4 = (f32[15,16,256]{2,1,0:T(8,128)S(1)}, f32[15,16,256]{2,1,0:T(8,128)S(1)}, u32[]{:S(2)}, u32[]{:S(2)}) collective-permute-start(f32[15,16,256]{2,1,0:T(8,128)S(1)} %pad_maximum_fusion.4), channel_id=1, source_target_pairs={{0,16},{16,32},{32,48},{48,64},{64,80},{80,96},{96,112},{112,128},... | collective-permute-start | bytes 737288 | tf_op jit(solution)/shard_map/ppermute | solution.py:11
  108.8 6.8 %collective-permute-start.5 = (f32[15,16,256]{2,1,0:T(8,128)S(1)}, f32[15,16,256]{2,1,0:T(8,128)S(1)}, u32[]{:S(2)}, u32[]{:S(2)}) collective-permute-start(f32[15,16,256]{2,1,0:T(8,128)S(1)} %pad_maximum_fusion.5), channel_id=1, source_target_pairs={{0,496},{16,0},{32,16},{48,32},{64,48},{80,64},{96,80},{112,96},{1... | collective-permute-start | bytes 737288 | tf_op jit(solution)/shard_map/ppermute | solution.py:11
  178.3 14.0 %slice-start.2 = ((s8[5505024]{0:T(1024)(128)(4,1)}), s8[4194304]{0:T(1024)(128)(4,1)S(1)}, s32[]{:S(2)}) async-start(s8[5505024]{0:T(1024)(128)(4,1)} %bitcast.240), calls=%async_computation.4 | async-start | bytes 8388608
  184.3 8.0 %slice-start.3 = ((s8[5505024]{0:T(1024)(128)(4,1)}), s8[1310720]{0:T(1024)(128)(4,1)S(1)}, s32[]{:S(2)}) async-start(s8[5505024]{0:T(1024)(128)(4,1)} %bitcast.240), calls=%async_computation.5 | async-start | bytes 2621440
  184.4 7.4 %collective-permute-start.6 = (f32[15,16,256]{2,1,0:T(8,128)S(1)}, f32[15,16,256]{2,1,0:T(8,128)S(1)}, u32[]{:S(2)}, u32[]{:S(2)}) collective-permute-start(f32[15,16,256]{2,1,0:T(8,128)S(1)} %pad_maximum_fusion.6), channel_id=1, source_target_pairs={{0,16},{16,32},{32,48},{48,64},{64,80},{80,96},{96,112},{112,128},... | collective-permute-start | bytes 737288 | tf_op jit(solution)/shard_map/ppermute | solution.py:11
  184.5 7.6 %collective-permute-start.7 = (f32[15,16,256]{2,1,0:T(8,128)S(1)}, f32[15,16,256]{2,1,0:T(8,128)S(1)}, u32[]{:S(2)}, u32[]{:S(2)}) collective-permute-start(f32[15,16,256]{2,1,0:T(8,128)S(1)} %pad_maximum_fusion.7), channel_id=1, source_target_pairs={{0,496},{16,0},{32,16},{48,32},{64,48},{80,64},{96,80},{112,96},{1... | collective-permute-start | bytes 737288 | tf_op jit(solution)/shard_map/ppermute | solution.py:11
Sparse Core Ops, SparseCore 0:
  10.4 77.3 all-gather.2
  106.0 72.2 all-gather.4

commit v8 on v7

--- a/solution.py
+++ b/solution.py
@@ -56,7 +56,7 @@
             window = jnp.concatenate([window[:, -shift:]] + [zeros] * (-shift), axis=1)
         shifted.append(window)
     stacked = jnp.stack(shifted, axis=3)
-    return jnp.einsum("ibcas,iasr->ibcr", stacked, shard_rows, precision=lax.Precision.HIGHEST)
+    return jnp.einsum("ibcas,iasr->ibcr", stacked, shard_rows, precision=lax.Precision.HIGH)
 
 
 def on_device(density, band_widths):

time: 205 us -> 199 us (0.971)
  matrix products: 18.3 us -> 12.3 us
    dot_general x4, matrix products: 18.3 us -> 12.3 us  [contract(): jnp.einsum('ibcas,iasr->ibcr', stacked, shard_rows, precision=lax.Precisi...]
  transfers between devices with their start and end apart: 10 -> 10, of which waited for: 6 -> 6; matrix products, arithmetic and copies ran while one was open for 3% -> 4% of each run, Pallas kernels for 0% -> 0%
where the time goes in v8:
time: 199 us; the launch traced here: 197 us
  waiting for transfers between devices  140 us (70%)
  starting transfers between devices  19 us (10%)
  between operations  14.3 us (7%)
  matrix products  12.3 us (6%)
  local copies, waits for them, and re-layouts  6.16 us (3%)
  other arithmetic  5.74 us (3%)
    all_gather x2, waiting for transfers between devices, on_device(): gathered = lax.all_gather(current, 'col', axis=2, tiled=True)  125 us
    ppermute x8, starting transfers between devices, send(): lax.ppermute(cells, 'blk', [(i, (i + shift) % count) for i in range(count)])  19 us
    ppermute x8, waiting for transfers between devices, send(): lax.ppermute(cells, 'blk', [(i, (i + shift) % count) for i in range(count)])  15.3 us
    dot_general x4, matrix products, contract(): jnp.einsum('ibcas,iasr->ibcr', stacked, shard_rows, precision=lax.Precisi...  12.3 us
    squeeze x12, local copies, waits for them, and re-layouts, halo_pieces(): head = [cells[k, :2 * W - k] for k in range(W)]  5.79 us
  transfers between devices with their start and end apart: 10, of which 6 were waited for; matrix products, arithmetic and copies ran while one was open for 4% of the time, Pallas kernels for 0%

profile of v8, /device:TPU:6, one launch (start us, length us, event | category | flops | bytes accessed | tf_op | source)
XLA Modules:
  0.0 197.5 jit_solution(4748352959868540587)
XLA Ops:
  6.5 0.7 compare_convert_fusion
  7.3 1.8 broadcast_multiply_fusion
  9.1 0.0 all-gather.3.cloned.1.call-update
  9.1 0.0 all-gather.5.cloned.1.call-start
  9.1 0.9 slice_bitcast_fusion.22
  10.1 1.0 slice_bitcast_fusion.14
  11.0 1.0 slice_bitcast_fusion.6
  12.0 0.0 copy-start.3
  12.0 0.0 collective-permute-start
  12.1 0.0 copy-start.2
  12.1 8.9 %collective-permute-start.1 = (f32[15,16,256]{2,1,0:T(8,128)S(1)}, f32[15,16,256]{2,1,0:T(8,128)S(1)}, u32[]{:S(2)}, u32[]{:S(2)}) collective-permute-start(f32[15,16,256]{2,1,0:T(8,128)S(1)} %pad_maximum_fusion.1), channel_id=1, source_target_pairs={{0,496},{16,0},{32,16},{48,32},{64,48},{80,64},{96,80},{112,96},{1... | collective-permute-start | bytes 737288 | tf_op jit(solution)/shard_map/ppermute | solution.py:11
  21.1 3.8 %collective-permute-done = f32[15,16,256]{2,1,0:T(8,128)S(1)} collective-permute-done((f32[15,16,256]{2,1,0:T(8,128)S(1)}, f32[15,16,256]{2,1,0:T(8,128)S(1)}, u32[]{:S(2)}, u32[]{:S(2)}) %collective-permute-start) | collective-permute-done | bytes 245792 | tf_op jit(solution)/shard_map/ppermute | solution.py:11
  24.9 0.0 collective-permute-done.1
  25.1 0.1 fusion.77
  25.2 0.1 bitcast_dynamic-update-slice_fusion.3
  25.4 62.4 %all-gather.3.cloned.1.call-done = f32[3,7,256,256]{3,2,1,0:T(8,128)} async-done(((f32[3,7,16,256]{3,2,1,0:T(8,128)}), f32[3,7,256,256]{3,2,1,0:T(8,128)}) %all-gather.3.cloned.1.call-update) | async-done | bytes 5505040 | tf_op jit(solution)/shard_map/all_gather | solution.py:67
  87.8 4.4 %fusion.6 = f32[3,7,16,256,1]{3,2,0,1,4:T(8,128)S(1)} fusion(f32[3,7,16,7,256]{4,2,1,0,3:T(8,128)S(1)} %fusion.61, f32[3,7,256,256]{3,2,1,0:T(8,128)} %all-gather.3.cloned.1.call-done), kind=kOutput, calls=%fused_computation.6 | convolution fusion | flops 924844032 | bytes 8257536 | tf_op jit(solution)/shard_map/ibcas,iasr->ibcr/dot_general | solution.py:59
  92.2 0.1 bitcast_multiply_fusion.3
  92.3 0.0 slice-start.1
  92.4 0.0 collective-permute-start.2
  92.5 3.5 %collective-permute-start.3 = (f32[15,16,256]{2,1,0:T(8,128)S(1)}, f32[15,16,256]{2,1,0:T(8,128)S(1)}, u32[]{:S(2)}, u32[]{:S(2)}) collective-permute-start(f32[15,16,256]{2,1,0:T(8,128)S(1)} %pad_maximum_fusion.3), channel_id=1, source_target_pairs={{0,496},{16,0},{32,16},{48,32},{64,48},{80,64},{96,80},{112,96},{1... | collective-permute-start | bytes 737288 | tf_op jit(solution)/shard_map/ppermute | solution.py:11
  96.0 3.8 %collective-permute-done.2 = f32[15,16,256]{2,1,0:T(8,128)S(1)} collective-permute-done((f32[15,16,256]{2,1,0:T(8,128)S(1)}, f32[15,16,256]{2,1,0:T(8,128)S(1)}, u32[]{:S(2)}, u32[]{:S(2)}) %collective-permute-start.2) | collective-permute-done | bytes 245792 | tf_op jit(solution)/shard_map/ppermute | solution.py:11
  100.0 0.1 bitcast_dynamic-update-slice_fusion.2
  100.1 0.0 collective-permute-done.3
  100.2 0.1 fusion.76
  100.4 1.8 fusion.4
  102.1 0.9 fusion.73
  103.0 0.0 all-gather.5.cloned.1.call-update
  103.0 0.9 slice_bitcast_fusion.18
  103.9 1.0 slice_bitcast_fusion.10
  104.9 1.0 slice_bitcast_fusion.2
  105.9 0.0 collective-permute-start.4
  106.0 2.9 %collective-permute-start.5 = (f32[15,16,256]{2,1,0:T(8,128)S(1)}, f32[15,16,256]{2,1,0:T(8,128)S(1)}, u32[]{:S(2)}, u32[]{:S(2)}) collective-permute-start(f32[15,16,256]{2,1,0:T(8,128)S(1)} %pad_maximum_fusion.5), channel_id=1, source_target_pairs={{0,496},{16,0},{32,16},{48,32},{64,48},{80,64},{96,80},{112,96},{1... | collective-permute-start | bytes 737288 | tf_op jit(solution)/shard_map/ppermute | solution.py:11
  108.9 3.8 %collective-permute-done.4 = f32[15,16,256]{2,1,0:T(8,128)S(1)} collective-permute-done((f32[15,16,256]{2,1,0:T(8,128)S(1)}, f32[15,16,256]{2,1,0:T(8,128)S(1)}, u32[]{:S(2)}, u32[]{:S(2)}) %collective-permute-start.4) | collective-permute-done | bytes 245792 | tf_op jit(solution)/shard_map/ppermute | solution.py:11
  112.8 0.0 collective-permute-done.5
  113.0 0.1 fusion.75
  113.2 62.2 %all-gather.5.cloned.1.call-done = f32[3,7,256,256]{3,2,1,0:T(8,128)} async-done(((f32[3,7,16,256]{3,2,1,0:T(8,128)}), f32[3,7,256,256]{3,2,1,0:T(8,128)}) %all-gather.5.cloned.1.call-update) | async-done | bytes 5505040 | tf_op jit(solution)/shard_map/all_gather | solution.py:67
  175.4 4.4 %fusion.2 = f32[3,7,16,256,1]{3,2,0,1,4:T(8,128)S(1)} fusion(f32[3,7,16,7,256]{4,2,1,0,3:T(8,128)S(1)} %fusion.25, f32[3,7,256,256]{3,2,1,0:T(8,128)} %all-gather.5.cloned.1.call-done), kind=kOutput, calls=%fused_computation.2 | convolution fusion | flops 924844032 | bytes 8257536 | tf_op jit(solution)/shard_map/ibcas,iasr->ibcr/dot_general | solution.py:59
  179.9 0.1 bitcast_multiply_fusion.1
  180.0 0.0 slice-start.3
  180.1 0.0 collective-permute-start.6
  180.1 3.5 %collective-permute-start.7 = (f32[15,16,256]{2,1,0:T(8,128)S(1)}, f32[15,16,256]{2,1,0:T(8,128)S(1)}, u32[]{:S(2)}, u32[]{:S(2)}) collective-permute-start(f32[15,16,256]{2,1,0:T(8,128)S(1)} %pad_maximum_fusion.7), channel_id=1, source_target_pairs={{0,496},{16,0},{32,16},{48,32},{64,48},{80,64},{96,80},{112,96},{1... | collective-permute-start | bytes 737288 | tf_op jit(solution)/shard_map/ppermute | solution.py:11
  183.6 3.8 %collective-permute-done.6 = f32[15,16,256]{2,1,0:T(8,128)S(1)} collective-permute-done((f32[15,16,256]{2,1,0:T(8,128)S(1)}, f32[15,16,256]{2,1,0:T(8,128)S(1)}, u32[]{:S(2)}, u32[]{:S(2)}) %collective-permute-start.6) | collective-permute-done | bytes 245792 | tf_op jit(solution)/shard_map/ppermute | solution.py:11
  187.6 0.1 bitcast_dynamic-update-slice_fusion
  187.7 0.0 collective-permute-done.7
  187.8 0.1 fusion.74
  188.0 1.8 fusion
  189.8 0.9 fusion.71
  (93 shorter events, 1.2 us)
Async XLA Ops:
  6.5 81.3 %all-gather.3.cloned.1.call-start = ((), (), s32[]{:S(2)}) async-start(), calls=%async_computation | async-start | bytes 5849088 | tf_op jit(solution)/shard_map/all_gather | solution.py:67
  9.1 16.0 %copy-start.1 = (f32[3,7,16,256]{3,2,1,0:T(8,128)S(1)}, f32[3,7,16,256]{3,2,1,0:T(8,128)}, u32[]{:S(2)}) copy-start(f32[3,7,16,256]{3,2,1,0:T(8,128)} %broadcast_multiply_fusion) | copy-start | bytes 1032196
  9.1 166.4 %all-gather.5.cloned.1.call-start = ((), (), s32[]{:S(2)}) async-start(), calls=%async_computation.1 | async-start | bytes 5849088 | tf_op jit(solution)/shard_map/all_gather | solution.py:67
  12.0 13.1 %copy-start.3 = (pred[7]{0:T(512)(128)(4,1)S(1)}, pred[7]{0:T(512)(128)(4,1)}, u32[]{:S(2)}) copy-start(pred[7]{0:T(512)(128)(4,1)} %constant.7.clone.1) | copy-start | bytes 25
  12.0 12.8 %collective-permute-start = (f32[15,16,256]{2,1,0:T(8,128)S(1)}, f32[15,16,256]{2,1,0:T(8,128)S(1)}, u32[]{:S(2)}, u32[]{:S(2)}) collective-permute-start(f32[15,16,256]{2,1,0:T(8,128)S(1)} %pad_maximum_fusion), channel_id=1, source_target_pairs={{0,16},{16,32},{32,48},{48,64},{64,80},{80,96},{96,112},{112,128},... | collective-permute-start | bytes 737288 | tf_op jit(solution)/shard_map/ppermute | solution.py:11
  12.1 13.1 %copy-start.2 = (f32[3,7,16,256]{3,2,1,0:T(8,128)S(1)}, f32[3,7,16,256]{3,2,1,0:T(8,128)}, u32[]{:S(2)}) copy-start(f32[3,7,16,256]{3,2,1,0:T(8,128)} %param.2) | copy-start | bytes 1032196
  12.1 12.8 %collective-permute-start.1 = (f32[15,16,256]{2,1,0:T(8,128)S(1)}, f32[15,16,256]{2,1,0:T(8,128)S(1)}, u32[]{:S(2)}, u32[]{:S(2)}) collective-permute-start(f32[15,16,256]{2,1,0:T(8,128)S(1)} %pad_maximum_fusion.1), channel_id=1, source_target_pairs={{0,496},{16,0},{32,16},{48,32},{64,48},{80,64},{96,80},{112,96},{1... | collective-permute-start | bytes 737288 | tf_op jit(solution)/shard_map/ppermute | solution.py:11
  87.8 12.5 %slice-start = ((s8[5505024]{0:T(1024)(128)(4,1)}), s8[4194304]{0:T(1024)(128)(4,1)S(1)}, s32[]{:S(2)}) async-start(s8[5505024]{0:T(1024)(128)(4,1)} %bitcast.238), calls=%async_computation.2 | async-start | bytes 8388608
  92.3 8.0 %slice-start.1 = ((s8[5505024]{0:T(1024)(128)(4,1)}), s8[1310720]{0:T(1024)(128)(4,1)S(1)}, s32[]{:S(2)}) async-start(s8[5505024]{0:T(1024)(128)(4,1)} %bitcast.238), calls=%async_computation.3 | async-start | bytes 2621440
  92.4 7.4 %collective-permute-start.2 = (f32[15,16,256]{2,1,0:T(8,128)S(1)}, f32[15,16,256]{2,1,0:T(8,128)S(1)}, u32[]{:S(2)}, u32[]{:S(2)}) collective-permute-start(f32[15,16,256]{2,1,0:T(8,128)S(1)} %pad_maximum_fusion.2), channel_id=1, source_target_pairs={{0,16},{16,32},{32,48},{48,64},{64,80},{80,96},{96,112},{112,128},... | collective-permute-start | bytes 737288 | tf_op jit(solution)/shard_map/ppermute | solution.py:11
  92.5 7.6 %collective-permute-start.3 = (f32[15,16,256]{2,1,0:T(8,128)S(1)}, f32[15,16,256]{2,1,0:T(8,128)S(1)}, u32[]{:S(2)}, u32[]{:S(2)}) collective-permute-start(f32[15,16,256]{2,1,0:T(8,128)S(1)} %pad_maximum_fusion.3), channel_id=1, source_target_pairs={{0,496},{16,0},{32,16},{48,32},{64,48},{80,64},{96,80},{112,96},{1... | collective-permute-start | bytes 737288 | tf_op jit(solution)/shard_map/ppermute | solution.py:11
  103.0 10.0 %copy-start = (f32[3,7,16,256]{3,2,1,0:T(8,128)S(1)}, f32[3,7,16,256]{3,2,1,0:T(8,128)}, u32[]{:S(2)}) copy-start(f32[3,7,16,256]{3,2,1,0:T(8,128)} %fusion.73) | copy-start | bytes 1032196
  105.9 6.8 %collective-permute-start.4 = (f32[15,16,256]{2,1,0:T(8,128)S(1)}, f32[15,16,256]{2,1,0:T(8,128)S(1)}, u32[]{:S(2)}, u32[]{:S(2)}) collective-permute-start(f32[15,16,256]{2,1,0:T(8,128)S(1)} %pad_maximum_fusion.4), channel_id=1, source_target_pairs={{0,16},{16,32},{32,48},{48,64},{64,80},{80,96},{96,112},{112,128},... | collective-permute-start | bytes 737288 | tf_op jit(solution)/shard_map/ppermute | solution.py:11
  106.0 6.8 %collective-permute-start.5 = (f32[15,16,256]{2,1,0:T(8,128)S(1)}, f32[15,16,256]{2,1,0:T(8,128)S(1)}, u32[]{:S(2)}, u32[]{:S(2)}) collective-permute-start(f32[15,16,256]{2,1,0:T(8,128)S(1)} %pad_maximum_fusion.5), channel_id=1, source_target_pairs={{0,496},{16,0},{32,16},{48,32},{64,48},{80,64},{96,80},{112,96},{1... | collective-permute-start | bytes 737288 | tf_op jit(solution)/shard_map/ppermute | solution.py:11
  175.4 12.5 %slice-start.2 = ((s8[5505024]{0:T(1024)(128)(4,1)}), s8[4194304]{0:T(1024)(128)(4,1)S(1)}, s32[]{:S(2)}) async-start(s8[5505024]{0:T(1024)(128)(4,1)} %bitcast.240), calls=%async_computation.4 | async-start | bytes 8388608
  180.0 8.0 %slice-start.3 = ((s8[5505024]{0:T(1024)(128)(4,1)}), s8[1310720]{0:T(1024)(128)(4,1)S(1)}, s32[]{:S(2)}) async-start(s8[5505024]{0:T(1024)(128)(4,1)} %bitcast.240), calls=%async_computation.5 | async-start | bytes 2621440
  180.1 7.4 %collective-permute-start.6 = (f32[15,16,256]{2,1,0:T(8,128)S(1)}, f32[15,16,256]{2,1,0:T(8,128)S(1)}, u32[]{:S(2)}, u32[]{:S(2)}) collective-permute-start(f32[15,16,256]{2,1,0:T(8,128)S(1)} %pad_maximum_fusion.6), channel_id=1, source_target_pairs={{0,16},{16,32},{32,48},{48,64},{64,80},{80,96},{96,112},{112,128},... | collective-permute-start | bytes 737288 | tf_op jit(solution)/shard_map/ppermute | solution.py:11
  180.1 7.6 %collective-permute-start.7 = (f32[15,16,256]{2,1,0:T(8,128)S(1)}, f32[15,16,256]{2,1,0:T(8,128)S(1)}, u32[]{:S(2)}, u32[]{:S(2)}) collective-permute-start(f32[15,16,256]{2,1,0:T(8,128)S(1)} %pad_maximum_fusion.7), channel_id=1, source_target_pairs={{0,496},{16,0},{32,16},{48,32},{64,48},{80,64},{96,80},{112,96},{1... | collective-permute-start | bytes 737288 | tf_op jit(solution)/shard_map/ppermute | solution.py:11
Sparse Core Ops, SparseCore 0:
  10.4 77.3 all-gather.2
  103.1 72.2 all-gather.4

commit v9 on v8

--- a/solution.py
+++ b/solution.py
@@ -42,7 +42,7 @@
     return jnp.concatenate([left, right, right_rows], axis=0)
 
 
-def contract(extended, shard_rows):
+def contract(extended, shard_rows, keep=None):
     local_rows = shard_rows.shape[0]
     span = 2 * W + 1
     zeros = jnp.zeros_like(extended[:local_rows, :1])
@@ -56,6 +56,8 @@
             window = jnp.concatenate([window[:, -shift:]] + [zeros] * (-shift), axis=1)
         shifted.append(window)
     stacked = jnp.stack(shifted, axis=3)
+    if keep is not None:
+        shard_rows = shard_rows * keep
     return jnp.einsum("ibcas,iasr->ibcr", stacked, shard_rows, precision=lax.Precision.HIGH)
 
 
@@ -64,9 +66,12 @@
     pattern = (offsets[None, :] <= band_widths[:, None]).astype(jnp.float32)[:, :, None, None]
     current = density * pattern
     for purify_step in range(2):
-        gathered = lax.all_gather(current, "col", axis=2, tiled=True)
-        square = contract(extend(current), gathered) * pattern
-        third_power = contract(extend(square), gathered) * pattern
+        if purify_step == 0:
+            gathered, keep = lax.all_gather(density, "col", axis=2, tiled=True), pattern
+        else:
+            gathered, keep = lax.all_gather(current, "col", axis=2, tiled=True), None
+        square = contract(extend(current), gathered, keep) * pattern
+        third_power = contract(extend(square), gathered, keep) * pattern
         current = 3.0 * square - 2.0 * third_power
     return current
 

time: 199 us -> 199 us (level)
  waiting for transfers between devices: 140 us -> 144 us
  local copies, waits for them, and re-layouts: 6.16 us -> 3.37 us
    all_gather x2, waiting for transfers between devices: 125 us -> 128 us  [the longest x1 65.2 us: on_device(): lax.all_gather(density, 'col', axis=2, tiled=True)]
    squeeze x12, local copies, waits for them, and re-layouts: 5.79 us -> 2.98 us  [halo_pieces(): head = [cells[k, :2 * W - k] for k in range(W)]]
  transfers between devices with their start and end apart: 10 -> 10, of which waited for: 6 -> 6; matrix products, arithmetic and copies ran while one was open for 4% -> 3% of each run, Pallas kernels for 0% -> 0%
where the time goes in v9:
time: 199 us; the launch traced here: 197 us
  waiting for transfers between devices  144 us (72%)
  starting transfers between devices  19 us (10%)
  between operations  14.3 us (7%)
  matrix products  12.3 us (6%)
  other arithmetic  4.81 us (2%)
  local copies, waits for them, and re-layouts  3.37 us (2%)
    all_gather x1, waiting for transfers between devices, on_device(): lax.all_gather(density, 'col', axis=2, tiled=True)  65.2 us
    all_gather x1, waiting for transfers between devices, on_device(): gathered, keep = (lax.all_gather(current, 'col', axis=2, tiled=True), None)  62.3 us
    ppermute x8, starting transfers between devices, send(): lax.ppermute(cells, 'blk', [(i, (i + shift) % count) for i in range(count)])  19 us
    ppermute x8, waiting for transfers between devices, send(): lax.ppermute(cells, 'blk', [(i, (i + shift) % count) for i in range(count)])  15.3 us
    dot_general x4, matrix products, contract(): jnp.einsum('ibcas,iasr->ibcr', stacked, shard_rows, precision=lax.Precisi...  12.3 us
  transfers between devices with their start and end apart: 10, of which 6 were waited for; matrix products, arithmetic and copies ran while one was open for 3% of the time, Pallas kernels for 0%

profile of v9, /device:TPU:6, one launch (start us, length us, event | category | flops | bytes accessed | tf_op | source)
XLA Modules:
  0.0 197.3 jit_solution(10707903417032842990)
XLA Ops:
  6.5 0.0 all-gather.3.cloned.1.call-start
  6.5 0.7 all-gather.3.cloned.1.call-update
  7.3 0.0 all-gather.5.cloned.1.call-start
  7.3 0.7 compare_convert_fusion
  8.0 1.1 broadcast_multiply_fusion
  9.2 0.0 copy-start.2
  9.2 0.0 collective-permute-start
  9.2 0.0 copy-start.1
  9.3 8.9 %collective-permute-start.1 = (f32[15,16,256]{2,1,0:T(8,128)S(1)}, f32[15,16,256]{2,1,0:T(8,128)S(1)}, u32[]{:S(2)}, u32[]{:S(2)}) collective-permute-start(f32[15,16,256]{2,1,0:T(8,128)S(1)} %pad_maximum_fusion.1), channel_id=1, source_target_pairs={{0,496},{16,0},{32,16},{48,32},{64,48},{80,64},{96,80},{112,96},{1... | collective-permute-start | bytes 737288 | tf_op jit(solution)/shard_map/ppermute | solution.py:11
  18.2 3.8 %collective-permute-done = f32[15,16,256]{2,1,0:T(8,128)S(1)} collective-permute-done((f32[15,16,256]{2,1,0:T(8,128)S(1)}, f32[15,16,256]{2,1,0:T(8,128)S(1)}, u32[]{:S(2)}, u32[]{:S(2)}) %collective-permute-start) | collective-permute-done | bytes 245792 | tf_op jit(solution)/shard_map/ppermute | solution.py:11
  22.1 0.0 collective-permute-done.1
  22.3 0.0 copy-done.2
  22.3 0.1 fusion.84
  22.4 0.0 copy-done.1
  22.4 0.1 bitcast_dynamic-update-slice_fusion
  22.6 65.2 %all-gather.3.cloned.1.call-done = f32[3,7,256,256]{3,2,1,0:T(8,128)} async-done(((f32[3,7,16,256]{3,2,1,0:T(8,128)}), f32[3,7,256,256]{3,2,1,0:T(8,128)}) %all-gather.3.cloned.1.call-update) | async-done | bytes 5505040 | tf_op jit(solution)/shard_map/all_gather | solution.py:70
  87.8 4.4 %fusion.16 = f32[3,7,16,256]{3,2,1,0:T(8,128)S(1)} fusion(f32[3,7,16,7,256]{4,2,3,1,0:T(8,128)S(1)} %fusion.68, f32[3,7,256,256]{3,2,1,0:T(8,128)} %all-gather.3.cloned.1.call-done, f32[3,7]{1,0:T(4,128)S(1)} %compare_convert_fusion), kind=kOutput, calls=%fused_computation.15 | convolution fusion | flops 926306304 | bytes 8257620 | tf_op jit(solution)/shard_map/ibcas,iasr->ibcr/dot_general | solution.py:61
  92.2 0.0 slice-start.1
  92.3 0.0 collective-permute-start.2
  92.4 3.5 %collective-permute-start.3 = (f32[15,16,256]{2,1,0:T(8,128)S(1)}, f32[15,16,256]{2,1,0:T(8,128)S(1)}, u32[]{:S(2)}, u32[]{:S(2)}) collective-permute-start(f32[15,16,256]{2,1,0:T(8,128)S(1)} %pad_maximum_fusion.3), channel_id=1, source_target_pairs={{0,496},{16,0},{32,16},{48,32},{64,48},{80,64},{96,80},{112,96},{1... | collective-permute-start | bytes 737288 | tf_op jit(solution)/shard_map/ppermute | solution.py:11
  95.9 3.8 %collective-permute-done.2 = f32[15,16,256]{2,1,0:T(8,128)S(1)} collective-permute-done((f32[15,16,256]{2,1,0:T(8,128)S(1)}, f32[15,16,256]{2,1,0:T(8,128)S(1)}, u32[]{:S(2)}, u32[]{:S(2)}) %collective-permute-start.2) | collective-permute-done | bytes 245792 | tf_op jit(solution)/shard_map/ppermute | solution.py:11
  99.9 0.0 collective-permute-done.3
  100.0 0.1 fusion.83
  100.2 0.0 slice-done
  100.2 0.0 slice-done.1
  100.2 1.7 fusion.2
  101.9 0.8 fusion.80
  102.7 0.0 all-gather.5.cloned.1.call-update
  102.8 0.9 slice_bitcast_fusion.18
  103.7 1.0 slice_bitcast_fusion.10
  104.7 1.0 slice_bitcast_fusion.2
  105.7 0.0 collective-permute-start.4
  105.7 2.9 %collective-permute-start.5 = (f32[15,16,256]{2,1,0:T(8,128)S(1)}, f32[15,16,256]{2,1,0:T(8,128)S(1)}, u32[]{:S(2)}, u32[]{:S(2)}) collective-permute-start(f32[15,16,256]{2,1,0:T(8,128)S(1)} %pad_maximum_fusion.5), channel_id=1, source_target_pairs={{0,496},{16,0},{32,16},{48,32},{64,48},{80,64},{96,80},{112,96},{1... | collective-permute-start | bytes 737288 | tf_op jit(solution)/shard_map/ppermute | solution.py:11
  108.7 3.8 %collective-permute-done.4 = f32[15,16,256]{2,1,0:T(8,128)S(1)} collective-permute-done((f32[15,16,256]{2,1,0:T(8,128)S(1)}, f32[15,16,256]{2,1,0:T(8,128)S(1)}, u32[]{:S(2)}, u32[]{:S(2)}) %collective-permute-start.4) | collective-permute-done | bytes 245792 | tf_op jit(solution)/shard_map/ppermute | solution.py:11
  112.5 0.0 collective-permute-done.5
  112.8 0.1 fusion.82
  113.0 62.3 %all-gather.5.cloned.1.call-done = f32[3,7,256,256]{3,2,1,0:T(8,128)} async-done(((f32[3,7,16,256]{3,2,1,0:T(8,128)}), f32[3,7,256,256]{3,2,1,0:T(8,128)}) %all-gather.5.cloned.1.call-update) | async-done | bytes 5505040 | tf_op jit(solution)/shard_map/all_gather | solution.py:72
  175.3 4.4 %fusion.6 = f32[3,7,16,256,1]{3,2,0,1,4:T(8,128)S(1)} fusion(f32[3,7,16,7,256]{4,2,1,0,3:T(8,128)S(1)} %fusion.32, f32[3,7,256,256]{3,2,1,0:T(8,128)} %all-gather.5.cloned.1.call-done), kind=kOutput, calls=%fused_computation.6 | convolution fusion | flops 924844032 | bytes 8257536 | tf_op jit(solution)/shard_map/ibcas,iasr->ibcr/dot_general | solution.py:61
  179.7 0.1 bitcast_multiply_fusion.1
  179.8 0.0 slice-start.3
  179.9 0.0 collective-permute-start.6
  179.9 3.5 %collective-permute-start.7 = (f32[15,16,256]{2,1,0:T(8,128)S(1)}, f32[15,16,256]{2,1,0:T(8,128)S(1)}, u32[]{:S(2)}, u32[]{:S(2)}) collective-permute-start(f32[15,16,256]{2,1,0:T(8,128)S(1)} %pad_maximum_fusion.7), channel_id=1, source_target_pairs={{0,496},{16,0},{32,16},{48,32},{64,48},{80,64},{96,80},{112,96},{1... | collective-permute-start | bytes 737288 | tf_op jit(solution)/shard_map/ppermute | solution.py:11
  183.4 3.8 %collective-permute-done.6 = f32[15,16,256]{2,1,0:T(8,128)S(1)} collective-permute-done((f32[15,16,256]{2,1,0:T(8,128)S(1)}, f32[15,16,256]{2,1,0:T(8,128)S(1)}, u32[]{:S(2)}, u32[]{:S(2)}) %collective-permute-start.6) | collective-permute-done | bytes 245792 | tf_op jit(solution)/shard_map/ppermute | solution.py:11
  187.5 0.1 bitcast_dynamic-update-slice_fusion.1
  187.5 0.0 collective-permute-done.7
  187.6 0.1 fusion.81
  187.8 1.8 fusion.4
  189.6 0.9 fusion.78
  (90 shorter events, 1.2 us)
Async XLA Ops:
  6.5 81.3 %all-gather.3.cloned.1.call-start = ((), (), s32[]{:S(2)}) async-start(), calls=%async_computation | async-start | bytes 5849088 | tf_op jit(solution)/shard_map/all_gather | solution.py:70
  7.3 168.0 %all-gather.5.cloned.1.call-start = ((), (), s32[]{:S(2)}) async-start(), calls=%async_computation.1 | async-start | bytes 5849088 | tf_op jit(solution)/shard_map/all_gather | solution.py:72
  9.2 13.1 %copy-start.2 = (pred[7]{0:T(512)(128)(4,1)S(1)}, pred[7]{0:T(512)(128)(4,1)}, u32[]{:S(2)}) copy-start(pred[7]{0:T(512)(128)(4,1)} %constant.7.clone.1) | copy-start | bytes 25
  9.2 12.8 %collective-permute-start = (f32[15,16,256]{2,1,0:T(8,128)S(1)}, f32[15,16,256]{2,1,0:T(8,128)S(1)}, u32[]{:S(2)}, u32[]{:S(2)}) collective-permute-start(f32[15,16,256]{2,1,0:T(8,128)S(1)} %pad_maximum_fusion), channel_id=1, source_target_pairs={{0,16},{16,32},{32,48},{48,64},{64,80},{80,96},{96,112},{112,128},... | collective-permute-start | bytes 737288 | tf_op jit(solution)/shard_map/ppermute | solution.py:11
  9.2 13.1 %copy-start.1 = (f32[3,7,16,256]{3,2,1,0:T(8,128)S(1)}, f32[3,7,16,256]{3,2,1,0:T(8,128)}, u32[]{:S(2)}) copy-start(f32[3,7,16,256]{3,2,1,0:T(8,128)} %param.2) | copy-start | bytes 1032196
  9.3 12.8 %collective-permute-start.1 = (f32[15,16,256]{2,1,0:T(8,128)S(1)}, f32[15,16,256]{2,1,0:T(8,128)S(1)}, u32[]{:S(2)}, u32[]{:S(2)}) collective-permute-start(f32[15,16,256]{2,1,0:T(8,128)S(1)} %pad_maximum_fusion.1), channel_id=1, source_target_pairs={{0,496},{16,0},{32,16},{48,32},{64,48},{80,64},{96,80},{112,96},{1... | collective-permute-start | bytes 737288 | tf_op jit(solution)/shard_map/ppermute | solution.py:11
  87.8 12.4 %slice-start = ((s8[5505024]{0:T(1024)(128)(4,1)}), s8[4194304]{0:T(1024)(128)(4,1)S(1)}, s32[]{:S(2)}) async-start(s8[5505024]{0:T(1024)(128)(4,1)} %bitcast.255), calls=%async_computation.2 | async-start | bytes 8388608
  92.2 7.9 %slice-start.1 = ((s8[5505024]{0:T(1024)(128)(4,1)}), s8[1310720]{0:T(1024)(128)(4,1)S(1)}, s32[]{:S(2)}) async-start(s8[5505024]{0:T(1024)(128)(4,1)} %bitcast.255), calls=%async_computation.3 | async-start | bytes 2621440
  92.3 7.4 %collective-permute-start.2 = (f32[15,16,256]{2,1,0:T(8,128)S(1)}, f32[15,16,256]{2,1,0:T(8,128)S(1)}, u32[]{:S(2)}, u32[]{:S(2)}) collective-permute-start(f32[15,16,256]{2,1,0:T(8,128)S(1)} %pad_maximum_fusion.2), channel_id=1, source_target_pairs={{0,16},{16,32},{32,48},{48,64},{64,80},{80,96},{96,112},{112,128},... | collective-permute-start | bytes 737288 | tf_op jit(solution)/shard_map/ppermute | solution.py:11
  92.4 7.6 %collective-permute-start.3 = (f32[15,16,256]{2,1,0:T(8,128)S(1)}, f32[15,16,256]{2,1,0:T(8,128)S(1)}, u32[]{:S(2)}, u32[]{:S(2)}) collective-permute-start(f32[15,16,256]{2,1,0:T(8,128)S(1)} %pad_maximum_fusion.3), channel_id=1, source_target_pairs={{0,496},{16,0},{32,16},{48,32},{64,48},{80,64},{96,80},{112,96},{1... | collective-permute-start | bytes 737288 | tf_op jit(solution)/shard_map/ppermute | solution.py:11
  102.7 10.0 %copy-start = (f32[3,7,16,256]{3,2,1,0:T(8,128)S(1)}, f32[3,7,16,256]{3,2,1,0:T(8,128)}, u32[]{:S(2)}) copy-start(f32[3,7,16,256]{3,2,1,0:T(8,128)} %fusion.80) | copy-start | bytes 1032196
  105.7 6.8 %collective-permute-start.4 = (f32[15,16,256]{2,1,0:T(8,128)S(1)}, f32[15,16,256]{2,1,0:T(8,128)S(1)}, u32[]{:S(2)}, u32[]{:S(2)}) collective-permute-start(f32[15,16,256]{2,1,0:T(8,128)S(1)} %pad_maximum_fusion.4), channel_id=1, source_target_pairs={{0,16},{16,32},{32,48},{48,64},{64,80},{80,96},{96,112},{112,128},... | collective-permute-start | bytes 737288 | tf_op jit(solution)/shard_map/ppermute | solution.py:11
  105.7 6.8 %collective-permute-start.5 = (f32[15,16,256]{2,1,0:T(8,128)S(1)}, f32[15,16,256]{2,1,0:T(8,128)S(1)}, u32[]{:S(2)}, u32[]{:S(2)}) collective-permute-start(f32[15,16,256]{2,1,0:T(8,128)S(1)} %pad_maximum_fusion.5), channel_id=1, source_target_pairs={{0,496},{16,0},{32,16},{48,32},{64,48},{80,64},{96,80},{112,96},{1... | collective-permute-start | bytes 737288 | tf_op jit(solution)/shard_map/ppermute | solution.py:11
  175.3 12.5 %slice-start.2 = ((s8[5505024]{0:T(1024)(128)(4,1)}), s8[4194304]{0:T(1024)(128)(4,1)S(1)}, s32[]{:S(2)}) async-start(s8[5505024]{0:T(1024)(128)(4,1)} %bitcast.257), calls=%async_computation.4 | async-start | bytes 8388608
  179.8 8.0 %slice-start.3 = ((s8[5505024]{0:T(1024)(128)(4,1)}), s8[1310720]{0:T(1024)(128)(4,1)S(1)}, s32[]{:S(2)}) async-start(s8[5505024]{0:T(1024)(128)(4,1)} %bitcast.257), calls=%async_computation.5 | async-start | bytes 2621440
  179.9 7.4 %collective-permute-start.6 = (f32[15,16,256]{2,1,0:T(8,128)S(1)}, f32[15,16,256]{2,1,0:T(8,128)S(1)}, u32[]{:S(2)}, u32[]{:S(2)}) collective-permute-start(f32[15,16,256]{2,1,0:T(8,128)S(1)} %pad_maximum_fusion.6), channel_id=1, source_target_pairs={{0,16},{16,32},{32,48},{48,64},{64,80},{80,96},{96,112},{112,128},... | collective-permute-start | bytes 737288 | tf_op jit(solution)/shard_map/ppermute | solution.py:11
  179.9 7.6 %collective-permute-start.7 = (f32[15,16,256]{2,1,0:T(8,128)S(1)}, f32[15,16,256]{2,1,0:T(8,128)S(1)}, u32[]{:S(2)}, u32[]{:S(2)}) collective-permute-start(f32[15,16,256]{2,1,0:T(8,128)S(1)} %pad_maximum_fusion.7), channel_id=1, source_target_pairs={{0,496},{16,0},{32,16},{48,32},{64,48},{80,64},{96,80},{112,96},{1... | collective-permute-start | bytes 737288 | tf_op jit(solution)/shard_map/ppermute | solution.py:11
Sparse Core Ops, SparseCore 0:
  10.4 77.3 all-gather.2
  102.9 72.3 all-gather.4

commit v10 on v9

--- a/solution.py
+++ b/solution.py
@@ -20,8 +20,22 @@
 
 def extend(right):
     tail, head = halo_pieces(right)
-    from_left = send(jnp.concatenate(tail, axis=0), 1)
-    from_right = send(jnp.concatenate(head, axis=0), -1)
+    tail = jnp.concatenate(tail, axis=0)
+    head = jnp.concatenate(head, axis=0)
+    count = lax.axis_size("blk")
+    odd = lax.axis_index("blk") % 2 == 1
+    across = lax.ppermute(
+        jnp.where(odd, tail, head),
+        "blk",
+        [(i, (i + 1) % count) if i % 2 else (i, (i - 1) % count) for i in range(count)],
+    )
+    within = lax.ppermute(
+        jnp.where(odd, head, tail),
+        "blk",
+        [(i, i - 1) if i % 2 else (i, i + 1) for i in range(count)],
+    )
+    from_left = jnp.where(odd, within, across)
+    from_right = jnp.where(odd, across, within)
     zero = jnp.zeros((1,) + right.shape[2:], right.dtype)
     rows = []
     start = 0

time: 199 us -> 206 us (1.035)
  starting transfers between devices: 19 us -> 36.5 us
  waiting for transfers between devices: 144 us -> 134 us
    ppermute x8, starting transfers between devices: 19 us -> 36.4 us  [the longest x4 28.5 us: extend(): lax.ppermute(jnp.where(odd, tail, head), 'blk', [(i, (i + 1) % count) if...]
    all_gather x1, waiting for transfers between devices: 65.2 us -> 60 us  [on_device(): lax.all_gather(density, 'col', axis=2, tiled=True)]
    all_gather x1, waiting for transfers between devices: 62.3 us -> 57.6 us  [on_device(): gathered, keep = (lax.all_gather(current, 'col', axis=2, tiled=True), None)]
where the time goes in v10:
time: 206 us
  waiting for transfers between devices  134 us (65%)
  starting transfers between devices  36.5 us (18%)
  between operations  14.3 us (7%)
  matrix products  12.3 us (6%)
  other arithmetic  4.95 us (2%)
  local copies, waits for them, and re-layouts  4.02 us (2%)
    all_gather x1, waiting for transfers between devices, on_device(): lax.all_gather(density, 'col', axis=2, tiled=True)  60 us
    all_gather x1, waiting for transfers between devices, on_device(): gathered, keep = (lax.all_gather(current, 'col', axis=2, tiled=True), None)  57.6 us
    ppermute x4, starting transfers between devices, extend(): lax.ppermute(jnp.where(odd, tail, head), 'blk', [(i, (i + 1) % count) if...  28.5 us
    ppermute x4, waiting for transfers between devices, extend(): lax.ppermute(jnp.where(odd, tail, head), 'blk', [(i, (i + 1) % count) if...  15.4 us
    dot_general x4, matrix products, contract(): jnp.einsum('ibcas,iasr->ibcr', stacked, shard_rows, precision=lax.Precisi...  12.3 us
    ppermute x4, starting transfers between devices, extend(): lax.ppermute(jnp.where(odd, head, tail), 'blk', [(i, i - 1) if i % 2 else...  7.95 us
  transfers between devices with their start and end apart: 10, of which 6 were waited for; matrix products, arithmetic and copies ran while one was open for 3% of the time, Pallas kernels for 0%

profile of v10, /device:TPU:6, one launch (start us, length us, event | category | flops | bytes accessed | tf_op | source)
XLA Modules:
  0.0 205.8 jit_solution(16128005041679561410)
XLA Ops:
  6.5 0.0 all-gather.3.cloned.1.call-start
  6.5 0.7 all-gather.3.cloned.1.call-update
  7.3 0.0 all-gather.5.cloned.1.call-start
  7.3 0.7 compare_convert_fusion
  8.1 1.1 broadcast_multiply_fusion
  9.2 1.9 collective-permute-start
  11.2 0.0 copy-start.2
  11.2 11.5 %collective-permute-start.1 = (f32[15,16,256]{2,1,0:T(8,128)S(1)}, f32[15,16,256]{2,1,0:T(8,128)S(1)}, u32[]{:S(2)}, u32[]{:S(2)}) collective-permute-start(f32[15,16,256]{2,1,0:T(8,128)S(1)} %get-tuple-element.19), channel_id=1, source_target_pairs={{0,496},{16,32},{32,16},{48,64},{64,48},{80,96},{96,80},{112,128},... | collective-permute-start | bytes 737288 | tf_op jit(solution)/shard_map/ppermute | solution.py:27
  22.7 0.0 collective-permute-done
  22.7 3.9 %collective-permute-done.1 = f32[15,16,256]{2,1,0:T(8,128)S(1)} collective-permute-done((f32[15,16,256]{2,1,0:T(8,128)S(1)}, f32[15,16,256]{2,1,0:T(8,128)S(1)}, u32[]{:S(2)}, u32[]{:S(2)}) %collective-permute-start.1) | collective-permute-done | bytes 245792 | tf_op jit(solution)/shard_map/ppermute | solution.py:27
  26.6 0.0 copy-start.1
  26.8 0.0 copy-done.2
  26.9 0.1 fusion.92
  26.9 0.6 copy-done.1
  27.6 0.1 bitcast_dynamic-update-slice_fusion
  27.8 60.0 %all-gather.3.cloned.1.call-done = f32[3,7,256,256]{3,2,1,0:T(8,128)} async-done(((f32[3,7,16,256]{3,2,1,0:T(8,128)}), f32[3,7,256,256]{3,2,1,0:T(8,128)}) %all-gather.3.cloned.1.call-update) | async-done | bytes 5505040 | tf_op jit(solution)/shard_map/all_gather | solution.py:84
  87.8 4.4 %fusion.16 = f32[3,7,16,256]{3,2,1,0:T(8,128)S(1)} fusion(f32[3,7,16,7,256]{4,2,3,1,0:T(8,128)S(1)} %fusion.68, f32[3,7,256,256]{3,2,1,0:T(8,128)} %all-gather.3.cloned.1.call-done, f32[3,7]{1,0:T(4,128)S(1)} %compare_convert_fusion), kind=kOutput, calls=%fused_computation.15 | convolution fusion | flops 926306304 | bytes 8257620 | tf_op jit(solution)/shard_map/ibcas,iasr->ibcr/dot_general | solution.py:75
  92.3 0.0 slice-start.1
  92.3 2.1 collective-permute-start.2
  94.4 6.1 %collective-permute-start.3 = (f32[15,16,256]{2,1,0:T(8,128)S(1)}, f32[15,16,256]{2,1,0:T(8,128)S(1)}, u32[]{:S(2)}, u32[]{:S(2)}) collective-permute-start(f32[15,16,256]{2,1,0:T(8,128)S(1)} %get-tuple-element.15), channel_id=1, source_target_pairs={{0,496},{16,32},{32,16},{48,64},{64,48},{80,96},{96,80},{112,128},... | collective-permute-start | bytes 737288 | tf_op jit(solution)/shard_map/ppermute | solution.py:27
  100.5 0.0 collective-permute-done.2
  100.5 3.9 %collective-permute-done.3 = f32[15,16,256]{2,1,0:T(8,128)S(1)} collective-permute-done((f32[15,16,256]{2,1,0:T(8,128)S(1)}, f32[15,16,256]{2,1,0:T(8,128)S(1)}, u32[]{:S(2)}, u32[]{:S(2)}) %collective-permute-start.3) | collective-permute-done | bytes 245792 | tf_op jit(solution)/shard_map/ppermute | solution.py:27
  104.4 0.1 fusion.91
  104.9 1.7 fusion.2
  106.6 0.8 fusion.80
  107.4 0.0 all-gather.5.cloned.1.call-update
  107.4 0.9 slice_bitcast_fusion.19
  108.3 1.0 slice_bitcast_fusion.11
  109.3 0.0 copy-start
  109.3 1.0 slice_bitcast_fusion.3
  110.4 1.9 collective-permute-start.4
  112.3 4.9 %collective-permute-start.5 = (f32[15,16,256]{2,1,0:T(8,128)S(1)}, f32[15,16,256]{2,1,0:T(8,128)S(1)}, u32[]{:S(2)}, u32[]{:S(2)}) collective-permute-start(f32[15,16,256]{2,1,0:T(8,128)S(1)} %get-tuple-element.11), channel_id=1, source_target_pairs={{0,496},{16,32},{32,16},{48,64},{64,48},{80,96},{96,80},{112,128},... | collective-permute-start | bytes 737288 | tf_op jit(solution)/shard_map/ppermute | solution.py:27
  117.1 0.0 collective-permute-done.4
  117.2 3.9 %collective-permute-done.5 = f32[15,16,256]{2,1,0:T(8,128)S(1)} collective-permute-done((f32[15,16,256]{2,1,0:T(8,128)S(1)}, f32[15,16,256]{2,1,0:T(8,128)S(1)}, u32[]{:S(2)}, u32[]{:S(2)}) %collective-permute-start.5) | collective-permute-done | bytes 245792 | tf_op jit(solution)/shard_map/ppermute | solution.py:27
  121.2 0.0 copy-done
  121.3 0.1 fusion.90
  121.5 57.6 %all-gather.5.cloned.1.call-done = f32[3,7,256,256]{3,2,1,0:T(8,128)} async-done(((f32[3,7,16,256]{3,2,1,0:T(8,128)}), f32[3,7,256,256]{3,2,1,0:T(8,128)}) %all-gather.5.cloned.1.call-update) | async-done | bytes 5505040 | tf_op jit(solution)/shard_map/all_gather | solution.py:86
  179.1 4.4 %fusion.6 = f32[3,7,16,256,1]{3,2,0,1,4:T(8,128)S(1)} fusion(f32[3,7,16,7,256]{4,2,1,0,3:T(8,128)S(1)} %fusion.32, f32[3,7,256,256]{3,2,1,0:T(8,128)} %all-gather.5.cloned.1.call-done), kind=kOutput, calls=%fused_computation.6 | convolution fusion | flops 924844032 | bytes 8257536 | tf_op jit(solution)/shard_map/ibcas,iasr->ibcr/dot_general | solution.py:75
  183.6 0.1 bitcast_multiply_fusion.1
  183.7 0.0 slice-start.3
  183.8 2.1 collective-permute-start.6
  185.8 6.1 %collective-permute-start.7 = (f32[15,16,256]{2,1,0:T(8,128)S(1)}, f32[15,16,256]{2,1,0:T(8,128)S(1)}, u32[]{:S(2)}, u32[]{:S(2)}) collective-permute-start(f32[15,16,256]{2,1,0:T(8,128)S(1)} %get-tuple-element.7), channel_id=1, source_target_pairs={{0,496},{16,32},{32,16},{48,64},{64,48},{80,96},{96,80},{112,128},... | collective-permute-start | bytes 737288 | tf_op jit(solution)/shard_map/ppermute | solution.py:27
  191.9 0.0 collective-permute-done.6
  191.9 3.9 %collective-permute-done.7 = f32[15,16,256]{2,1,0:T(8,128)S(1)} collective-permute-done((f32[15,16,256]{2,1,0:T(8,128)S(1)}, f32[15,16,256]{2,1,0:T(8,128)S(1)}, u32[]{:S(2)}, u32[]{:S(2)}) %collective-permute-start.7) | collective-permute-done | bytes 245792 | tf_op jit(solution)/shard_map/ppermute | solution.py:27
  195.9 0.1 fusion.89
  196.1 0.1 bitcast_dynamic-update-slice_fusion.1
  196.4 1.8 fusion.4
  198.1 0.9 fusion.78
  (90 shorter events, 1.4 us)
Async XLA Ops:
  6.5 81.3 %all-gather.3.cloned.1.call-start = ((), (), s32[]{:S(2)}) async-start(), calls=%async_computation | async-start | bytes 5849088 | tf_op jit(solution)/shard_map/all_gather | solution.py:84
  7.3 171.9 %all-gather.5.cloned.1.call-start = ((), (), s32[]{:S(2)}) async-start(), calls=%async_computation.1 | async-start | bytes 5849088 | tf_op jit(solution)/shard_map/all_gather | solution.py:86
  9.2 13.5 %collective-permute-start = (f32[15,16,256]{2,1,0:T(8,128)S(1)}, f32[15,16,256]{2,1,0:T(8,128)S(1)}, u32[]{:S(2)}, u32[]{:S(2)}) collective-permute-start(f32[15,16,256]{2,1,0:T(8,128)S(1)} %get-tuple-element.20), channel_id=1, source_target_pairs={{0,16},{16,0},{32,48},{48,32},{64,80},{80,64},{96,112},{112,96},{1... | collective-permute-start | bytes 737288 | tf_op jit(solution)/shard_map/ppermute | solution.py:32
  11.2 15.7 %copy-start.2 = (pred[7]{0:T(512)(128)(4,1)S(1)}, pred[7]{0:T(512)(128)(4,1)}, u32[]{:S(2)}) copy-start(pred[7]{0:T(512)(128)(4,1)} %constant.42.clone.1) | copy-start | bytes 25
  11.2 15.4 %collective-permute-start.1 = (f32[15,16,256]{2,1,0:T(8,128)S(1)}, f32[15,16,256]{2,1,0:T(8,128)S(1)}, u32[]{:S(2)}, u32[]{:S(2)}) collective-permute-start(f32[15,16,256]{2,1,0:T(8,128)S(1)} %get-tuple-element.19), channel_id=1, source_target_pairs={{0,496},{16,32},{32,16},{48,64},{64,48},{80,96},{96,80},{112,128},... | collective-permute-start | bytes 737288 | tf_op jit(solution)/shard_map/ppermute | solution.py:27
  26.6 1.0 copy-start.1
  87.8 17.0 %slice-start = ((s8[5505024]{0:T(1024)(128)(4,1)}), s8[4194304]{0:T(1024)(128)(4,1)S(1)}, s32[]{:S(2)}) async-start(s8[5505024]{0:T(1024)(128)(4,1)} %bitcast.255), calls=%async_computation.2 | async-start | bytes 8388608
  92.3 12.6 %slice-start.1 = ((s8[5505024]{0:T(1024)(128)(4,1)}), s8[1310720]{0:T(1024)(128)(4,1)S(1)}, s32[]{:S(2)}) async-start(s8[5505024]{0:T(1024)(128)(4,1)} %bitcast.255), calls=%async_computation.3 | async-start | bytes 2621440
  92.3 8.1 %collective-permute-start.2 = (f32[15,16,256]{2,1,0:T(8,128)S(1)}, f32[15,16,256]{2,1,0:T(8,128)S(1)}, u32[]{:S(2)}, u32[]{:S(2)}) collective-permute-start(f32[15,16,256]{2,1,0:T(8,128)S(1)} %get-tuple-element.16), channel_id=1, source_target_pairs={{0,16},{16,0},{32,48},{48,32},{64,80},{80,64},{96,112},{112,96},{1... | collective-permute-start | bytes 737288 | tf_op jit(solution)/shard_map/ppermute | solution.py:32
  94.4 9.9 %collective-permute-start.3 = (f32[15,16,256]{2,1,0:T(8,128)S(1)}, f32[15,16,256]{2,1,0:T(8,128)S(1)}, u32[]{:S(2)}, u32[]{:S(2)}) collective-permute-start(f32[15,16,256]{2,1,0:T(8,128)S(1)} %get-tuple-element.15), channel_id=1, source_target_pairs={{0,496},{16,32},{32,16},{48,64},{64,48},{80,96},{96,80},{112,128},... | collective-permute-start | bytes 737288 | tf_op jit(solution)/shard_map/ppermute | solution.py:27
  109.3 12.0 %copy-start = (f32[3,7,16,256]{3,2,1,0:T(8,128)S(1)}, f32[3,7,16,256]{3,2,1,0:T(8,128)}, u32[]{:S(2)}) copy-start(f32[3,7,16,256]{3,2,1,0:T(8,128)} %fusion.80) | copy-start | bytes 1032196
  110.4 6.8 %collective-permute-start.4 = (f32[15,16,256]{2,1,0:T(8,128)S(1)}, f32[15,16,256]{2,1,0:T(8,128)S(1)}, u32[]{:S(2)}, u32[]{:S(2)}) collective-permute-start(f32[15,16,256]{2,1,0:T(8,128)S(1)} %get-tuple-element.12), channel_id=1, source_target_pairs={{0,16},{16,0},{32,48},{48,32},{64,80},{80,64},{96,112},{112,96},{1... | collective-permute-start | bytes 737288 | tf_op jit(solution)/shard_map/ppermute | solution.py:32
  112.3 8.7 %collective-permute-start.5 = (f32[15,16,256]{2,1,0:T(8,128)S(1)}, f32[15,16,256]{2,1,0:T(8,128)S(1)}, u32[]{:S(2)}, u32[]{:S(2)}) collective-permute-start(f32[15,16,256]{2,1,0:T(8,128)S(1)} %get-tuple-element.11), channel_id=1, source_target_pairs={{0,496},{16,32},{32,16},{48,64},{64,48},{80,96},{96,80},{112,128},... | collective-permute-start | bytes 737288 | tf_op jit(solution)/shard_map/ppermute | solution.py:27
  179.1 17.2 %slice-start.2 = ((s8[5505024]{0:T(1024)(128)(4,1)}), s8[4194304]{0:T(1024)(128)(4,1)S(1)}, s32[]{:S(2)}) async-start(s8[5505024]{0:T(1024)(128)(4,1)} %bitcast.257), calls=%async_computation.4 | async-start | bytes 8388608
  183.7 12.6 %slice-start.3 = ((s8[5505024]{0:T(1024)(128)(4,1)}), s8[1310720]{0:T(1024)(128)(4,1)S(1)}, s32[]{:S(2)}) async-start(s8[5505024]{0:T(1024)(128)(4,1)} %bitcast.257), calls=%async_computation.5 | async-start | bytes 2621440
  183.8 8.1 %collective-permute-start.6 = (f32[15,16,256]{2,1,0:T(8,128)S(1)}, f32[15,16,256]{2,1,0:T(8,128)S(1)}, u32[]{:S(2)}, u32[]{:S(2)}) collective-permute-start(f32[15,16,256]{2,1,0:T(8,128)S(1)} %get-tuple-element.8), channel_id=1, source_target_pairs={{0,16},{16,0},{32,48},{48,32},{64,80},{80,64},{96,112},{112,96},{1... | collective-permute-start | bytes 737288 | tf_op jit(solution)/shard_map/ppermute | solution.py:32
  185.8 9.9 %collective-permute-start.7 = (f32[15,16,256]{2,1,0:T(8,128)S(1)}, f32[15,16,256]{2,1,0:T(8,128)S(1)}, u32[]{:S(2)}, u32[]{:S(2)}) collective-permute-start(f32[15,16,256]{2,1,0:T(8,128)S(1)} %get-tuple-element.7), channel_id=1, source_target_pairs={{0,496},{16,32},{32,16},{48,64},{64,48},{80,96},{96,80},{112,128},... | collective-permute-start | bytes 737288 | tf_op jit(solution)/shard_map/ppermute | solution.py:27
Sparse Core Ops, SparseCore 0:
  10.4 77.3 all-gather.2
  107.5 71.5 all-gather.4

commit v11 on v9

--- a/solution.py
+++ b/solution.py
@@ -42,7 +42,7 @@
     return jnp.concatenate([left, right, right_rows], axis=0)
 
 
-def contract(extended, shard_rows, keep=None):
+def contract(extended, shard_rows, keep=None, scale=None):
     local_rows = shard_rows.shape[0]
     span = 2 * W + 1
     zeros = jnp.zeros_like(extended[:local_rows, :1])
@@ -56,6 +56,8 @@
             window = jnp.concatenate([window[:, -shift:]] + [zeros] * (-shift), axis=1)
         shifted.append(window)
     stacked = jnp.stack(shifted, axis=3)
+    if scale is not None:
+        stacked = stacked * scale[:, :, :, None]
     if keep is not None:
         shard_rows = shard_rows * keep
     return jnp.einsum("ibcas,iasr->ibcr", stacked, shard_rows, precision=lax.Precision.HIGH)
@@ -71,8 +73,8 @@
         else:
             gathered, keep = lax.all_gather(current, "col", axis=2, tiled=True), None
         square = contract(extend(current), gathered, keep) * pattern
-        third_power = contract(extend(square), gathered, keep) * pattern
-        current = 3.0 * square - 2.0 * third_power
+        scaled_third = contract(extend(square), gathered, keep, -2.0 * pattern)
+        current = 3.0 * square + scaled_third
     return current
 
 

time: 199 us -> 199 us (level)
  no operation moved by 1% of the time
where the time goes in v11:
time: 199 us; the launch traced here: 197 us
  waiting for transfers between devices  144 us (72%)
  starting transfers between devices  19 us (10%)
  between operations  14.3 us (7%)
  matrix products  12.4 us (6%)
  other arithmetic  4.8 us (2%)
  local copies, waits for them, and re-layouts  3.38 us (2%)
    all_gather x1, waiting for transfers between devices, on_device(): lax.all_gather(density, 'col', axis=2, tiled=True)  65.2 us
    all_gather x1, waiting for transfers between devices, on_device(): gathered, keep = (lax.all_gather(current, 'col', axis=2, tiled=True), None)  62.4 us
    ppermute x8, starting transfers between devices, send(): lax.ppermute(cells, 'blk', [(i, (i + shift) % count) for i in range(count)])  19 us
    ppermute x8, waiting for transfers between devices, send(): lax.ppermute(cells, 'blk', [(i, (i + shift) % count) for i in range(count)])  15.3 us
    dot_general x4, matrix products, contract(): jnp.einsum('ibcas,iasr->ibcr', stacked, shard_rows, precision=lax.Precisi...  12.4 us
  transfers between devices with their start and end apart: 10, of which 6 were waited for; matrix products, arithmetic and copies ran while one was open for 3% of the time, Pallas kernels for 0%

profile of v11, /device:TPU:6, one launch (start us, length us, event | category | flops | bytes accessed | tf_op | source)
XLA Modules:
  0.0 197.5 jit_solution(13729601706990014882)
XLA Ops:
  6.5 0.7 all-gather.3.cloned.1.call-update
  7.3 0.0 all-gather.5.cloned.1.call-start
  7.3 0.7 compare_convert_fusion
  8.0 1.1 broadcast_multiply_fusion.2
  9.2 0.0 copy-start.2
  9.2 0.0 collective-permute-start
  9.2 0.0 copy-start.1
  9.3 8.9 %collective-permute-start.1 = (f32[15,16,256]{2,1,0:T(8,128)S(1)}, f32[15,16,256]{2,1,0:T(8,128)S(1)}, u32[]{:S(2)}, u32[]{:S(2)}) collective-permute-start(f32[15,16,256]{2,1,0:T(8,128)S(1)} %pad_maximum_fusion.1), channel_id=1, source_target_pairs={{0,496},{16,0},{32,16},{48,32},{64,48},{80,64},{96,80},{112,96},{1... | collective-permute-start | bytes 737288 | tf_op jit(solution)/shard_map/ppermute | solution.py:11
  18.2 3.8 %collective-permute-done = f32[15,16,256]{2,1,0:T(8,128)S(1)} collective-permute-done((f32[15,16,256]{2,1,0:T(8,128)S(1)}, f32[15,16,256]{2,1,0:T(8,128)S(1)}, u32[]{:S(2)}, u32[]{:S(2)}) %collective-permute-start) | collective-permute-done | bytes 245792 | tf_op jit(solution)/shard_map/ppermute | solution.py:11
  22.1 0.0 collective-permute-done.1
  22.3 0.0 copy-done.2
  22.3 0.1 fusion.80
  22.4 0.1 bitcast_dynamic-update-slice_fusion
  22.6 0.0 copy-start.3
  22.6 65.2 %all-gather.3.cloned.1.call-done = f32[3,7,256,256]{3,2,1,0:T(8,128)} async-done(((f32[3,7,16,256]{3,2,1,0:T(8,128)}), f32[3,7,256,256]{3,2,1,0:T(8,128)}) %all-gather.3.cloned.1.call-update) | async-done | bytes 5505040 | tf_op jit(solution)/shard_map/all_gather | solution.py:72
  87.8 4.4 %fusion.16 = f32[3,7,16,256]{3,2,1,0:T(8,128)S(1)} fusion(f32[3,7,16,7,256]{4,2,3,1,0:T(8,128)S(1)} %fusion.68, f32[3,7,256,256]{3,2,1,0:T(8,128)} %all-gather.3.cloned.1.call-done, f32[3,7]{1,0:T(4,128)S(1)} %compare_convert_fusion), kind=kOutput, calls=%fused_computation.17 | convolution fusion | flops 926306304 | bytes 8257620 | tf_op jit(solution)/shard_map/ibcas,iasr->ibcr/dot_general | solution.py:63
  92.2 0.0 slice-start.1
  92.3 0.0 collective-permute-start.2
  92.3 0.1 compare_select_fusion
  92.4 3.5 %collective-permute-start.3 = (f32[15,16,256]{2,1,0:T(8,128)S(1)}, f32[15,16,256]{2,1,0:T(8,128)S(1)}, u32[]{:S(2)}, u32[]{:S(2)}) collective-permute-start(f32[15,16,256]{2,1,0:T(8,128)S(1)} %pad_maximum_fusion.3), channel_id=1, source_target_pairs={{0,496},{16,0},{32,16},{48,32},{64,48},{80,64},{96,80},{112,96},{1... | collective-permute-start | bytes 737288 | tf_op jit(solution)/shard_map/ppermute | solution.py:11
  95.9 3.8 %collective-permute-done.2 = f32[15,16,256]{2,1,0:T(8,128)S(1)} collective-permute-done((f32[15,16,256]{2,1,0:T(8,128)S(1)}, f32[15,16,256]{2,1,0:T(8,128)S(1)}, u32[]{:S(2)}, u32[]{:S(2)}) %collective-permute-start.2) | collective-permute-done | bytes 245792 | tf_op jit(solution)/shard_map/ppermute | solution.py:11
  99.9 0.0 collective-permute-done.3
  100.0 0.1 fusion.79
  100.2 1.8 fusion.2
  102.0 0.8 bitcast_add_fusion.1
  102.8 0.0 all-gather.5.cloned.1.call-update
  102.8 0.9 slice_bitcast_fusion.18
  103.8 1.0 slice_bitcast_fusion.10
  104.7 1.0 slice_bitcast_fusion.2
  105.7 0.0 collective-permute-start.4
  105.8 2.9 %collective-permute-start.5 = (f32[15,16,256]{2,1,0:T(8,128)S(1)}, f32[15,16,256]{2,1,0:T(8,128)S(1)}, u32[]{:S(2)}, u32[]{:S(2)}) collective-permute-start(f32[15,16,256]{2,1,0:T(8,128)S(1)} %pad_maximum_fusion.5), channel_id=1, source_target_pairs={{0,496},{16,0},{32,16},{48,32},{64,48},{80,64},{96,80},{112,96},{1... | collective-permute-start | bytes 737288 | tf_op jit(solution)/shard_map/ppermute | solution.py:11
  108.7 3.8 %collective-permute-done.4 = f32[15,16,256]{2,1,0:T(8,128)S(1)} collective-permute-done((f32[15,16,256]{2,1,0:T(8,128)S(1)}, f32[15,16,256]{2,1,0:T(8,128)S(1)}, u32[]{:S(2)}, u32[]{:S(2)}) %collective-permute-start.4) | collective-permute-done | bytes 245792 | tf_op jit(solution)/shard_map/ppermute | solution.py:11
  112.6 0.0 collective-permute-done.5
  112.8 0.1 fusion.78
  113.0 62.4 %all-gather.5.cloned.1.call-done = f32[3,7,256,256]{3,2,1,0:T(8,128)} async-done(((f32[3,7,16,256]{3,2,1,0:T(8,128)}), f32[3,7,256,256]{3,2,1,0:T(8,128)}) %all-gather.5.cloned.1.call-update) | async-done | bytes 5505040 | tf_op jit(solution)/shard_map/all_gather | solution.py:74
  175.4 4.4 %fusion.6 = f32[3,7,16,256,1]{3,2,0,1,4:T(8,128)S(1)} fusion(f32[3,7,16,7,256]{4,2,1,0,3:T(8,128)S(1)} %fusion.32, f32[3,7,256,256]{3,2,1,0:T(8,128)} %all-gather.5.cloned.1.call-done), kind=kOutput, calls=%fused_computation.6 | convolution fusion | flops 924844032 | bytes 8257536 | tf_op jit(solution)/shard_map/ibcas,iasr->ibcr/dot_general | solution.py:63
  179.8 0.1 bitcast_multiply_fusion
  179.9 0.0 slice-start.3
  180.0 0.0 collective-permute-start.6
  180.1 3.5 %collective-permute-start.7 = (f32[15,16,256]{2,1,0:T(8,128)S(1)}, f32[15,16,256]{2,1,0:T(8,128)S(1)}, u32[]{:S(2)}, u32[]{:S(2)}) collective-permute-start(f32[15,16,256]{2,1,0:T(8,128)S(1)} %pad_maximum_fusion.7), channel_id=1, source_target_pairs={{0,496},{16,0},{32,16},{48,32},{64,48},{80,64},{96,80},{112,96},{1... | collective-permute-start | bytes 737288 | tf_op jit(solution)/shard_map/ppermute | solution.py:11
  183.6 3.8 %collective-permute-done.6 = f32[15,16,256]{2,1,0:T(8,128)S(1)} collective-permute-done((f32[15,16,256]{2,1,0:T(8,128)S(1)}, f32[15,16,256]{2,1,0:T(8,128)S(1)}, u32[]{:S(2)}, u32[]{:S(2)}) %collective-permute-start.6) | collective-permute-done | bytes 245792 | tf_op jit(solution)/shard_map/ppermute | solution.py:11
  187.6 0.1 bitcast_dynamic-update-slice_fusion.1
  187.7 0.0 collective-permute-done.7
  187.8 0.1 fusion.77
  187.9 0.0 slice-done.2
  187.9 0.0 slice-done.3
  188.0 1.8 fusion.4
  189.8 0.8 bitcast_add_fusion
  (93 shorter events, 1.2 us)
Async XLA Ops:
  6.5 81.3 %all-gather.3.cloned.1.call-start = ((), (), s32[]{:S(2)}) async-start(), calls=%async_computation | async-start | bytes 5849088 | tf_op jit(solution)/shard_map/all_gather | solution.py:72
  7.3 168.1 %all-gather.5.cloned.1.call-start = ((), (), s32[]{:S(2)}) async-start(), calls=%async_computation.1 | async-start | bytes 5849088 | tf_op jit(solution)/shard_map/all_gather | solution.py:74
  9.2 13.1 %copy-start.2 = (pred[7]{0:T(512)(128)(4,1)S(1)}, pred[7]{0:T(512)(128)(4,1)}, u32[]{:S(2)}) copy-start(pred[7]{0:T(512)(128)(4,1)} %constant.8.clone.1) | copy-start | bytes 25
  9.2 12.8 %collective-permute-start = (f32[15,16,256]{2,1,0:T(8,128)S(1)}, f32[15,16,256]{2,1,0:T(8,128)S(1)}, u32[]{:S(2)}, u32[]{:S(2)}) collective-permute-start(f32[15,16,256]{2,1,0:T(8,128)S(1)} %pad_maximum_fusion), channel_id=1, source_target_pairs={{0,16},{16,32},{32,48},{48,64},{64,80},{80,96},{96,112},{112,128},... | collective-permute-start | bytes 737288 | tf_op jit(solution)/shard_map/ppermute | solution.py:11
  9.2 13.1 %copy-start.1 = (f32[3,7,16,256]{3,2,1,0:T(8,128)S(1)}, f32[3,7,16,256]{3,2,1,0:T(8,128)}, u32[]{:S(2)}) copy-start(f32[3,7,16,256]{3,2,1,0:T(8,128)} %param.2) | copy-start | bytes 1032196
  9.3 12.8 %collective-permute-start.1 = (f32[15,16,256]{2,1,0:T(8,128)S(1)}, f32[15,16,256]{2,1,0:T(8,128)S(1)}, u32[]{:S(2)}, u32[]{:S(2)}) collective-permute-start(f32[15,16,256]{2,1,0:T(8,128)S(1)} %pad_maximum_fusion.1), channel_id=1, source_target_pairs={{0,496},{16,0},{32,16},{48,32},{64,48},{80,64},{96,80},{112,96},{1... | collective-permute-start | bytes 737288 | tf_op jit(solution)/shard_map/ppermute | solution.py:11
  22.6 69.8 %copy-start.3 = (s32[3]{0:T(128)S(1)}, s32[3]{0:T(128)}, u32[]{:S(2)}) copy-start(s32[3]{0:T(128)} %param.3) | copy-start | bytes 40
  87.8 12.4 %slice-start = ((s8[5505024]{0:T(1024)(128)(4,1)}), s8[4194304]{0:T(1024)(128)(4,1)S(1)}, s32[]{:S(2)}) async-start(s8[5505024]{0:T(1024)(128)(4,1)} %bitcast.247), calls=%async_computation.2 | async-start | bytes 8388608
  92.2 7.9 %slice-start.1 = ((s8[5505024]{0:T(1024)(128)(4,1)}), s8[1310720]{0:T(1024)(128)(4,1)S(1)}, s32[]{:S(2)}) async-start(s8[5505024]{0:T(1024)(128)(4,1)} %bitcast.247), calls=%async_computation.3 | async-start | bytes 2621440
  92.3 7.4 %collective-permute-start.2 = (f32[15,16,256]{2,1,0:T(8,128)S(1)}, f32[15,16,256]{2,1,0:T(8,128)S(1)}, u32[]{:S(2)}, u32[]{:S(2)}) collective-permute-start(f32[15,16,256]{2,1,0:T(8,128)S(1)} %pad_maximum_fusion.2), channel_id=1, source_target_pairs={{0,16},{16,32},{32,48},{48,64},{64,80},{80,96},{96,112},{112,128},... | collective-permute-start | bytes 737288 | tf_op jit(solution)/shard_map/ppermute | solution.py:11
  92.4 7.5 %collective-permute-start.3 = (f32[15,16,256]{2,1,0:T(8,128)S(1)}, f32[15,16,256]{2,1,0:T(8,128)S(1)}, u32[]{:S(2)}, u32[]{:S(2)}) collective-permute-start(f32[15,16,256]{2,1,0:T(8,128)S(1)} %pad_maximum_fusion.3), channel_id=1, source_target_pairs={{0,496},{16,0},{32,16},{48,32},{64,48},{80,64},{96,80},{112,96},{1... | collective-permute-start | bytes 737288 | tf_op jit(solution)/shard_map/ppermute | solution.py:11
  102.8 10.0 %copy-start = (f32[3,7,16,256]{3,2,1,0:T(8,128)S(1)}, f32[3,7,16,256]{3,2,1,0:T(8,128)}, u32[]{:S(2)}) copy-start(f32[3,7,16,256]{3,2,1,0:T(8,128)} %bitcast_add_fusion.1) | copy-start | bytes 1032196
  105.7 6.8 %collective-permute-start.4 = (f32[15,16,256]{2,1,0:T(8,128)S(1)}, f32[15,16,256]{2,1,0:T(8,128)S(1)}, u32[]{:S(2)}, u32[]{:S(2)}) collective-permute-start(f32[15,16,256]{2,1,0:T(8,128)S(1)} %pad_maximum_fusion.4), channel_id=1, source_target_pairs={{0,16},{16,32},{32,48},{48,64},{64,80},{80,96},{96,112},{112,128},... | collective-permute-start | bytes 737288 | tf_op jit(solution)/shard_map/ppermute | solution.py:11
  105.8 6.8 %collective-permute-start.5 = (f32[15,16,256]{2,1,0:T(8,128)S(1)}, f32[15,16,256]{2,1,0:T(8,128)S(1)}, u32[]{:S(2)}, u32[]{:S(2)}) collective-permute-start(f32[15,16,256]{2,1,0:T(8,128)S(1)} %pad_maximum_fusion.5), channel_id=1, source_target_pairs={{0,496},{16,0},{32,16},{48,32},{64,48},{80,64},{96,80},{112,96},{1... | collective-permute-start | bytes 737288 | tf_op jit(solution)/shard_map/ppermute | solution.py:11
  175.4 12.5 %slice-start.2 = ((s8[5505024]{0:T(1024)(128)(4,1)}), s8[4194304]{0:T(1024)(128)(4,1)S(1)}, s32[]{:S(2)}) async-start(s8[5505024]{0:T(1024)(128)(4,1)} %bitcast.249), calls=%async_computation.4 | async-start | bytes 8388608
  179.9 8.0 %slice-start.3 = ((s8[5505024]{0:T(1024)(128)(4,1)}), s8[1310720]{0:T(1024)(128)(4,1)S(1)}, s32[]{:S(2)}) async-start(s8[5505024]{0:T(1024)(128)(4,1)} %bitcast.249), calls=%async_computation.5 | async-start | bytes 2621440
  180.0 7.4 %collective-permute-start.6 = (f32[15,16,256]{2,1,0:T(8,128)S(1)}, f32[15,16,256]{2,1,0:T(8,128)S(1)}, u32[]{:S(2)}, u32[]{:S(2)}) collective-permute-start(f32[15,16,256]{2,1,0:T(8,128)S(1)} %pad_maximum_fusion.6), channel_id=1, source_target_pairs={{0,16},{16,32},{32,48},{48,64},{64,80},{80,96},{96,112},{112,128},... | collective-permute-start | bytes 737288 | tf_op jit(solution)/shard_map/ppermute | solution.py:11
  180.1 7.6 %collective-permute-start.7 = (f32[15,16,256]{2,1,0:T(8,128)S(1)}, f32[15,16,256]{2,1,0:T(8,128)S(1)}, u32[]{:S(2)}, u32[]{:S(2)}) collective-permute-start(f32[15,16,256]{2,1,0:T(8,128)S(1)} %pad_maximum_fusion.7), channel_id=1, source_target_pairs={{0,496},{16,0},{32,16},{48,32},{64,48},{80,64},{96,80},{112,96},{1... | collective-permute-start | bytes 737288 | tf_op jit(solution)/shard_map/ppermute | solution.py:11
Sparse Core Ops, SparseCore 0:
  10.4 77.3 all-gather.2
  102.9 72.4 all-gather.4

commit v12 on v9

--- a/solution.py
+++ b/solution.py
@@ -45,20 +45,31 @@
 def contract(extended, shard_rows, keep=None):
     local_rows = shard_rows.shape[0]
     span = 2 * W + 1
-    zeros = jnp.zeros_like(extended[:local_rows, :1])
-    shifted = []
-    for inner_band in range(span):
-        window = extended[inner_band : inner_band + local_rows]
-        shift = inner_band - W
-        if shift > 0:
-            window = jnp.concatenate([zeros] * shift + [window[:, : span - shift]], axis=1)
-        elif shift < 0:
-            window = jnp.concatenate([window[:, -shift:]] + [zeros] * (-shift), axis=1)
-        shifted.append(window)
-    stacked = jnp.stack(shifted, axis=3)
     if keep is not None:
         shard_rows = shard_rows * keep
-    return jnp.einsum("ibcas,iasr->ibcr", stacked, shard_rows, precision=lax.Precision.HIGH)
+    zeros = jnp.zeros_like(extended[:local_rows, :1])
+    total = None
+    for first, last in ((0, W - 2), (W - 1, W + 1), (W + 2, 2 * W)):
+        out_low = max(0, first - W)
+        out_high = min(2 * W, last + W)
+        shifted = []
+        for inner_band in range(first, last + 1):
+            window = extended[inner_band : inner_band + local_rows]
+            low = out_low - inner_band + W
+            high = out_high - inner_band + W
+            pieces = [zeros] * max(0, -low) + [window[:, max(0, low) : min(span, high + 1)]]
+            pieces += [zeros] * max(0, high - (span - 1))
+            shifted.append(jnp.concatenate(pieces, axis=1) if len(pieces) > 1 else pieces[0])
+        stacked = jnp.stack(shifted, axis=3)
+        part = jnp.einsum(
+            "ibcas,iasr->ibcr",
+            stacked,
+            shard_rows[:, first : last + 1],
+            precision=lax.Precision.HIGH,
+        )
+        part = jnp.pad(part, ((0, 0), (out_low, 2 * W - out_high), (0, 0), (0, 0)))
+        total = part if total is None else total + part
+    return total
 
 
 def on_device(density, band_widths):

time: 199 us -> 204 us (1.025)
  waiting for transfers between devices: 144 us -> 149 us
  local copies, waits for them, and re-layouts: 3.37 us -> 7.04 us
  other arithmetic: 4.81 us -> 8.14 us
  matrix products: 12.3 us -> 9.03 us
  starting transfers between devices: 19 us -> 16.6 us
    ppermute x8, waiting for transfers between devices: 15.3 us -> 26.6 us  [send(): lax.ppermute(cells, 'blk', [(i, (i + shift) % count) for i in range(count)])]
    dot_general x4 -> x12, matrix products: 12.3 us -> 9.03 us  [contract(): jnp.einsum('ibcas,iasr->ibcr', stacked, shard_rows[:, first:last + 1], pr...]
    mul x0 -> x1, other arithmetic: none -> 3.18 us  [contract(): shard_rows = shard_rows * keep]
    all_gather x1, waiting for transfers between devices: 62.3 us -> 59.2 us  [on_device(): gathered, keep = (lax.all_gather(current, 'col', axis=2, tiled=True), None)]
    all_gather x1, waiting for transfers between devices: 65.2 us -> 62.4 us  [on_device(): lax.all_gather(density, 'col', axis=2, tiled=True)]
    slice x0 -> x2, local copies, waits for them, and re-layouts: none -> 2.46 us  [contract(): shard_rows[:, first:last + 1]]
    ppermute x8, starting transfers between devices: 19 us -> 16.5 us  [send(): lax.ppermute(cells, 'blk', [(i, (i + shift) % count) for i in range(count)])]
  transfers between devices with their start and end apart: 10 -> 10, of which waited for: 6 -> 10; matrix products, arithmetic and copies ran while one was open for 3% -> 3% of each run, Pallas kernels for 0% -> 0%
where the time goes in v12:
time: 204 us
  waiting for transfers between devices  149 us (73%)
  starting transfers between devices  16.6 us (8%)
  between operations  14 us (7%)
  matrix products  9.03 us (4%)
  other arithmetic  8.14 us (4%)
  local copies, waits for them, and re-layouts  7.04 us (3%)
    all_gather x1, waiting for transfers between devices, on_device(): lax.all_gather(density, 'col', axis=2, tiled=True)  62.4 us
    all_gather x1, waiting for transfers between devices, on_device(): gathered, keep = (lax.all_gather(current, 'col', axis=2, tiled=True), None)  59.2 us
    ppermute x8, waiting for transfers between devices, send(): lax.ppermute(cells, 'blk', [(i, (i + shift) % count) for i in range(count)])  26.6 us
    ppermute x8, starting transfers between devices, send(): lax.ppermute(cells, 'blk', [(i, (i + shift) % count) for i in range(count)])  16.5 us
    dot_general x12, matrix products, contract(): jnp.einsum('ibcas,iasr->ibcr', stacked, shard_rows[:, first:last + 1], pr...  9.03 us
  transfers between devices with their start and end apart: 10, of which 10 were waited for; matrix products, arithmetic and copies ran while one was open for 3% of the time, Pallas kernels for 0%

profile of v12, /device:TPU:6, one launch (start us, length us, event | category | flops | bytes accessed | tf_op | source)
XLA Modules:
  0.0 203.7 jit_solution(3933374202663070505)
XLA Ops:
  6.5 0.7 all-gather.3.cloned.1.call-update
  7.3 0.7 compare_convert_fusion
  8.0 1.1 broadcast_multiply_fusion.1
  9.2 8.9 %collective-permute-start.1 = (f32[15,16,256]{2,1,0:T(8,128)S(1)}, f32[15,16,256]{2,1,0:T(8,128)S(1)}, u32[]{:S(2)}, u32[]{:S(2)}) collective-permute-start(f32[15,16,256]{2,1,0:T(8,128)S(1)} %pad_maximum_fusion.28), channel_id=1, source_target_pairs={{0,496},{16,0},{32,16},{48,32},{64,48},{80,64},{96,80},{112,96},{1... | collective-permute-start | bytes 737288 | tf_op jit(solution)/shard_map/ppermute | solution.py:11
  18.2 0.1 fusion.93
  18.3 3.6 %collective-permute-done.1 = f32[15,16,256]{2,1,0:T(8,128)S(1)} collective-permute-done((f32[15,16,256]{2,1,0:T(8,128)S(1)}, f32[15,16,256]{2,1,0:T(8,128)S(1)}, u32[]{:S(2)}, u32[]{:S(2)}) %collective-permute-start.1) | collective-permute-done | bytes 245792 | tf_op jit(solution)/shard_map/ppermute | solution.py:11
  21.9 3.1 %collective-permute-done = f32[15,16,256]{2,1,0:T(8,128)S(1)} collective-permute-done((f32[15,16,256]{2,1,0:T(8,128)S(1)}, f32[15,16,256]{2,1,0:T(8,128)S(1)}, u32[]{:S(2)}, u32[]{:S(2)}) %collective-permute-start) | collective-permute-done | bytes 245792 | tf_op jit(solution)/shard_map/ppermute | solution.py:11
  25.1 0.1 fusion.91
  25.3 0.1 fusion.87
  25.4 62.4 %all-gather.3.cloned.1.call-done = f32[3,7,256,256]{3,2,1,0:T(8,128)} async-done(((f32[3,7,16,256]{3,2,1,0:T(8,128)}), f32[3,7,256,256]{3,2,1,0:T(8,128)}) %all-gather.3.cloned.1.call-update) | async-done | bytes 5505040 | tf_op jit(solution)/shard_map/all_gather | solution.py:81
  87.8 3.2 %broadcast_multiply_fusion = f32[3,7,256,256]{3,2,1,0:T(8,128)S(1)} fusion(f32[3,7,256,256]{3,2,1,0:T(8,128)} %all-gather.3.cloned.1.call-done, f32[3,7]{1,0:T(4,128)S(1)} %compare_convert_fusion), kind=kLoop, calls=%fused_computation | loop fusion | flops 1376256 | bytes 11010132 | tf_op jit(solution)/shard_map/mul | solution.py:49
  91.0 0.2 slice_bitcast_fusion.5
  91.2 0.7 fusion.23
  91.9 0.7 fusion.25
  92.6 0.9 fusion.6
  93.5 0.1 fusion.61
  93.7 3.5 %collective-permute-start.3 = (f32[15,16,256]{2,1,0:T(8,128)S(1)}, f32[15,16,256]{2,1,0:T(8,128)S(1)}, u32[]{:S(2)}, u32[]{:S(2)}) collective-permute-start(f32[15,16,256]{2,1,0:T(8,128)S(1)} %pad_maximum_fusion.30), channel_id=1, source_target_pairs={{0,496},{16,0},{32,16},{48,32},{64,48},{80,64},{96,80},{112,96},{1... | collective-permute-start | bytes 737288 | tf_op jit(solution)/shard_map/ppermute | solution.py:11
  97.2 3.7 %collective-permute-done.3 = f32[15,16,256]{2,1,0:T(8,128)S(1)} collective-permute-done((f32[15,16,256]{2,1,0:T(8,128)S(1)}, f32[15,16,256]{2,1,0:T(8,128)S(1)}, u32[]{:S(2)}, u32[]{:S(2)}) %collective-permute-start.3) | collective-permute-done | bytes 245792 | tf_op jit(solution)/shard_map/ppermute | solution.py:11
  101.0 3.1 %collective-permute-done.2 = f32[15,16,256]{2,1,0:T(8,128)S(1)} collective-permute-done((f32[15,16,256]{2,1,0:T(8,128)S(1)}, f32[15,16,256]{2,1,0:T(8,128)S(1)}, u32[]{:S(2)}, u32[]{:S(2)}) %collective-permute-start.2) | collective-permute-done | bytes 245792 | tf_op jit(solution)/shard_map/ppermute | solution.py:11
  104.1 0.1 fusion.90
  104.3 0.1 fusion.84
  104.4 0.7 fusion.10
  105.1 0.7 fusion.21
  105.8 0.9 fusion.4
  106.7 0.8 fusion.59
  107.6 0.9 slice_bitcast_fusion.25
  108.5 1.0 slice_bitcast_fusion.17
  109.5 1.0 slice_bitcast_fusion.9
  110.6 0.5 collective-permute-start.4
  111.0 3.2 %collective-permute-done.5 = f32[15,16,256]{2,1,0:T(8,128)S(1)} collective-permute-done((f32[15,16,256]{2,1,0:T(8,128)S(1)}, f32[15,16,256]{2,1,0:T(8,128)S(1)}, u32[]{:S(2)}, u32[]{:S(2)}) %collective-permute-start.5) | collective-permute-done | bytes 245792 | tf_op jit(solution)/shard_map/ppermute | solution.py:11
  114.3 3.1 %collective-permute-done.4 = f32[15,16,256]{2,1,0:T(8,128)S(1)} collective-permute-done((f32[15,16,256]{2,1,0:T(8,128)S(1)}, f32[15,16,256]{2,1,0:T(8,128)S(1)}, u32[]{:S(2)}, u32[]{:S(2)}) %collective-permute-start.4) | collective-permute-done | bytes 245792 | tf_op jit(solution)/shard_map/ppermute | solution.py:11
  117.7 0.1 fusion.68
  117.8 59.2 %all-gather.5.cloned.1.call-done = f32[3,7,256,256]{3,2,1,0:T(8,128)} async-done(((f32[3,7,16,256]{3,2,1,0:T(8,128)}), f32[3,7,256,256]{3,2,1,0:T(8,128)}) %all-gather.5.cloned.1.call-update) | async-done | bytes 5505040 | tf_op jit(solution)/shard_map/all_gather | solution.py:83
  177.0 2.3 %slice_bitcast_fusion.3 = (f32[3,2,256,256,1]{3,2,1,0,4:T(8,128)S(1)}, f32[3,2,256,256,1]{3,2,1,0,4:T(8,128)S(1)}) fusion(f32[3,7,256,256]{3,2,1,0:T(8,128)} %all-gather.5.cloned.1.call-done), kind=kLoop, calls=%fused_computation.12 | loop fusion | bytes 6291456 | tf_op jit(solution)/shard_map/slice | solution.py:67
  179.3 0.7 fusion.19
  180.0 0.7 fusion.15
  180.7 1.2 copy-done.1
  181.9 0.9 fusion.2
  182.8 0.1 fusion.55
  183.0 3.5 %collective-permute-start.7 = (f32[15,16,256]{2,1,0:T(8,128)S(1)}, f32[15,16,256]{2,1,0:T(8,128)S(1)}, u32[]{:S(2)}, u32[]{:S(2)}) collective-permute-start(f32[15,16,256]{2,1,0:T(8,128)S(1)} %pad_maximum_fusion.34), channel_id=1, source_target_pairs={{0,496},{16,0},{32,16},{48,32},{64,48},{80,64},{96,80},{112,96},{1... | collective-permute-start | bytes 737288 | tf_op jit(solution)/shard_map/ppermute | solution.py:11
  186.5 3.7 %collective-permute-done.7 = f32[15,16,256]{2,1,0:T(8,128)S(1)} collective-permute-done((f32[15,16,256]{2,1,0:T(8,128)S(1)}, f32[15,16,256]{2,1,0:T(8,128)S(1)}, u32[]{:S(2)}, u32[]{:S(2)}) %collective-permute-start.7) | collective-permute-done | bytes 245792 | tf_op jit(solution)/shard_map/ppermute | solution.py:11
  190.2 3.1 %collective-permute-done.6 = f32[15,16,256]{2,1,0:T(8,128)S(1)} collective-permute-done((f32[15,16,256]{2,1,0:T(8,128)S(1)}, f32[15,16,256]{2,1,0:T(8,128)S(1)}, u32[]{:S(2)}, u32[]{:S(2)}) %collective-permute-start.6) | collective-permute-done | bytes 245792 | tf_op jit(solution)/shard_map/ppermute | solution.py:11
  193.4 0.1 fusion.88
  193.6 0.1 fusion.64
  193.7 0.7 fusion.17
  194.4 0.7 fusion.13
  195.1 0.9 fusion
  196.0 0.9 fusion.53
  (82 shorter events, 1.2 us)
Async XLA Ops:
  6.5 11.7 %copy-start.2 = (f32[3,7,16,256]{3,2,1,0:T(8,128)S(1)}, f32[3,7,16,256]{3,2,1,0:T(8,128)}, u32[]{:S(2)}) copy-start(f32[3,7,16,256]{3,2,1,0:T(8,128)} %param.2) | copy-start | bytes 1032196
  6.5 81.3 %all-gather.3.cloned.1.call-start = ((), (), s32[]{:S(2)}) async-start(), calls=%async_computation | async-start | bytes 5849088 | tf_op jit(solution)/shard_map/all_gather | solution.py:81
  7.3 169.8 %all-gather.5.cloned.1.call-start = ((), (), s32[]{:S(2)}) async-start(), calls=%async_computation.1 | async-start | bytes 5849088 | tf_op jit(solution)/shard_map/all_gather | solution.py:83
  8.0 17.1 %copy-start.3 = (pred[7]{0:T(512)(128)(4,1)S(1)}, pred[7]{0:T(512)(128)(4,1)}, u32[]{:S(2)}) copy-start(pred[7]{0:T(512)(128)(4,1)} %constant.16.clone.1) | copy-start | bytes 25
  9.2 12.7 %collective-permute-start.1 = (f32[15,16,256]{2,1,0:T(8,128)S(1)}, f32[15,16,256]{2,1,0:T(8,128)S(1)}, u32[]{:S(2)}, u32[]{:S(2)}) collective-permute-start(f32[15,16,256]{2,1,0:T(8,128)S(1)} %pad_maximum_fusion.28), channel_id=1, source_target_pairs={{0,496},{16,0},{32,16},{48,32},{64,48},{80,64},{96,80},{112,96},{1... | collective-permute-start | bytes 737288 | tf_op jit(solution)/shard_map/ppermute | solution.py:11
  18.2 6.8 %collective-permute-start = (f32[15,16,256]{2,1,0:T(8,128)S(1)}, f32[15,16,256]{2,1,0:T(8,128)S(1)}, u32[]{:S(2)}, u32[]{:S(2)}) collective-permute-start(f32[15,16,256]{2,1,0:T(8,128)S(1)} %pad_maximum_fusion.27), channel_id=1, source_target_pairs={{0,16},{16,32},{32,48},{48,64},{64,80},{80,96},{96,112},{112,128},... | collective-permute-start | bytes 737288 | tf_op jit(solution)/shard_map/ppermute | solution.py:11
  93.7 7.2 %collective-permute-start.3 = (f32[15,16,256]{2,1,0:T(8,128)S(1)}, f32[15,16,256]{2,1,0:T(8,128)S(1)}, u32[]{:S(2)}, u32[]{:S(2)}) collective-permute-start(f32[15,16,256]{2,1,0:T(8,128)S(1)} %pad_maximum_fusion.30), channel_id=1, source_target_pairs={{0,496},{16,0},{32,16},{48,32},{64,48},{80,64},{96,80},{112,96},{1... | collective-permute-start | bytes 737288 | tf_op jit(solution)/shard_map/ppermute | solution.py:11
  97.2 6.8 %collective-permute-start.2 = (f32[15,16,256]{2,1,0:T(8,128)S(1)}, f32[15,16,256]{2,1,0:T(8,128)S(1)}, u32[]{:S(2)}, u32[]{:S(2)}) collective-permute-start(f32[15,16,256]{2,1,0:T(8,128)S(1)} %pad_maximum_fusion.29), channel_id=1, source_target_pairs={{0,16},{16,32},{32,48},{48,64},{64,80},{80,96},{96,112},{112,128},... | collective-permute-start | bytes 737288 | tf_op jit(solution)/shard_map/ppermute | solution.py:11
  107.6 10.0 %copy-start = (f32[3,7,16,256]{3,2,1,0:T(8,128)S(1)}, f32[3,7,16,256]{3,2,1,0:T(8,128)}, u32[]{:S(2)}) copy-start(f32[3,7,16,256]{3,2,1,0:T(8,128)} %fusion.59) | copy-start | bytes 1032196
  110.5 3.8 %collective-permute-start.5 = (f32[15,16,256]{2,1,0:T(8,128)S(1)}, f32[15,16,256]{2,1,0:T(8,128)S(1)}, u32[]{:S(2)}, u32[]{:S(2)}) collective-permute-start(f32[15,16,256]{2,1,0:T(8,128)S(1)} %pad_maximum_fusion.32), channel_id=1, source_target_pairs={{0,496},{16,0},{32,16},{48,32},{64,48},{80,64},{96,80},{112,96},{1... | collective-permute-start | bytes 737288 | tf_op jit(solution)/shard_map/ppermute | solution.py:11
  110.6 6.8 %collective-permute-start.4 = (f32[15,16,256]{2,1,0:T(8,128)S(1)}, f32[15,16,256]{2,1,0:T(8,128)S(1)}, u32[]{:S(2)}, u32[]{:S(2)}) collective-permute-start(f32[15,16,256]{2,1,0:T(8,128)S(1)} %pad_maximum_fusion.31), channel_id=1, source_target_pairs={{0,16},{16,32},{32,48},{48,64},{64,80},{80,96},{96,112},{112,128},... | collective-permute-start | bytes 737288 | tf_op jit(solution)/shard_map/ppermute | solution.py:11
  179.3 2.6 %copy-start.1 = (f32[3,7,256,256]{3,2,1,0:T(8,128)S(1)}, f32[3,7,256,256]{3,2,1,0:T(8,128)}, u32[]{:S(2)}) copy-start(f32[3,7,256,256]{3,2,1,0:T(8,128)} %all-gather.5.cloned.1.call-done) | copy-start | bytes 16515076
  183.0 7.2 %collective-permute-start.7 = (f32[15,16,256]{2,1,0:T(8,128)S(1)}, f32[15,16,256]{2,1,0:T(8,128)S(1)}, u32[]{:S(2)}, u32[]{:S(2)}) collective-permute-start(f32[15,16,256]{2,1,0:T(8,128)S(1)} %pad_maximum_fusion.34), channel_id=1, source_target_pairs={{0,496},{16,0},{32,16},{48,32},{64,48},{80,64},{96,80},{112,96},{1... | collective-permute-start | bytes 737288 | tf_op jit(solution)/shard_map/ppermute | solution.py:11
  186.5 6.8 %collective-permute-start.6 = (f32[15,16,256]{2,1,0:T(8,128)S(1)}, f32[15,16,256]{2,1,0:T(8,128)S(1)}, u32[]{:S(2)}, u32[]{:S(2)}) collective-permute-start(f32[15,16,256]{2,1,0:T(8,128)S(1)} %pad_maximum_fusion.33), channel_id=1, source_target_pairs={{0,16},{16,32},{32,48},{48,64},{64,80},{80,96},{96,112},{112,128},... | collective-permute-start | bytes 737288 | tf_op jit(solution)/shard_map/ppermute | solution.py:11
Sparse Core Ops, SparseCore 0:
  10.4 77.3 all-gather.2
  107.7 69.2 all-gather.4
